TPU v7x, 512 devices: a whole 4x8x8 slice. The times are simulated.
512 devices in a mesh: seq: 32 (over y, x), head: 16 (over z, core).
Axes of the slice: x: 4, y: 8, z: 8, core: 2. Of those that a mesh axis runs over, the one named last changes fastest.
Arguments:
- features: bfloat16 [65536, 8192], P(('seq', 'head')), may hold values from -6 to 6
- increment_per_head: bfloat16 [65536, 128], P(('seq', 'head')), may hold values from 0.0049743652 to 0.049804688
- token_log_decay: bfloat16 [65536, 128], P(('seq', 'head')), may hold values from -2 to 0, as said below
- b_matrix: bfloat16 [65536, 1024], P(('seq', 'head')), may hold values from -6 to 6
- c_matrix: bfloat16 [65536, 1024], P(('seq', 'head')), may hold values from -0.5 to 0.5
- skip_gain: float32 [128], P('head'), may hold values from 0.5 to 1.5
Outputs:
- mixed_out: bfloat16 [65536, 8192], P(('seq', 'head'))
Inputs may be any that keep to these rules, and one draw needn't show every extreme that they name: `token_log_decay`: log decays are never positive.
All inputs are finite; a program needn't handle non-finite values.
Results may differ from a plain program's by a relative error of at most 0.01.
Values may be sent and summed in bfloat16 or wider, within the bound.
No kernel may reach another device: no remote copies, remote signals or barrier semaphores. Data moves between devices by JAX's collectives and lax.ppermute only.
A program may use at most 128 MiB of HBM per device.

v0:
```python
import jax
import jax.numpy as jnp
from jax import lax
from jax.sharding import PartitionSpec as P

G = 8
Q = 128


def prefix_2(value, axis, combine, identity):
    size, index = (lax.axis_size(axis), lax.axis_index(axis))
    everything = jax.tree.map(
        lambda part, kind: lax.all_gather(part.astype(kind), axis),
        value,
        (jnp.bfloat16, jnp.bfloat16),
    )
    start = jax.tree.map(
        lambda part, zero: jnp.broadcast_to(jnp.asarray(zero, part.dtype), part.shape),
        value,
        identity,
    )

    def lap(k, before):
        reached = k < index
        new = combine(
            before, jax.tree.map(lambda part, own: part[k].astype(own.dtype), everything, value)
        )
        return jax.tree.map(lambda a, b: jnp.where(reached, a, b), new, before)

    return lax.fori_loop(0, size, lap, start)


def combine(earlier, latter):
    return (earlier[0] + latter[0], jnp.exp(latter[0])[:, None, None] * earlier[1] + latter[1])


def local(features, increment_per_head, token_log_decay, b_matrix, c_matrix, skip_gain):
    n_groups = lax.axis_size("head")
    local_rows = features.shape[0]
    head_count = increment_per_head.shape[1]
    local_heads = head_count // n_groups
    head_width = features.shape[1] // head_count
    state_width = b_matrix.shape[1] // G
    b_slots = jnp.repeat(b_matrix.reshape(local_rows, G, state_width), n_groups // G, axis=1)
    c_slots = jnp.repeat(c_matrix.reshape(local_rows, G, state_width), n_groups // G, axis=1)
    local_groups = max(1, G // n_groups)
    per_group = local_heads // local_groups
    paired = jnp.concatenate([b_slots, c_slots], axis=2)
    rates = jnp.concatenate(
        [
            increment_per_head.reshape(local_rows, n_groups, local_heads),
            token_log_decay.reshape(local_rows, n_groups, local_heads),
        ],
        axis=2,
    )
    blocks_in = features.reshape(local_rows, n_groups, local_heads * head_width)
    moved_x, moved_rates, moved_bc = (
        lax.all_to_all(blocks_in, "head", split_axis=1, concat_axis=0, tiled=True),
        lax.all_to_all(rates, "head", split_axis=1, concat_axis=0, tiled=True),
        lax.all_to_all(paired, "head", split_axis=1, concat_axis=0, tiled=True),
    )
    token_count = local_rows * n_groups
    block_count = token_count // Q
    grouped_input_matrix = moved_x.reshape(block_count, Q, local_heads, head_width)
    step_local = (
        moved_rates[:, 0, :local_heads]
        .astype(jnp.float32)
        .reshape(block_count, Q, local_heads)
        .transpose(0, 2, 1)
    )
    shrinkage_within_segment = (
        moved_rates[:, 0, local_heads:]
        .astype(jnp.float32)
        .reshape(block_count, Q, local_heads)
        .transpose(0, 2, 1)
    )
    b_local = moved_bc[:, 0, : local_groups * state_width].reshape(
        block_count, Q, local_groups, state_width
    )
    c_local = moved_bc[:, 0, local_groups * state_width :].reshape(
        block_count, Q, local_groups, state_width
    )
    within = jnp.cumsum(shrinkage_within_segment, axis=2)
    block_total = within[:, :, -1]
    scores = jnp.einsum("ctgn,csgn->cgts", c_local, b_local, preferred_element_type=jnp.float32)
    scores = jnp.repeat(scores, per_group, axis=1)
    causal = (jnp.arange(Q)[:, None] >= jnp.arange(Q)[None, :])[None, None]
    gap_log = within[:, :, :, None] - within[:, :, None, :]
    damping = jnp.where(causal, jnp.exp(jnp.where(causal, gap_log, 0.0)), 0.0)
    weight = (scores * damping * step_local[:, :, None, :]).astype(jnp.bfloat16)
    inside = jnp.einsum(
        "chts,cshp->cthp", weight, grouped_input_matrix, preferred_element_type=jnp.float32
    )
    factor = (jnp.exp(block_total[:, :, None] - within) * step_local).transpose(0, 2, 1)
    scaled = (grouped_input_matrix * factor[..., None]).astype(jnp.bfloat16)
    update = jnp.einsum(
        "csgn,csgkp->cgknp",
        b_local,
        scaled.reshape(block_count, Q, local_groups, per_group, head_width),
        preferred_element_type=jnp.float32,
    ).reshape(block_count, local_heads, state_width, head_width)

    def advance(state_now, inputs):
        total_now, update_now = inputs
        return (jnp.exp(total_now)[:, None, None] * state_now + update_now, state_now)

    dev_state, local_carried = lax.scan(
        advance,
        jnp.zeros((local_heads, state_width, head_width), jnp.float32),
        (block_total, update),
    )
    prefix = jnp.cumsum(block_total, axis=0) - block_total
    dev_total = jnp.sum(block_total, axis=0)
    _, incoming = prefix_2(
        (dev_total, dev_state),
        "seq",
        combine,
        (jnp.zeros_like(dev_total), jnp.zeros_like(dev_state)),
    )
    carried = local_carried + jnp.exp(prefix)[:, :, None, None] * incoming[None]
    carried_in = carried.astype(jnp.bfloat16)
    outside = jnp.einsum(
        "ctgn,cgknp->ctgkp",
        c_local,
        carried_in.reshape(block_count, local_groups, per_group, state_width, head_width),
        preferred_element_type=jnp.float32,
    ).reshape(block_count, Q, local_heads, head_width)
    mixed = (
        inside
        + jnp.exp(within).transpose(0, 2, 1)[..., None] * outside
        + skip_gain[None, None, :, None] * grouped_input_matrix
    )
    leaving = mixed.astype(jnp.bfloat16).reshape(token_count, 1, local_heads * head_width)
    returned = lax.all_to_all(leaving, "head", split_axis=0, concat_axis=1, tiled=True)
    return returned.reshape(local_rows, head_count * head_width)


def solution(mesh):
    in_specs = (
        P(("seq", "head"), None),
        P(("seq", "head"), None),
        P(("seq", "head"), None),
        P(("seq", "head"), None),
        P(("seq", "head"), None),
        P("head"),
    )
    out_specs = P(("seq", "head"), None)
    return jax.shard_map(local, mesh=mesh, in_specs=in_specs, out_specs=out_specs, check_vma=False)
```

profile of v0, /device:TPU:1, one launch (start us, length us, event | category | flops | bytes accessed | tf_op | source)
XLA Modules:
  0.0 408.8 jit_solution(9127890750724101850)
XLA Ops:
  9.1 11.8 %all-to-all-start.1 = ((bf16[128,16,16]{0,2,1:T(8,128)(2,1)}), bf16[128,16,16]{0,2,1:T(8,128)(2,1)S(1)}, u32[]{:S(2)}, u32[]{:S(2)}) async-start(bf16[128,16,16]{0,2,1:T(8,128)(2,1)} %pad_maximum_fusion.1), calls=%async_computation.1 | async-start | bytes 131072 | tf_op jit(solution)/shard_map/all_to_all | solution.py:59
  23.3 5.4 %all-to-all-done.1 = bf16[128,16,16]{0,2,1:T(8,128)(2,1)S(1)} async-done(((bf16[128,16,16]{0,2,1:T(8,128)(2,1)}), bf16[128,16,16]{0,2,1:T(8,128)(2,1)S(1)}, u32[]{:S(2)}, u32[]{:S(2)}) %all-to-all-start.1) | async-done | bytes 65568 | tf_op jit(solution)/shard_map/all_to_all | solution.py:59
  28.7 3.6 all-to-all-start
  32.3 2.4 copy.71
  34.8 25.5 %all-to-all-done = bf16[128,16,256]{2,0,1:T(8,128)(2,1)S(1)} async-done(((bf16[128,16,256]{2,0,1:T(8,128)(2,1)}), bf16[128,16,256]{2,0,1:T(8,128)(2,1)S(1)}, u32[]{:S(2)}, u32[]{:S(2)}) %all-to-all-start) | async-done | bytes 1048608 | tf_op jit(solution)/shard_map/all_to_all | solution.py:60
  61.4 3.6 all-to-all-start.2
  65.7 4.5 %reduce_window_sum.22 = f32[16,8,128]{2,1,0:T(8,128)S(1)} reduce-window(f32[16,8,128]{2,1,0:T(8,128)S(1)} %get-tuple-element.214, f32[]{:T(128)} %constant.47.clone.1), window={size=1x1x128 pad=0_0x0_0x127_0}, to_apply=%region_0.0 | reduce-window | flops 2080768 | bytes 131076 | tf_op jit(solution)/shard_map/jit(cumsum)/reduce_window_sum | solution.py:83
  72.7 41.1 %all-to-all-done.2 = bf16[128,16,512]{0,2,1:T(8,128)(2,1)S(1)} async-done(((bf16[128,16,512]{0,2,1:T(8,128)(2,1)}), bf16[128,16,512]{0,2,1:T(8,128)(2,1)S(1)}, u32[]{:S(2)}, u32[]{:S(2)}) %all-to-all-start.2) | async-done | bytes 2097184 | tf_op jit(solution)/shard_map/all_to_all | solution.py:58
  113.8 4.1 convolution_bitcast_fusion
  117.9 34.9 %while.27 = (s32[]{:T(128)}, f32[8,128,64]{2,1,0:T(8,128)S(1)}, f32[16,8,128,64]{3,2,1,0:T(8,128)}, f32[16,8]{1,0:T(8,128)S(1)}, f32[16,8,128,64]{2,3,1,0:T(8,128)}, /*index=5*/s32[]{:T(128)}, s32[]{:T(128)}) while((s32[]{:T(128)}, f32[8,128,64]{2,1,0:T(8,128)S(1)}, f32[16,8,128,64]{3,2,1,0:T(8,128)}, f32[16,8]{1,0:T(8,128)S(1)}, ...), condition=%wide.region_2.3_spmd.clone, body=%wide.region_1.2_spmd.clone.sunk | while | flops 262147 | bytes 2621644 | solution.py:107
  155.8 61.7 %all-reduce = bf16[256]{0:T(256)(128)(2,1)S(1)} all-reduce(bf16[256]{0:T(256)(128)(2,1)S(1)} %dynamic-update-slice), channel_id=2, replica_groups=mesh['seq'=32,'head'=16] {'seq'}, use_global_device_ids=true, to_apply=%add | all-reduce | flops 256 | bytes 1024
  217.6 2.6 fusion.21
  220.2 16.5 %all-gather.4.cloned.1.call-done = bf16[256,128,64]{1,2,0:T(8,128)(2,1)} async-done(((bf16[8,128,64]{1,2,0:T(8,128)(2,1)}), bf16[256,128,64]{1,2,0:T(8,128)(2,1)}) %all-gather.4.cloned.1.call-update) | async-done | bytes 4194320 | tf_op jit(solution)/shard_map/all_gather | solution.py:13
  236.7 41.5 %while.28 = (s32[]{:T(128)}, f32[8,128,64]{2,1,0:T(8,128)S(1)}, s32[]{:T(128)}, bf16[32,8]{1,0:T(8,128)(2,1)S(1)}, bf16[32,8,128,64]{2,3,1,0:T(8,128)(2,1)}, /*index=5*/s32[]{:T(128)}, s32[]{:T(128)}) while((s32[]{:T(128)}, f32[8,128,64]{2,1,0:T(8,128)S(1)}, s32[]{:T(128)}, bf16[32,8]{1,0:T(8,128)(2,1)S(1)}, ...), condition=%wide.region_6.7_spmd.clone, body=%wide.region_5.6_spmd.clone.sunk | while | flops 327692 | bytes 1179841 | solution.py:30
  278.3 6.0 %fusion.7 = f32[16,8,64,128]{3,2,1,0:T(8,128)S(1)} fusion(bf16[16,128,128,1]{2,1,3,0:T(8,128)(2,1)S(1)} %bitcast.127, f32[16,8,128,64]{3,2,1,0:T(8,128)} %get-tuple-element.127, f32[8,128,64]{2,1,0:T(8,128)S(1)} %get-tuple-element.129, f32[16,8]{1,0:T(8,128)S(1)} %subtract_exponential_fusion), kind=kOutput, calls=%fused_computation.18 | convolution fusion | flops 271581184 | bytes 9175552 | tf_op jit(solution)/shard_map/ctgn,cgknp->ctgkp/dot_general | solution.py:122
  284.3 4.2 %fusion.6 = bf16[16,128,8,64]{1,3,2,0:T(8,128)(2,1)S(1)} fusion(bf16[16,128,8,64]{1,3,2,0:T(8,128)(2,1)S(1)} %bitcast.123, f32[16,8,64,128]{3,2,1,0:T(8,128)S(1)} %fusion.7, f32[8]{0:T(128)S(1)} %copy-done.7, f32[16,128,8]{1,2,0:T(8,128)S(1)} %exponential_bitcast_fusion.1, f32[16,8,128]{2,1,0:T(8,128)S(1)} %copy-done.6, ...), kind=kOutput, calls=%fused_computation.17 | convolution fusion | flops 287309824 | bytes 9650208 | tf_op jit(solution)/shard_map/chts,cshp->cthp/dot_general | solution.py:91
  288.5 3.6 copy.76
  292.1 14.9 %reshape.157 = bf16[2048,1,512]{2,1,0:T(2,128)(2,1)} reshape(bf16[16,128,8,64]{3,2,1,0:T(8,128)(2,1)} %copy.76) | data formatting | bytes 4194304 | tf_op jit(solution)/shard_map/reshape | solution.py:133
  307.5 14.1 %reduce.1 = bf16[2048,512]{1,0:T(8,128)(2,1)S(1)} reduce(bf16[2048,1,512]{2,1,0:T(2,128)(2,1)} %reshape.157, bf16[]{:T(256)} %broadcast.37), dimensions={1}, to_apply=%reshape.157.reduce_sub_computation | reduce | bytes 4194306 | tf_op jit(solution)/shard_map/reshape | solution.py:133
  321.6 2.8 reshape.164
  324.3 61.7 %all_to_all.66 = bf16[16,2,32768]{2,1,0:T(2,128)(2,1)S(1)} all-to-all(bf16[16,2,32768]{2,1,0:T(2,128)(2,1)} %reshape.164), channel_id=1, replica_groups=mesh['seq'=32,'head'=16] {'head'}, dimensions={0} | all-to-all | bytes 4194304 | tf_op jit(solution)/shard_map/all_to_all | solution.py:134
  386.1 6.7 %reshape.165 = bf16[2048,1,512]{2,1,0:T(2,128)(2,1)} reshape(bf16[16,2,32768]{2,1,0:T(2,128)(2,1)S(1)} %all_to_all.66) | data formatting | bytes 4194304
  392.7 2.8 copy.80
  397.9 4.1 copy.67
  (254 shorter events, 88.9 us)
Async XLA Ops:
  6.5 14.4 %copy-start = (bf16[128,1024]{1,0:T(8,128)(2,1)S(1)}, bf16[128,1024]{1,0:T(8,128)(2,1)}, u32[]{:S(2)}) copy-start(bf16[128,1024]{1,0:T(8,128)(2,1)} %param.14) | copy-start | bytes 786436
  6.5 25.8 %copy-start.4 = (bf16[128,8192]{1,0:T(8,128)(2,1)S(1)}, bf16[128,8192]{1,0:T(8,128)(2,1)}, u32[]{:S(2)}) copy-start(bf16[128,8192]{1,0:T(8,128)(2,1)} %param.10) | copy-start | bytes 6291460
  9.1 19.6 %all-to-all-start.1 = ((bf16[128,16,16]{0,2,1:T(8,128)(2,1)}), bf16[128,16,16]{0,2,1:T(8,128)(2,1)S(1)}, u32[]{:S(2)}, u32[]{:S(2)}) async-start(bf16[128,16,16]{0,2,1:T(8,128)(2,1)} %pad_maximum_fusion.1), calls=%async_computation.1 | async-start | bytes 131072 | tf_op jit(solution)/shard_map/all_to_all | solution.py:59
  28.7 31.6 %all-to-all-start = ((bf16[128,16,256]{2,0,1:T(8,128)(2,1)}), bf16[128,16,256]{2,0,1:T(8,128)(2,1)S(1)}, u32[]{:S(2)}, u32[]{:S(2)}) async-start(bf16[128,16,256]{2,0,1:T(8,128)(2,1)} %pad_maximum_fusion), calls=%async_computation | async-start | bytes 2097152 | tf_op jit(solution)/shard_map/all_to_all | solution.py:60
  60.3 1.0 copy-start.3
  61.4 52.5 %all-to-all-start.2 = ((bf16[128,16,512]{0,2,1:T(8,128)(2,1)}), bf16[128,16,512]{0,2,1:T(8,128)(2,1)S(1)}, u32[]{:S(2)}, u32[]{:S(2)}) async-start(bf16[128,16,512]{0,2,1:T(8,128)(2,1)} %bitcast.124), calls=%async_computation.2 | async-start | bytes 4194304 | tf_op jit(solution)/shard_map/all_to_all | solution.py:58
  65.0 171.8 %all-gather.4.cloned.1.call-start = ((), (), s32[]{:S(2)}) async-start(), calls=%async_computation.4 | async-start | bytes 4325376 | tf_op jit(solution)/shard_map/all_gather | solution.py:13
  113.8 4.1 copy-start.1
  278.2 6.0 %copy-start.2 = (bf16[128,16,512]{0,2,1:T(8,128)(2,1)S(1)}, bf16[128,16,512]{0,2,1:T(8,128)(2,1)}, u32[]{:S(2)}) copy-start(bf16[128,16,512]{0,2,1:T(8,128)(2,1)} %copy-done.1) | copy-start | bytes 6291460
  278.2 6.0 %copy-start.5 = (f32[16,128,128]{2,1,0:T(8,128)S(1)}, f32[16,128,128]{2,1,0:T(8,128)}, u32[]{:S(2)}) copy-start(f32[16,128,128]{2,1,0:T(8,128)} %fusion.21) | copy-start | bytes 3145732
  278.2 6.0 %copy-start.6 = (f32[16,8,128]{2,1,0:T(8,128)S(1)}, f32[16,8,128]{2,1,0:T(8,128)}, u32[]{:S(2)}) copy-start(f32[16,8,128]{2,1,0:T(8,128)} %get-tuple-element.213) | copy-start | bytes 196612
  278.2 6.0 %copy-start.7 = (f32[8]{0:T(128)S(1)}, f32[8]{0:T(128)}, u32[]{:S(2)}) copy-start(f32[8]{0:T(128)} %param.15) | copy-start | bytes 100
Sparse Core Ops, SparseCore 0:
  153.7 83.0 all-gather.3
where the time goes:
time: 411 us; the launch traced here: 409 us
  blocking collectives  123 us (30%)
  local copies, waits for them, and re-layouts  103 us (25%)
  waiting for transfers between devices  88.6 us (22%)
  other arithmetic  41.7 us (10%)
  starting transfers between devices  19.1 us (5%)
  matrix products  16.8 us (4%)
  between operations  14.3 us (3%)
    all_to_all x1, blocking collectives, local(): lax.all_to_all(leaving, 'head', split_axis=0, concat_axis=1, tiled=True)  61.7 us
    unnamed x1, blocking collectives  61.7 us
    all_to_all x1, waiting for transfers between devices, local(): lax.all_to_all(blocks_in, 'head', split_axis=1, concat_axis=0, tiled=True)  41.1 us
    dynamic_slice x64, local copies, waits for them, and re-layouts, lap(): part[k].astype(own.dtype)  35.1 us
    all_to_all x1, waiting for transfers between devices, local(): lax.all_to_all(paired, 'head', split_axis=1, concat_axis=0, tiled=True)  25.5 us
    reshape x3, local copies, waits for them, and re-layouts, local(): mixed.astype(jnp.bfloat16).reshape(token_count, 1, local_heads * head_width)  19 us
    dynamic_slice x32, local copies, waits for them, and re-layouts, local(): lax.scan(advance, jnp.zeros((local_heads, state_width, head_width), jnp.f...  18.7 us
    unnamed x24, local copies, waits for them, and re-layouts  16.7 us
  transfers between devices with their start and end apart: 4, of which 4 were waited for; matrix products, arithmetic and copies ran while one was open for 4% of the time, Pallas kernels for 0%

commit v1 on v0

v1 whole, which is shorter than its diff:
```python
import jax
import jax.numpy as jnp
from jax import lax
from jax.sharding import Mesh
from jax.sharding import PartitionSpec as P

G = 8
CORES = 2


def swap(value):
    return lax.ppermute(value, "core", [(0, 1), (1, 0)])


def shift_seq(value, distance, count):
    return lax.ppermute(value, "seq", [(i, i + distance) for i in range(count - distance)])


def local(features, increment_per_head, token_log_decay, b_matrix, c_matrix, skip_gain):
    f32, bf16 = jnp.float32, jnp.bfloat16
    n_seq = lax.axis_size("seq")
    n_z = lax.axis_size("z")
    n_core = lax.axis_size("core")
    z_idx = lax.axis_index("z")
    c_idx = lax.axis_index("core")
    tokens = features.shape[0]
    heads = increment_per_head.shape[1]
    width = features.shape[1] // heads
    state = b_matrix.shape[1] // G
    per_group = heads // G
    half = heads // n_core
    quarter = half // n_z

    x = features.reshape(tokens, heads, width)
    step = increment_per_head.astype(f32)
    within = jnp.cumsum(token_log_decay.astype(f32), axis=0)
    total = within[-1]
    b = b_matrix.reshape(tokens, G, state)
    c = c_matrix.reshape(tokens, G, state)
    totals = lax.all_gather(total, ("z", "core")).reshape(n_z, n_core, heads)
    skip = lax.all_gather(skip_gain, ("z", "core"), tiled=True)

    factor = jnp.exp(total[None, :] - within) * step
    scaled = (x * factor[..., None]).astype(bf16)
    update = jnp.einsum(
        "sgn,sghp->ghnp", b, scaled.reshape(tokens, G, per_group, width),
        preferred_element_type=f32,
    ).reshape(heads, state, width)

    own = lax.dynamic_slice_in_dim(update, c_idx * half, half, 0)
    got = swap(lax.dynamic_slice_in_dim(update, (1 - c_idx) * half, half, 0))
    first = jnp.where(c_idx == 0, own, got)
    second = jnp.where(c_idx == 0, got, own)
    mine = lax.dynamic_index_in_dim(totals, z_idx, 0, keepdims=False)
    t_first = lax.dynamic_slice_in_dim(mine[0], c_idx * half, half)
    t_second = lax.dynamic_slice_in_dim(mine[1], c_idx * half, half)
    pair = jnp.exp(t_second)[:, None, None] * first + second

    pair = pair.astype(bf16).reshape(n_z, quarter, state, width)
    rows = lax.all_to_all(pair, "z", 0, 0, tiled=True).astype(f32)
    chip_totals = lax.dynamic_slice_in_dim(
        totals[:, 0] + totals[:, 1], c_idx * half + z_idx * quarter, quarter, 1
    )
    run = jnp.zeros((quarter, state, width), f32)
    before = jnp.zeros((quarter,), f32)
    starts, lead = [], []
    for chip in range(n_z):
        starts.append(run)
        lead.append(before)
        run = jnp.exp(chip_totals[chip])[:, None, None] * run + rows[chip]
        before = before + chip_totals[chip]

    acc_t, acc_s = shift_seq((before, run), 1, n_seq)
    distance = 1
    while distance < n_seq:
        got_t, got_s = shift_seq((acc_t, acc_s), distance, n_seq)
        acc_s = jnp.exp(acc_t)[:, None, None] * got_s + acc_s
        acc_t = acc_t + got_t
        distance *= 2

    chip_in = jnp.stack(starts) + jnp.exp(jnp.stack(lead))[:, :, None, None] * acc_s[None]
    back = lax.all_to_all(chip_in.astype(bf16), "z", 0, 0, tiled=True)
    entry = back.astype(f32).reshape(half, state, width)

    into_second = jnp.exp(t_first)[:, None, None] * entry + first
    keep = jnp.where(c_idx == 0, entry, into_second).astype(bf16)
    send = jnp.where(c_idx == 0, into_second, entry).astype(bf16)
    other = swap(send)
    carried_in = jnp.where(
        c_idx == 0,
        jnp.concatenate([keep, other], axis=0),
        jnp.concatenate([other, keep], axis=0),
    )

    scores = jnp.einsum("tgn,sgn->gts", c, b, preferred_element_type=f32)
    scores = jnp.repeat(scores, per_group, axis=0)
    causal = (jnp.arange(tokens)[:, None] >= jnp.arange(tokens)[None, :])[None]
    w_t = within.T
    gap = w_t[:, :, None] - w_t[:, None, :]
    damping = jnp.where(causal, jnp.exp(jnp.where(causal, gap, 0.0)), 0.0)
    weight = (scores * damping * step.T[:, None, :]).astype(bf16)
    inside = jnp.einsum("hts,shp->thp", weight, x, preferred_element_type=f32)

    outside = jnp.einsum(
        "tgn,ghnp->tghp", c, carried_in.reshape(G, per_group, state, width),
        preferred_element_type=f32,
    ).reshape(tokens, heads, width)
    mixed = inside + jnp.exp(within)[..., None] * outside + skip[None, :, None] * x.astype(f32)
    return mixed.astype(bf16).reshape(tokens, heads * width)


def solution(mesh):
    n_seq, n_head = mesh.devices.shape
    grid = Mesh(mesh.devices.reshape(n_seq, n_head // CORES, CORES), ("seq", "z", "core"))
    rows = P(("seq", "z", "core"), None)
    in_specs = (rows, rows, rows, rows, rows, P(("z", "core")))
    return jax.shard_map(local, mesh=grid, in_specs=in_specs, out_specs=rows, check_vma=False)
```

time: 411 us -> 230 us (0.56)
  local copies, waits for them, and re-layouts: 103 us -> 15.8 us
  blocking collectives: 123 us -> 40.4 us
  starting transfers between devices: 19.1 us -> 89.5 us
  waiting for transfers between devices: 88.6 us -> 53.4 us
  other arithmetic: 41.7 us -> 23.3 us
  between operations: 14.3 us -> 1.23 us
  matrix products: 16.8 us -> 5.64 us
    ppermute x0 -> x13, starting transfers between devices: none -> 81.7 us  [the longest x11 55.2 us: shift_seq(): lax.ppermute(value, 'seq', [(i, i + distance) for i in range(count - dist...]
    all_to_all x1 -> x0, blocking collectives: 61.7 us -> none  [local(): lax.all_to_all(leaving, 'head', split_axis=0, concat_axis=1, tiled=True)]
    dynamic_slice x96 -> x2, local copies, waits for them, and re-layouts: 53.7 us -> 1.59 us  [the longest x1 1.58 us: local(): got = swap(lax.dynamic_slice_in_dim(update, (1 - c_idx) * half, half, 0))]
    unnamed x1, blocking collectives: 61.7 us -> 22.9 us
    all_to_all x3 -> x2, waiting for transfers between devices: 72.1 us -> 41.3 us  [the longest x1 23.6 us: local(): rows = lax.all_to_all(pair, 'z', 0, 0, tiled=True).astype(f32)]
    reshape x7 -> x1, local copies, waits for them, and re-layouts: 26.6 us -> 2.89 us  [local(): return mixed.astype(bf16).reshape(tokens, heads * width)]
    all_gather x0 -> x1, blocking collectives: none -> 17.5 us  [local(): totals = lax.all_gather(total, ('z', 'core')).reshape(n_z, n_core, heads)]
    all_gather x1 -> x0, waiting for transfers between devices: 16.5 us -> none  [prefix_2(): lax.all_gather(part.astype(kind), axis)]
  transfers between devices with their start and end apart: 4 -> 15, of which waited for: 4 -> 8; matrix products, arithmetic and copies ran while one was open for 4% -> 8% of each run, Pallas kernels for 0% -> 0%
where the time goes in v1:
time: 230 us; the launch traced here: 229 us
  starting transfers between devices  89.5 us (39%)
  waiting for transfers between devices  53.4 us (23%)
  blocking collectives  40.4 us (18%)
  other arithmetic  23.3 us (10%)
  local copies, waits for them, and re-layouts  15.8 us (7%)
  matrix products  5.64 us (2%)
    ppermute x11, starting transfers between devices, shift_seq(): lax.ppermute(value, 'seq', [(i, i + distance) for i in range(count - dist...  55.2 us
    ppermute x2, starting transfers between devices, swap(): return lax.ppermute(value, 'core', [(0, 1), (1, 0)])  26.5 us
    all_to_all x1, waiting for transfers between devices, local(): rows = lax.all_to_all(pair, 'z', 0, 0, tiled=True).astype(f32)  23.6 us
    unnamed x1, blocking collectives  22.9 us
    all_to_all x1, waiting for transfers between devices, local(): back = lax.all_to_all(chip_in.astype(bf16), 'z', 0, 0, tiled=True)  17.7 us
    all_gather x1, blocking collectives, local(): totals = lax.all_gather(total, ('z', 'core')).reshape(n_z, n_core, heads)  17.5 us
    ppermute x11, waiting for transfers between devices, shift_seq(): lax.ppermute(value, 'seq', [(i, i + distance) for i in range(count - dist...  12.1 us
    unnamed x64, local copies, waits for them, and re-layouts  9.56 us
  transfers between devices with their start and end apart: 15, of which 8 were waited for; matrix products, arithmetic and copies ran while one was open for 8% of the time, Pallas kernels for 0%

profile of v1, /device:TPU:1, one launch (start us, length us, event | category | flops | bytes accessed | tf_op | source)
XLA Modules:
  0.0 229.3 jit_solution(17800479091251320167)
XLA Ops:
  0.0 3.3 %copy.36 = bf16[128,8192]{0,1:T(8,128)(2,1)S(1)} copy(bf16[128,8192]{1,0:T(8,128)(2,1)} %param.6) | data formatting | bytes 4194304 | tf_op args[0]
  7.3 8.7 %collective-permute-start = (f32[64,128,64]{1,2,0:T(8,128)}, f32[64,128,64]{1,2,0:T(8,128)S(1)}, u32[]{:S(2)}, u32[]{:S(2)}) collective-permute-start(f32[64,128,64]{1,2,0:T(8,128)} %constant_dynamic-slice_fusion.1), channel_id=1, source_target_pairs={{0,1},{1,0},{2,3},{3,2},{4,5},{5,4},{6,7},{7,6},{8,9},{9,8},{10,11... | collective-permute-start | bytes 6291464 | tf_op jit(solution)/shard_map/ppermute | solution.py:12
  16.1 17.5 %all-gather = f32[16,1,128]{2,1,0:T(1,128)S(1)} all-gather(f32[1,1,128]{2,1,0:T(1,128)S(1)} %get-tuple-element.27), channel_id=1, replica_groups=mesh['seq'=32,'z'=8,'core'=2] {'z','core'}, dimensions={0}, use_global_device_ids=true | all-gather | bytes 8704 | tf_op jit(solution)/shard_map/all_gather | solution.py:40
  34.3 3.7 %add_convert_fusion.1 = bf16[64,128,64]{1,2,0:T(8,128)(2,1)} fusion(f32[64,128,64]{1,2,0:T(8,128)S(1)} %collective-permute-done, f32[128,128,64]{1,2,0:T(8,128)} %bitcast.184, s32[]{:T(128)S(6)} %select_n.60, f32[64]{0:T(128)S(1)} %fusion.32, pred[]{:T(512)S(6)} %eq.2), kind=kLoop, calls=%fused_computation.18 | loop fusion | flops 2621440 | bytes 5243141 | tf_op jit(solution)/shard_map/convert_element_type | solution.py:59
  38.0 3.6 %all-to-all-start = ((bf16[8,8,128,64]{2,3,1,0:T(8,128)(2,1)}), bf16[8,8,128,64]{2,3,1,0:T(8,128)(2,1)S(1)}, u32[]{:S(2)}, u32[]{:S(2)}) async-start(bf16[8,8,128,64]{2,3,1,0:T(8,128)(2,1)} %bitcast.190), calls=%async_computation | async-start | bytes 2097152 | tf_op jit(solution)/shard_map/all_to_all | solution.py:60
  42.9 3.7 %collective-permute-start.1 = (f32[8]{0:T(128)}, f32[8]{0:T(128)}, u32[]{:S(2)}, u32[]{:S(2)}) collective-permute-start(f32[8]{0:T(128)} %get-tuple-element.31), channel_id=1, source_target_pairs={{0,16},{16,32},{32,48},{48,64},{64,80},{80,96},{96,112},{112,128},... | collective-permute-start | bytes 104 | tf_op jit(solution)/shard_map/ppermute | solution.py:16
  47.2 23.6 %all-to-all-done = bf16[8,8,128,64]{2,3,1,0:T(8,128)(2,1)S(1)} async-done(((bf16[8,8,128,64]{2,3,1,0:T(8,128)(2,1)}), bf16[8,8,128,64]{2,3,1,0:T(8,128)(2,1)S(1)}, u32[]{:S(2)}, u32[]{:S(2)}) %all-to-all-start) | async-done | bytes 1048608 | tf_op jit(solution)/shard_map/all_to_all | solution.py:60
  71.7 3.1 %collective-permute-start.6 = (f32[8,128,64]{1,2,0:T(8,128)S(1)}, f32[8,128,64]{1,2,0:T(8,128)S(1)}, u32[]{:S(2)}, u32[]{:S(2)}) collective-permute-start(f32[8,128,64]{1,2,0:T(8,128)S(1)} %fusion.17), channel_id=1, source_target_pairs={{0,16},{16,32},{32,48},{48,64},{64,80},{80,96},{96,112},{112,128},... | collective-permute-start | bytes 786440 | tf_op jit(solution)/shard_map/ppermute | solution.py:16
  75.7 3.1 %collective-permute-start.2 = (f32[8]{0:T(128)}, f32[8]{0:T(128)S(1)}, u32[]{:S(2)}, u32[]{:S(2)}) collective-permute-start(f32[8]{0:T(128)} %collective-permute-done.1), channel_id=1, source_target_pairs={{0,16},{16,32},{32,48},{48,64},{64,80},{80,96},{96,112},{112,128},... | collective-permute-start | bytes 104 | tf_op jit(solution)/shard_map/ppermute | solution.py:16
  80.7 5.6 %collective-permute-start.3 = (f32[8]{0:T(128)S(1)}, f32[8]{0:T(128)S(1)}, u32[]{:S(2)}, u32[]{:S(2)}) collective-permute-start(f32[8]{0:T(128)S(1)} %get-tuple-element.16), channel_id=1, source_target_pairs={{0,32},{16,48},{32,64},{48,80},{64,96},{80,112},{96,128},{112,144}... | collective-permute-start | bytes 104 | tf_op jit(solution)/shard_map/ppermute | solution.py:16
  88.6 5.1 %collective-permute-start.4 = (f32[8]{0:T(128)S(1)}, f32[8]{0:T(128)S(1)}, u32[]{:S(2)}, u32[]{:S(2)}) collective-permute-start(f32[8]{0:T(128)S(1)} %get-tuple-element.14), channel_id=1, source_target_pairs={{0,64},{16,80},{32,96},{48,112},{64,128},{80,144},{96,160},{112,17... | collective-permute-start | bytes 104 | tf_op jit(solution)/shard_map/ppermute | solution.py:16
  94.4 4.6 %collective-permute-start.5 = (f32[8]{0:T(128)S(1)}, f32[8]{0:T(128)S(1)}, u32[]{:S(2)}, u32[]{:S(2)}) collective-permute-start(f32[8]{0:T(128)S(1)} %get-tuple-element.12), channel_id=1, source_target_pairs={{0,128},{16,144},{32,160},{48,176},{64,192},{80,208},{96,224},{112... | collective-permute-start | bytes 104 | tf_op jit(solution)/shard_map/ppermute | solution.py:16
  99.1 5.1 %collective-permute-start.8 = (f32[8,128,64]{1,2,0:T(8,128)S(1)}, f32[8,128,64]{1,2,0:T(8,128)S(1)}, u32[]{:S(2)}, u32[]{:S(2)}) collective-permute-start(f32[8,128,64]{1,2,0:T(8,128)S(1)} %multiply_add_fusion.4), channel_id=1, source_target_pairs={{0,32},{16,48},{32,64},{48,80},{64,96},{80,112},{96,128},{112,144}... | collective-permute-start | bytes 786440 | tf_op jit(solution)/shard_map/ppermute | solution.py:16
  107.6 7.6 %collective-permute-start.9 = (f32[8,128,64]{1,2,0:T(8,128)S(1)}, f32[8,128,64]{1,2,0:T(8,128)S(1)}, u32[]{:S(2)}, u32[]{:S(2)}) collective-permute-start(f32[8,128,64]{1,2,0:T(8,128)S(1)} %multiply_add_fusion.3), channel_id=1, source_target_pairs={{0,64},{16,80},{32,96},{48,112},{64,128},{80,144},{96,160},{112,17... | collective-permute-start | bytes 786440 | tf_op jit(solution)/shard_map/ppermute | solution.py:16
  118.6 6.7 %collective-permute-start.10 = (f32[8,128,64]{1,2,0:T(8,128)S(1)}, f32[8,128,64]{1,2,0:T(8,128)S(1)}, u32[]{:S(2)}, u32[]{:S(2)}) collective-permute-start(f32[8,128,64]{1,2,0:T(8,128)S(1)} %multiply_add_fusion.2), channel_id=1, source_target_pairs={{0,128},{16,144},{32,160},{48,176},{64,192},{80,208},{96,224},{112... | collective-permute-start | bytes 786440 | tf_op jit(solution)/shard_map/ppermute | solution.py:16
  128.7 8.4 %collective-permute-start.11 = (f32[8,128,64]{1,2,0:T(8,128)S(1)}, f32[8,128,64]{1,2,0:T(8,128)S(1)}, u32[]{:S(2)}, u32[]{:S(2)}) collective-permute-start(f32[8,128,64]{1,2,0:T(8,128)S(1)} %multiply_add_fusion.1), channel_id=1, source_target_pairs={{0,256},{16,272},{32,288},{48,304},{64,320},{80,336},{96,352},{112... | collective-permute-start | bytes 786440 | tf_op jit(solution)/shard_map/ppermute | solution.py:16
  138.8 4.3 %collective-permute-done.11 = f32[8,128,64]{1,2,0:T(8,128)S(1)} collective-permute-done((f32[8,128,64]{1,2,0:T(8,128)S(1)}, f32[8,128,64]{1,2,0:T(8,128)S(1)}, u32[]{:S(2)}, u32[]{:S(2)}) %collective-permute-start.11) | collective-permute-done | bytes 262176 | tf_op jit(solution)/shard_map/ppermute | solution.py:16
  143.2 3.0 %add_convert_fusion = bf16[8,8,128,64]{2,3,1,0:T(8,128)(2,1)} fusion(f32[8,8,128,64]{2,3,1,0:T(8,128)} %add_dynamic-update-slice_fusion, f32[8,128,64]{1,2,0:T(8,128)S(1)} %multiply_add_fusion, f32[8,8]{1,0:T(8,128)S(1)} %exp.128), kind=kLoop, calls=%fused_computation.17 | loop fusion | flops 1572864 | bytes 3408128 | tf_op jit(solution)/shard_map/convert_element_type | solution.py:82
  146.2 4.2 %all-to-all-start.1 = ((bf16[8,8,128,64]{2,3,1,0:T(8,128)(2,1)}), bf16[8,8,128,64]{2,3,1,0:T(8,128)(2,1)}, u32[]{:S(2)}, u32[]{:S(2)}) async-start(bf16[8,8,128,64]{2,3,1,0:T(8,128)(2,1)} %add_convert_fusion), calls=%async_computation.1 | async-start | bytes 2097152 | tf_op jit(solution)/shard_map/all_to_all | solution.py:82
  150.5 17.7 %all-to-all-done.1 = bf16[8,8,128,64]{2,3,1,0:T(8,128)(2,1)} async-done(((bf16[8,8,128,64]{2,3,1,0:T(8,128)(2,1)}), bf16[8,8,128,64]{2,3,1,0:T(8,128)(2,1)}, u32[]{:S(2)}, u32[]{:S(2)}) %all-to-all-start.1) | async-done | bytes 1048608 | tf_op jit(solution)/shard_map/all_to_all | solution.py:82
  168.2 3.5 %fusion.7 = (bf16[64,128,64]{1,2,0:T(8,128)(2,1)S(1)}, bf16[64,128,64]{1,2,0:T(8,128)(2,1)}) fusion(bf16[8,8,128,64]{2,3,1,0:T(8,128)(2,1)} %all-to-all-done.1, f32[64]{0:T(128)S(1)} %fusion.34, pred[]{:T(512)S(6)} %eq.2, f32[64,128,64]{1,2,0:T(8,128)S(1)} %copy-done.5, f32[128,128,64]{1,2,0:T(8,128)} %bitcast.185, s32[]{:T(128)S(6)} %select_n.60), kind=kLoop, calls=%fused_computation.13 | loop fusion | flops 4194304 | bytes 7340293 | tf_op jit(solution)/shard_map/convert_element_type | solution.py:86
  171.8 17.7 %collective-permute-start.12 = (bf16[64,128,64]{1,2,0:T(8,128)(2,1)}, bf16[64,128,64]{1,2,0:T(8,128)(2,1)S(1)}, u32[]{:S(2)}, u32[]{:S(2)}) collective-permute-start(bf16[64,128,64]{1,2,0:T(8,128)(2,1)} %get-tuple-element.24), channel_id=1, source_target_pairs={{0,1},{1,0},{2,3},{3,2},{4,5},{5,4},{6,7},{7,6},{8,9},{9,8},{10,11... | collective-permute-start | bytes 3145736 | tf_op jit(solution)/shard_map/ppermute | solution.py:12
  193.3 4.0 %fusion.1 = bf16[128,128,128]{2,1,0:T(8,128)(2,1)} fusion(f32[128,128]{1,0:T(8,128)S(1)} %copy.35, f32[128,128]{1,0:T(8,128)S(1)} %copy.33, f32[8,128,128]{2,1,0:T(8,128)S(1)} %fusion.12, pred[128,128]{1,0:T(8,128)(4,1)S(1)} %iota_compare_fusion), kind=kLoop, calls=%fused_computation.2 | loop fusion | flops 12582912 | bytes 4866048 | tf_op jit(solution)/shard_map/convert_element_type | solution.py:101
  197.3 22.9 %all-reduce = f32[128]{0:T(128)S(1)} all-reduce(f32[128]{0:T(128)S(1)} %dynamic-update-slice), channel_id=1, replica_groups=mesh['seq'=32,'z'=8,'core'=2] {'z','core'}, use_global_device_ids=true, to_apply=%add | all-reduce | flops 128 | bytes 1024
  (121 shorter events, 37.3 us)
Async XLA Ops:
  7.3 27.0 %collective-permute-start = (f32[64,128,64]{1,2,0:T(8,128)}, f32[64,128,64]{1,2,0:T(8,128)S(1)}, u32[]{:S(2)}, u32[]{:S(2)}) collective-permute-start(f32[64,128,64]{1,2,0:T(8,128)} %constant_dynamic-slice_fusion.1), channel_id=1, source_target_pairs={{0,1},{1,0},{2,3},{3,2},{4,5},{5,4},{6,7},{7,6},{8,9},{9,8},{10,11... | collective-permute-start | bytes 6291464 | tf_op jit(solution)/shard_map/ppermute | solution.py:12
  38.0 32.8 %all-to-all-start = ((bf16[8,8,128,64]{2,3,1,0:T(8,128)(2,1)}), bf16[8,8,128,64]{2,3,1,0:T(8,128)(2,1)S(1)}, u32[]{:S(2)}, u32[]{:S(2)}) async-start(bf16[8,8,128,64]{2,3,1,0:T(8,128)(2,1)} %bitcast.190), calls=%async_computation | async-start | bytes 2097152 | tf_op jit(solution)/shard_map/all_to_all | solution.py:60
  42.9 32.7 %collective-permute-start.1 = (f32[8]{0:T(128)}, f32[8]{0:T(128)}, u32[]{:S(2)}, u32[]{:S(2)}) collective-permute-start(f32[8]{0:T(128)} %get-tuple-element.31), channel_id=1, source_target_pairs={{0,16},{16,32},{32,48},{48,64},{64,80},{80,96},{96,112},{112,128},... | collective-permute-start | bytes 104 | tf_op jit(solution)/shard_map/ppermute | solution.py:16
  71.0 4.5 %copy-start.16 = (f32[1,8]{1,0:T(1,128)S(1)}, f32[1,8]{1,0:T(1,128)}, u32[]{:S(2)}) copy-start(f32[1,8]{1,0:T(1,128)} %copy-done.15) | copy-start | bytes 100
  71.7 14.6 %collective-permute-start.6 = (f32[8,128,64]{1,2,0:T(8,128)S(1)}, f32[8,128,64]{1,2,0:T(8,128)S(1)}, u32[]{:S(2)}, u32[]{:S(2)}) collective-permute-start(f32[8,128,64]{1,2,0:T(8,128)S(1)} %fusion.17), channel_id=1, source_target_pairs={{0,16},{16,32},{32,48},{48,64},{64,80},{80,96},{96,112},{112,128},... | collective-permute-start | bytes 786440 | tf_op jit(solution)/shard_map/ppermute | solution.py:16
  75.7 4.4 %collective-permute-start.2 = (f32[8]{0:T(128)}, f32[8]{0:T(128)S(1)}, u32[]{:S(2)}, u32[]{:S(2)}) collective-permute-start(f32[8]{0:T(128)} %collective-permute-done.1), channel_id=1, source_target_pairs={{0,16},{16,32},{32,48},{48,64},{64,80},{80,96},{96,112},{112,128},... | collective-permute-start | bytes 104 | tf_op jit(solution)/shard_map/ppermute | solution.py:16
  80.7 7.8 %collective-permute-start.3 = (f32[8]{0:T(128)S(1)}, f32[8]{0:T(128)S(1)}, u32[]{:S(2)}, u32[]{:S(2)}) collective-permute-start(f32[8]{0:T(128)S(1)} %get-tuple-element.16), channel_id=1, source_target_pairs={{0,32},{16,48},{32,64},{48,80},{64,96},{80,112},{96,128},{112,144}... | collective-permute-start | bytes 104 | tf_op jit(solution)/shard_map/ppermute | solution.py:16
  86.3 12.6 %collective-permute-start.7 = (f32[8,128,64]{1,2,0:T(8,128)S(1)}, f32[8,128,64]{1,2,0:T(8,128)S(1)}, u32[]{:S(2)}, u32[]{:S(2)}) collective-permute-start(f32[8,128,64]{1,2,0:T(8,128)S(1)} %collective-permute-done.6), channel_id=1, source_target_pairs={{0,16},{16,32},{32,48},{48,64},{64,80},{80,96},{96,112},{112,128},... | collective-permute-start | bytes 786440 | tf_op jit(solution)/shard_map/ppermute | solution.py:16
  88.6 5.8 %collective-permute-start.4 = (f32[8]{0:T(128)S(1)}, f32[8]{0:T(128)S(1)}, u32[]{:S(2)}, u32[]{:S(2)}) collective-permute-start(f32[8]{0:T(128)S(1)} %get-tuple-element.14), channel_id=1, source_target_pairs={{0,64},{16,80},{32,96},{48,112},{64,128},{80,144},{96,160},{112,17... | collective-permute-start | bytes 104 | tf_op jit(solution)/shard_map/ppermute | solution.py:16
  94.4 9.9 %collective-permute-start.5 = (f32[8]{0:T(128)S(1)}, f32[8]{0:T(128)S(1)}, u32[]{:S(2)}, u32[]{:S(2)}) collective-permute-start(f32[8]{0:T(128)S(1)} %get-tuple-element.12), channel_id=1, source_target_pairs={{0,128},{16,144},{32,160},{48,176},{64,192},{80,208},{96,224},{112... | collective-permute-start | bytes 104 | tf_op jit(solution)/shard_map/ppermute | solution.py:16
  99.1 26.2 %copy-start.14 = (f32[8]{0:T(128)S(1)}, f32[8]{0:T(128)}, u32[]{:S(2)}) copy-start(f32[8]{0:T(128)} %get-tuple-element.36) | copy-start | bytes 100
  99.1 8.4 %collective-permute-start.8 = (f32[8,128,64]{1,2,0:T(8,128)S(1)}, f32[8,128,64]{1,2,0:T(8,128)S(1)}, u32[]{:S(2)}, u32[]{:S(2)}) collective-permute-start(f32[8,128,64]{1,2,0:T(8,128)S(1)} %multiply_add_fusion.4), channel_id=1, source_target_pairs={{0,32},{16,48},{32,64},{48,80},{64,96},{80,112},{96,128},{112,144}... | collective-permute-start | bytes 786440 | tf_op jit(solution)/shard_map/ppermute | solution.py:16
  107.6 10.9 %collective-permute-start.9 = (f32[8,128,64]{1,2,0:T(8,128)S(1)}, f32[8,128,64]{1,2,0:T(8,128)S(1)}, u32[]{:S(2)}, u32[]{:S(2)}) collective-permute-start(f32[8,128,64]{1,2,0:T(8,128)S(1)} %multiply_add_fusion.3), channel_id=1, source_target_pairs={{0,64},{16,80},{32,96},{48,112},{64,128},{80,144},{96,160},{112,17... | collective-permute-start | bytes 786440 | tf_op jit(solution)/shard_map/ppermute | solution.py:16
  116.0 21.1 %copy-start.12 = (f32[8]{0:T(128)S(1)}, f32[8]{0:T(128)}, u32[]{:S(2)}) copy-start(f32[8]{0:T(128)} %get-tuple-element.34) | copy-start | bytes 100
  118.6 19.4 %copy-start.18 = (f32[8]{0:T(128)S(1)}, f32[8]{0:T(128)}, u32[]{:S(2)}) copy-start(f32[8]{0:T(128)} %get-tuple-element.33) | copy-start | bytes 100
  118.6 10.1 %collective-permute-start.10 = (f32[8,128,64]{1,2,0:T(8,128)S(1)}, f32[8,128,64]{1,2,0:T(8,128)S(1)}, u32[]{:S(2)}, u32[]{:S(2)}) collective-permute-start(f32[8,128,64]{1,2,0:T(8,128)S(1)} %multiply_add_fusion.2), channel_id=1, source_target_pairs={{0,128},{16,144},{32,160},{48,176},{64,192},{80,208},{96,224},{112... | collective-permute-start | bytes 786440 | tf_op jit(solution)/shard_map/ppermute | solution.py:16
  128.7 14.3 %collective-permute-start.11 = (f32[8,128,64]{1,2,0:T(8,128)S(1)}, f32[8,128,64]{1,2,0:T(8,128)S(1)}, u32[]{:S(2)}, u32[]{:S(2)}) collective-permute-start(f32[8,128,64]{1,2,0:T(8,128)S(1)} %multiply_add_fusion.1), channel_id=1, source_target_pairs={{0,256},{16,272},{32,288},{48,304},{64,320},{80,336},{96,352},{112... | collective-permute-start | bytes 786440 | tf_op jit(solution)/shard_map/ppermute | solution.py:16
  143.1 7.3 %copy-start.26 = (f32[1,1,128]{2,1,0:T(1,128)S(1)}, f32[1,1,128]{2,1,0:T(1,128)}, u32[]{:S(2)}) copy-start(f32[1,1,128]{2,1,0:T(1,128)} %get-tuple-element.40) | copy-start | bytes 1540
  143.1 25.1 %copy-start.5 = (f32[64,128,64]{1,2,0:T(8,128)S(1)}, f32[64,128,64]{1,2,0:T(8,128)}, u32[]{:S(2)}) copy-start(f32[64,128,64]{1,2,0:T(8,128)} %copy-done.4) | copy-start | bytes 6291460
  146.2 22.1 %all-to-all-start.1 = ((bf16[8,8,128,64]{2,3,1,0:T(8,128)(2,1)}), bf16[8,8,128,64]{2,3,1,0:T(8,128)(2,1)}, u32[]{:S(2)}, u32[]{:S(2)}) async-start(bf16[8,8,128,64]{2,3,1,0:T(8,128)(2,1)} %add_convert_fusion), calls=%async_computation.1 | async-start | bytes 2097152 | tf_op jit(solution)/shard_map/all_to_all | solution.py:82
  150.5 41.3 %copy-start.27 = (f32[8]{0:T(128)S(1)}, f32[8]{0:T(128)}, u32[]{:S(2)}) copy-start(f32[8]{0:T(128)} %param.11) | copy-start | bytes 100
  168.2 21.3 %copy-start.7 = (bf16[128,1024]{1,0:T(8,128)(2,1)S(1)}, bf16[128,1024]{1,0:T(8,128)(2,1)}, u32[]{:S(2)}) copy-start(bf16[128,1024]{1,0:T(8,128)(2,1)} %param.10) | copy-start | bytes 786436
  168.2 21.3 %copy-start.9 = (bf16[128,128]{1,0:T(8,128)(2,1)S(1)}, bf16[128,128]{1,0:T(8,128)(2,1)}, u32[]{:S(2)}) copy-start(bf16[128,128]{1,0:T(8,128)(2,1)} %param.7) | copy-start | bytes 98308
  171.8 48.5 %collective-permute-start.12 = (bf16[64,128,64]{1,2,0:T(8,128)(2,1)}, bf16[64,128,64]{1,2,0:T(8,128)(2,1)S(1)}, u32[]{:S(2)}, u32[]{:S(2)}) collective-permute-start(bf16[64,128,64]{1,2,0:T(8,128)(2,1)} %get-tuple-element.24), channel_id=1, source_target_pairs={{0,1},{1,0},{2,3},{3,2},{4,5},{5,4},{6,7},{7,6},{8,9},{9,8},{10,11... | collective-permute-start | bytes 3145736 | tf_op jit(solution)/shard_map/ppermute | solution.py:12
  (19 other events, 56.7 us)

commit v2 on v1

--- a/solution.py
+++ b/solution.py
@@ -10,10 +10,6 @@
 
 def swap(value):
     return lax.ppermute(value, "core", [(0, 1), (1, 0)])
-
-
-def shift_seq(value, distance, count):
-    return lax.ppermute(value, "seq", [(i, i + distance) for i in range(count - distance)])
 
 
 def local(features, increment_per_head, token_log_decay, b_matrix, c_matrix, skip_gain):
@@ -37,8 +33,9 @@
     total = within[-1]
     b = b_matrix.reshape(tokens, G, state)
     c = c_matrix.reshape(tokens, G, state)
-    totals = lax.all_gather(total, ("z", "core")).reshape(n_z, n_core, heads)
-    skip = lax.all_gather(skip_gain, ("z", "core"), tiled=True)
+    small = lax.all_gather(jnp.concatenate([total, skip_gain.astype(f32)]), ("z", "core"))
+    totals = small[:, :heads].reshape(n_z, n_core, heads)
+    skip = small[:, heads:].reshape(heads)
 
     factor = jnp.exp(total[None, :] - within) * step
     scaled = (x * factor[..., None]).astype(bf16)
@@ -70,13 +67,29 @@
         run = jnp.exp(chip_totals[chip])[:, None, None] * run + rows[chip]
         before = before + chip_totals[chip]
 
-    acc_t, acc_s = shift_seq((before, run), 1, n_seq)
-    distance = 1
-    while distance < n_seq:
-        got_t, got_s = shift_seq((acc_t, acc_s), distance, n_seq)
-        acc_s = jnp.exp(acc_t)[:, None, None] * got_s + acc_s
-        acc_t = acc_t + got_t
-        distance *= 2
+    piece = state // n_seq
+    packed = jnp.concatenate(
+        [
+            run.reshape(quarter, n_seq, piece, width),
+            jnp.broadcast_to(before[:, None, None, None], (quarter, n_seq, 1, width)),
+        ],
+        axis=2,
+    ).transpose(1, 0, 2, 3)
+    gathered = lax.all_to_all(packed, "seq", 0, 0, tiled=True)
+    row_state = gathered[:, :, :piece]
+    row_total = gathered[:, :, piece, 0]
+    order = jnp.arange(n_seq)
+    between = (order[None, None, :] > order[None, :, None]) & (order[None, None, :] < order[:, None, None])
+    exponent = jnp.einsum(
+        "abi,ih->hab", between.astype(f32), row_total, precision=lax.Precision.HIGHEST
+    )
+    earlier = (order[None, :] < order[:, None])[None]
+    decay = jnp.where(earlier, jnp.exp(jnp.where(earlier, exponent, 0.0)), 0.0)
+    entering = jnp.einsum(
+        "hab,bhrw->ahrw", decay, row_state, precision=lax.Precision.HIGHEST
+    )
+    acc_s = lax.all_to_all(entering, "seq", 0, 0, tiled=True)
+    acc_s = acc_s.transpose(1, 0, 2, 3).reshape(quarter, state, width)
 
     chip_in = jnp.stack(starts) + jnp.exp(jnp.stack(lead))[:, :, None, None] * acc_s[None]
     back = lax.all_to_all(chip_in.astype(bf16), "z", 0, 0, tiled=True)

time: 230 us -> 234 us (1.017)
  starting transfers between devices: 89.5 us -> 36.8 us
  local copies, waits for them, and re-layouts: 15.8 us -> 40.9 us
  other arithmetic: 23.3 us -> 35.8 us
  waiting for transfers between devices: 53.4 us -> 61.8 us
  blocking collectives: 40.4 us -> 45.8 us
  matrix products: 5.64 us -> 9.97 us
    ppermute x11 -> x0, starting transfers between devices: 55.2 us -> none  [shift_seq(): lax.ppermute(value, 'seq', [(i, i + distance) for i in range(count - dist...]
    unnamed x1, blocking collectives: 22.9 us -> 45.8 us
    all_gather x1 -> x0, blocking collectives: 17.5 us -> none  [local(): totals = lax.all_gather(total, ('z', 'core')).reshape(n_z, n_core, heads)]
    slice x1 -> x10, local copies, waits for them, and re-layouts: 0.56 us -> 16.1 us  [local(): run = jnp.exp(chip_totals[chip])[:, None, None] * run + rows[chip]]
    all_to_all x0 -> x2, starting transfers between devices: none -> 14 us  [the longest x1 9.67 us: local(): gathered = lax.all_to_all(packed, 'seq', 0, 0, tiled=True)]
    ppermute x11 -> x0, waiting for transfers between devices: 12.1 us -> none  [shift_seq(): lax.ppermute(value, 'seq', [(i, i + distance) for i in range(count - dist...]
    all_to_all x0 -> x2, waiting for transfers between devices: none -> 12.1 us  [the longest x1 7.21 us: local(): gathered = lax.all_to_all(packed, 'seq', 0, 0, tiled=True)]
    ppermute x2, starting transfers between devices: 26.5 us -> 14.7 us  [swap(): return lax.ppermute(value, 'core', [(0, 1), (1, 0)])]
  transfers between devices with their start and end apart: 15 -> 6, of which waited for: 8 -> 4; matrix products, arithmetic and copies ran while one was open for 8% -> 9% of each run, Pallas kernels for 0% -> 0%
where the time goes in v2:
time: 234 us; the launch traced here: 232 us
  waiting for transfers between devices  61.8 us (26%)
  blocking collectives  45.8 us (20%)
  local copies, waits for them, and re-layouts  40.9 us (17%)
  starting transfers between devices  36.8 us (16%)
  other arithmetic  35.8 us (15%)
  matrix products  9.97 us (4%)
    unnamed x1, blocking collectives  45.8 us
    all_to_all x1, waiting for transfers between devices, local(): back = lax.all_to_all(chip_in.astype(bf16), 'z', 0, 0, tiled=True)  25 us
    all_to_all x1, waiting for transfers between devices, local(): rows = lax.all_to_all(pair, 'z', 0, 0, tiled=True).astype(f32)  24.7 us
    slice x10, local copies, waits for them, and re-layouts, local(): run = jnp.exp(chip_totals[chip])[:, None, None] * run + rows[chip]  16.1 us
    ppermute x2, starting transfers between devices, swap(): return lax.ppermute(value, 'core', [(0, 1), (1, 0)])  14.7 us
    unnamed x45, local copies, waits for them, and re-layouts  12.5 us
    all_to_all x1, starting transfers between devices, local(): gathered = lax.all_to_all(packed, 'seq', 0, 0, tiled=True)  9.67 us
    unnamed x8, other arithmetic  7.93 us
  transfers between devices with their start and end apart: 6, of which 4 were waited for; matrix products, arithmetic and copies ran while one was open for 9% of the time, Pallas kernels for 0%

profile of v2, /device:TPU:1, one launch (start us, length us, event | category | flops | bytes accessed | tf_op | source)
XLA Modules:
  0.0 232.2 jit_solution(12544638022148386665)
XLA Ops:
  2.5 3.3 %copy.103 = bf16[128,8192]{0,1:T(8,128)(2,1)S(1)} copy(bf16[128,8192]{1,0:T(8,128)(2,1)} %param.6) | data formatting | bytes 4194304 | tf_op args[0]
  9.1 8.8 %collective-permute-start = (f32[64,128,64]{1,2,0:T(8,128)}, f32[64,128,64]{1,2,0:T(8,128)}, u32[]{:S(2)}, u32[]{:S(2)}) collective-permute-start(f32[64,128,64]{1,2,0:T(8,128)} %constant_dynamic-slice_fusion.1), channel_id=1, source_target_pairs={{0,1},{1,0},{2,3},{3,2},{4,5},{5,4},{6,7},{7,6},{8,9},{9,8},{10,11... | collective-permute-start | bytes 6291464 | tf_op jit(solution)/shard_map/ppermute | solution.py:12
  20.1 45.8 %all-reduce = f32[2176]{0:T(1024)S(1)} all-reduce(f32[2176]{0:T(1024)S(1)} %maximum_dynamic-update-slice_fusion), channel_id=2, replica_groups=mesh['seq'=32,'z'=8,'core'=2] {'z','core'}, use_global_device_ids=true, to_apply=%add | all-reduce | flops 2176 | bytes 17408
  66.6 3.6 %add_convert_fusion.1 = bf16[64,128,64]{1,2,0:T(8,128)(2,1)} fusion(f32[64,128,64]{1,2,0:T(8,128)} %collective-permute-done, f32[128,128,64]{1,2,0:T(8,128)} %bitcast.162, s32[]{:T(128)S(6)} %select_n.67, f32[64]{0:T(128)S(1)} %fusion.32, pred[]{:T(512)S(6)} %eq.2), kind=kLoop, calls=%fused_computation.18 | loop fusion | flops 2621440 | bytes 5243141 | tf_op jit(solution)/shard_map/convert_element_type | solution.py:56
  70.2 3.9 %all-to-all-start = ((bf16[8,8,128,64]{2,3,1,0:T(8,128)(2,1)}), bf16[8,8,128,64]{2,3,1,0:T(8,128)(2,1)S(1)}, u32[]{:S(2)}, u32[]{:S(2)}) async-start(bf16[8,8,128,64]{2,3,1,0:T(8,128)(2,1)} %bitcast.168), calls=%async_computation | async-start | bytes 2097152 | tf_op jit(solution)/shard_map/all_to_all | solution.py:57
  76.3 24.7 %all-to-all-done = bf16[8,8,128,64]{2,3,1,0:T(8,128)(2,1)S(1)} async-done(((bf16[8,8,128,64]{2,3,1,0:T(8,128)(2,1)}), bf16[8,8,128,64]{2,3,1,0:T(8,128)(2,1)S(1)}, u32[]{:S(2)}, u32[]{:S(2)}) %all-to-all-start) | async-done | bytes 1048608 | tf_op jit(solution)/shard_map/all_to_all | solution.py:57
  102.2 2.0 copy.108
  108.1 2.0 copy.111
  110.1 2.0 copy.112
  117.1 2.7 %multiply_add_fusion = f32[8,32,4,64]{3,0,2,1:T(8,128)S(1)} fusion(f32[8,32,4,64]{3,0,2,1:T(8,128)} %bitcast.180, f32[8,32,4,64]{3,0,2,1:T(8,128)} %bitcast.179, f32[8,32,4,64]{3,0,2,1:T(8,128)} %bitcast.178, f32[8,32,4,64]{3,0,2,1:T(8,128)} %bitcast.177, f32[8,32,4,64]{3,0,2,1:T(8,128)} %bitcast.176, f32[8,32,4,64]{3,0,2,1:T(8,128)} %bitcast.175, ...), kind=kLoop, calls=%fused_computation.28 | loop fusion | flops 983040 | bytes 2359552 | tf_op jit(solution)/shard_map/add | solution.py:67
  120.8 2.2 reshape.313
  123.0 9.7 %all-to-all-start.1 = ((f32[32,1,2560]{2,1,0:T(1,128)}), f32[32,1,2560]{2,1,0:T(1,128)S(1)}, u32[]{:S(2)}, u32[]{:S(2)}) async-start(f32[32,1,2560]{2,1,0:T(1,128)} %reshape.313), calls=%async_computation.1 | async-start | bytes 655360 | tf_op jit(solution)/shard_map/all_to_all | solution.py:78
  136.3 7.2 %all-to-all-done.1 = f32[32,1,2560]{2,1,0:T(1,128)S(1)} async-done(((f32[32,1,2560]{2,1,0:T(1,128)}), f32[32,1,2560]{2,1,0:T(1,128)S(1)}, u32[]{:S(2)}, u32[]{:S(2)}) %all-to-all-start.1) | async-done | bytes 327712 | tf_op jit(solution)/shard_map/all_to_all | solution.py:78
  144.0 2.2 reduce
  153.4 4.4 %all-to-all-start.2 = ((f32[32,1,2048]{2,1,0:T(1,128)}), f32[32,1,2048]{2,1,0:T(1,128)S(1)}, u32[]{:S(2)}, u32[]{:S(2)}) async-start(f32[32,1,2048]{2,1,0:T(1,128)} %reshape.315), calls=%async_computation.2 | async-start | bytes 524288 | tf_op jit(solution)/shard_map/all_to_all | solution.py:91
  163.1 4.9 %all-to-all-done.2 = f32[32,1,2048]{2,1,0:T(1,128)S(1)} async-done(((f32[32,1,2048]{2,1,0:T(1,128)}), f32[32,1,2048]{2,1,0:T(1,128)S(1)}, u32[]{:S(2)}, u32[]{:S(2)}) %all-to-all-start.2) | async-done | bytes 262176 | tf_op jit(solution)/shard_map/all_to_all | solution.py:91
  169.9 3.0 %add_convert_fusion = bf16[8,8,128,64]{2,3,1,0:T(8,128)(2,1)} fusion(f32[8,8,128,64]{2,3,1,0:T(8,128)} %add_dynamic-update-slice_fusion, f32[8,128,64]{1,2,0:T(8,128)S(1)} %copy.121, f32[8,8]{1,0:T(8,128)S(1)} %copy-done.8), kind=kLoop, calls=%fused_computation.17 | loop fusion | flops 1572864 | bytes 3408128 | tf_op jit(solution)/shard_map/convert_element_type | solution.py:95
  172.8 4.2 %all-to-all-start.3 = ((bf16[8,8,128,64]{2,3,1,0:T(8,128)(2,1)}), bf16[8,8,128,64]{2,3,1,0:T(8,128)(2,1)}, u32[]{:S(2)}, u32[]{:S(2)}) async-start(bf16[8,8,128,64]{2,3,1,0:T(8,128)(2,1)} %add_convert_fusion), calls=%async_computation.3 | async-start | bytes 2097152 | tf_op jit(solution)/shard_map/all_to_all | solution.py:95
  177.2 25.0 %all-to-all-done.3 = bf16[8,8,128,64]{2,3,1,0:T(8,128)(2,1)} async-done(((bf16[8,8,128,64]{2,3,1,0:T(8,128)(2,1)}), bf16[8,8,128,64]{2,3,1,0:T(8,128)(2,1)}, u32[]{:S(2)}, u32[]{:S(2)}) %all-to-all-start.3) | async-done | bytes 1048608 | tf_op jit(solution)/shard_map/all_to_all | solution.py:95
  202.2 4.2 %fusion.7 = (bf16[64,128,64]{1,2,0:T(8,128)(2,1)S(1)}, bf16[64,128,64]{1,2,0:T(8,128)(2,1)}) fusion(bf16[8,8,128,64]{2,3,1,0:T(8,128)(2,1)} %all-to-all-done.3, f32[64]{0:T(128)S(1)} %fusion.34, pred[]{:T(512)S(6)} %eq.2, f32[64,128,64]{1,2,0:T(8,128)} %collective-permute-done, f32[128,128,64]{1,2,0:T(8,128)} %bitcast.163, s32[]{:T(128)S(6)} %select_n.67), kind=kLoop, calls=%fused_computation.13 | loop fusion | flops 4194304 | bytes 7340293 | tf_op jit(solution)/shard_map/convert_element_type | solution.py:99
  206.4 5.9 %collective-permute-start.1 = (bf16[64,128,64]{1,2,0:T(8,128)(2,1)}, bf16[64,128,64]{1,2,0:T(8,128)(2,1)}, u32[]{:S(2)}, u32[]{:S(2)}) collective-permute-start(bf16[64,128,64]{1,2,0:T(8,128)(2,1)} %get-tuple-element.18), channel_id=1, source_target_pairs={{0,1},{1,0},{2,3},{3,2},{4,5},{5,4},{6,7},{7,6},{8,9},{9,8},{10,11... | collective-permute-start | bytes 3145736 | tf_op jit(solution)/shard_map/ppermute | solution.py:12
  218.2 2.7 %fusion.1 = bf16[128,128,128]{2,1,0:T(8,128)(2,1)S(1)} fusion(f32[128,128]{1,0:T(8,128)S(1)} %copy.102, f32[128,128]{1,0:T(8,128)S(1)} %copy.100, f32[8,128,128]{2,1,0:T(8,128)S(1)} %fusion.17, pred[128,128]{1,0:T(8,128)(4,1)S(1)} %iota_compare_fusion), kind=kLoop, calls=%fused_computation.2 | loop fusion | flops 12582912 | bytes 4866048 | tf_op jit(solution)/shard_map/convert_element_type | solution.py:114
  223.7 4.5 %fusion.4 = bf16[128,128,64]{0,2,1:T(8,128)(2,1)} fusion(f32[8,16,64,128]{3,2,1,0:T(8,128)S(1)} %fusion.22, bf16[128,128,64]{0,2,1:T(8,128)(2,1)S(1)} %bitcast.165, bf16[128,128,128]{2,1,0:T(8,128)(2,1)S(1)} %fusion.1, f32[128]{0:T(128)S(1)} %mul.258, f32[128,128]{0,1:T(8,128)S(1)} %copy-done.6), kind=kOutput, calls=%fused_computation.6 | convolution fusion | flops 274726912 | bytes 12648960 | tf_op jit(solution)/shard_map/hts,shp->thp/dot_general | solution.py:115
  228.1 4.1 %copy.123 = bf16[128,8192]{1,0:T(8,128)(2,1)} copy(bf16[128,8192]{0,1:T(8,128)(2,1)} %bitcast.166) | data formatting | bytes 4194304 | tf_op jit(solution)/shard_map/reshape | solution.py:122
  (102 shorter events, 48.3 us)
Async XLA Ops:
  0.9 1.4 copy-start.4
  2.5 3.3 %copy-start.2 = (bf16[128,1024]{1,0:T(8,128)(2,1)S(1)}, bf16[128,1024]{1,0:T(8,128)(2,1)}, u32[]{:S(2)}) copy-start(bf16[128,1024]{1,0:T(8,128)(2,1)} %param.9) | copy-start | bytes 786436
  6.5 2.6 %copy-start = (f32[8,16,64,128]{3,2,1,0:T(8,128)}, f32[8,16,64,128]{3,2,1,0:T(8,128)S(1)}, u32[]{:S(2)}) copy-start(f32[8,16,64,128]{3,2,1,0:T(8,128)S(1)} %fusion.9) | copy-start | bytes 12582916
  6.5 13.5 %copy-start.15 = (f32[8]{0:T(128)S(1)}, f32[8]{0:T(128)}, u32[]{:S(2)}) copy-start(f32[8]{0:T(128)} %param.11) | copy-start | bytes 100
  9.1 57.5 %collective-permute-start = (f32[64,128,64]{1,2,0:T(8,128)}, f32[64,128,64]{1,2,0:T(8,128)}, u32[]{:S(2)}, u32[]{:S(2)}) collective-permute-start(f32[64,128,64]{1,2,0:T(8,128)} %constant_dynamic-slice_fusion.1), channel_id=1, source_target_pairs={{0,1},{1,0},{2,3},{3,2},{4,5},{5,4},{6,7},{7,6},{8,9},{9,8},{10,11... | collective-permute-start | bytes 6291464 | tf_op jit(solution)/shard_map/ppermute | solution.py:12
  70.2 30.7 %all-to-all-start = ((bf16[8,8,128,64]{2,3,1,0:T(8,128)(2,1)}), bf16[8,8,128,64]{2,3,1,0:T(8,128)(2,1)S(1)}, u32[]{:S(2)}, u32[]{:S(2)}) async-start(bf16[8,8,128,64]{2,3,1,0:T(8,128)(2,1)} %bitcast.168), calls=%async_computation | async-start | bytes 2097152 | tf_op jit(solution)/shard_map/all_to_all | solution.py:57
  76.3 40.8 %copy-start.9 = (f32[8]{0:T(128)}, f32[8]{0:T(128)S(1)}, u32[]{:S(2)}) copy-start(f32[8]{0:T(128)S(1)} %get-tuple-element.35) | copy-start | bytes 100
  76.3 40.8 %copy-start.11 = (f32[8]{0:T(128)}, f32[8]{0:T(128)S(1)}, u32[]{:S(2)}) copy-start(f32[8]{0:T(128)S(1)} %get-tuple-element.34) | copy-start | bytes 100
  76.3 40.8 %copy-start.13 = (f32[8]{0:T(128)}, f32[8]{0:T(128)S(1)}, u32[]{:S(2)}) copy-start(f32[8]{0:T(128)S(1)} %get-tuple-element.33) | copy-start | bytes 100
  123.0 20.5 %all-to-all-start.1 = ((f32[32,1,2560]{2,1,0:T(1,128)}), f32[32,1,2560]{2,1,0:T(1,128)S(1)}, u32[]{:S(2)}, u32[]{:S(2)}) async-start(f32[32,1,2560]{2,1,0:T(1,128)} %reshape.313), calls=%async_computation.1 | async-start | bytes 655360 | tf_op jit(solution)/shard_map/all_to_all | solution.py:78
  132.9 2.5 %copy-start.1 = (f32[8,8,128,64]{2,3,1,0:T(8,128)}, f32[8,8,128,64]{2,3,1,0:T(8,128)S(1)}, u32[]{:S(2)}) copy-start(f32[8,8,128,64]{2,3,1,0:T(8,128)S(1)} %convert_element_type.50) | copy-start | bytes 6291460
  148.0 9.8 %copy-start.10 = (f32[8]{0:T(128)S(1)}, f32[8]{0:T(128)}, u32[]{:S(2)}) copy-start(f32[8]{0:T(128)} %copy-done.9) | copy-start | bytes 100
  150.9 8.6 %copy-start.12 = (f32[8]{0:T(128)S(1)}, f32[8]{0:T(128)}, u32[]{:S(2)}) copy-start(f32[8]{0:T(128)} %copy-done.11) | copy-start | bytes 100
  151.8 9.5 %copy-start.14 = (f32[8]{0:T(128)S(1)}, f32[8]{0:T(128)}, u32[]{:S(2)}) copy-start(f32[8]{0:T(128)} %copy-done.13) | copy-start | bytes 100
  153.4 14.6 %all-to-all-start.2 = ((f32[32,1,2048]{2,1,0:T(1,128)}), f32[32,1,2048]{2,1,0:T(1,128)S(1)}, u32[]{:S(2)}, u32[]{:S(2)}) async-start(f32[32,1,2048]{2,1,0:T(1,128)} %reshape.315), calls=%async_computation.2 | async-start | bytes 524288 | tf_op jit(solution)/shard_map/all_to_all | solution.py:91
  161.4 8.5 %copy-start.8 = (f32[8,8]{1,0:T(8,128)S(1)}, f32[8,8]{1,0:T(8,128)}, u32[]{:S(2)}) copy-start(f32[8,8]{1,0:T(8,128)} %exp.116) | copy-start | bytes 772
  169.8 7.2 %copy-start.16 = (f32[1,1,128]{2,1,0:T(1,128)S(1)}, f32[1,1,128]{2,1,0:T(1,128)}, u32[]{:S(2)}) copy-start(f32[1,1,128]{2,1,0:T(1,128)} %get-tuple-element.40) | copy-start | bytes 1540
  172.8 29.4 %all-to-all-start.3 = ((bf16[8,8,128,64]{2,3,1,0:T(8,128)(2,1)}), bf16[8,8,128,64]{2,3,1,0:T(8,128)(2,1)}, u32[]{:S(2)}, u32[]{:S(2)}) async-start(bf16[8,8,128,64]{2,3,1,0:T(8,128)(2,1)} %add_convert_fusion), calls=%async_computation.3 | async-start | bytes 2097152 | tf_op jit(solution)/shard_map/all_to_all | solution.py:95
  177.2 35.7 %copy-start.7 = (f32[128,128]{1,0:T(8,128)S(1)}, f32[128,128]{1,0:T(8,128)}, u32[]{:S(2)}) copy-start(f32[128,128]{1,0:T(8,128)} %get-tuple-element.27) | copy-start | bytes 196612
  177.2 37.2 %copy-start.5 = (f32[128,128]{1,0:T(8,128)S(1)}, f32[128,128]{1,0:T(8,128)}, u32[]{:S(2)}) copy-start(f32[128,128]{1,0:T(8,128)} %copy-done.4) | copy-start | bytes 196612
  202.2 10.6 %copy-start.3 = (bf16[128,1024]{1,0:T(8,128)(2,1)S(1)}, bf16[128,1024]{1,0:T(8,128)(2,1)}, u32[]{:S(2)}) copy-start(bf16[128,1024]{1,0:T(8,128)(2,1)} %param.10) | copy-start | bytes 786436
  206.4 14.5 %collective-permute-start.1 = (bf16[64,128,64]{1,2,0:T(8,128)(2,1)}, bf16[64,128,64]{1,2,0:T(8,128)(2,1)}, u32[]{:S(2)}, u32[]{:S(2)}) collective-permute-start(bf16[64,128,64]{1,2,0:T(8,128)(2,1)} %get-tuple-element.18), channel_id=1, source_target_pairs={{0,1},{1,0},{2,3},{3,2},{4,5},{5,4},{6,7},{7,6},{8,9},{9,8},{10,11... | collective-permute-start | bytes 3145736 | tf_op jit(solution)/shard_map/ppermute | solution.py:12
  222.8 0.8 copy-start.6

commit v3 on v2

--- a/solution.py
+++ b/solution.py
@@ -10,6 +10,33 @@
 
 def swap(value):
     return lax.ppermute(value, "core", [(0, 1), (1, 0)])
+
+
+def split3(value):
+    hi = lax.reduce_precision(value, exponent_bits=8, mantissa_bits=7)
+    rest = value - hi
+    mid = lax.reduce_precision(rest, exponent_bits=8, mantissa_bits=7)
+    return jnp.stack([hi, mid, rest - mid], axis=-1).astype(jnp.bfloat16)
+
+
+def join3(parts):
+    parts = parts.astype(jnp.float32)
+    return (parts[..., 0] + parts[..., 1]) + parts[..., 2]
+
+
+def lower_mask(outs, ins):
+    return (jnp.arange(ins)[None, :] < jnp.arange(outs)[:, None]).astype(jnp.float32)
+
+
+def decay_matrix(totals, outs):
+    count = totals.shape[0]
+    a = jnp.arange(outs)[:, None, None]
+    b = jnp.arange(count)[None, :, None]
+    m = jnp.arange(count)[None, None, :]
+    between = ((b < m) & (m < a)).astype(jnp.float32)
+    exponent = jnp.einsum("abm,mh->hab", between, totals, precision=lax.Precision.HIGHEST)
+    earlier = (b < a)[None, :, :, 0]
+    return jnp.where(earlier, jnp.exp(jnp.where(earlier, exponent, 0.0)), 0.0)
 
 
 def local(features, increment_per_head, token_log_decay, b_matrix, c_matrix, skip_gain):
@@ -33,9 +60,14 @@
     total = within[-1]
     b = b_matrix.reshape(tokens, G, state)
     c = c_matrix.reshape(tokens, G, state)
-    small = lax.all_gather(jnp.concatenate([total, skip_gain.astype(f32)]), ("z", "core"))
-    totals = small[:, :heads].reshape(n_z, n_core, heads)
-    skip = small[:, heads:].reshape(heads)
+    partner = swap(jnp.concatenate([total, skip_gain.astype(f32)]))
+    t_first = jnp.where(c_idx == 0, total, partner[:heads])
+    t_second = jnp.where(c_idx == 0, partner[:heads], total)
+    chip_skip = jnp.where(
+        c_idx == 0,
+        jnp.concatenate([skip_gain.astype(f32), partner[heads:]]),
+        jnp.concatenate([partner[heads:], skip_gain.astype(f32)]),
+    )
 
     factor = jnp.exp(total[None, :] - within) * step
     scaled = (x * factor[..., None]).astype(bf16)
@@ -48,24 +80,40 @@
     got = swap(lax.dynamic_slice_in_dim(update, (1 - c_idx) * half, half, 0))
     first = jnp.where(c_idx == 0, own, got)
     second = jnp.where(c_idx == 0, got, own)
-    mine = lax.dynamic_index_in_dim(totals, z_idx, 0, keepdims=False)
-    t_first = lax.dynamic_slice_in_dim(mine[0], c_idx * half, half)
-    t_second = lax.dynamic_slice_in_dim(mine[1], c_idx * half, half)
+    t_first = lax.dynamic_slice_in_dim(t_first, c_idx * half, half)
+    t_second = lax.dynamic_slice_in_dim(t_second, c_idx * half, half)
     pair = jnp.exp(t_second)[:, None, None] * first + second
 
     pair = pair.astype(bf16).reshape(n_z, quarter, state, width)
-    rows = lax.all_to_all(pair, "z", 0, 0, tiled=True).astype(f32)
-    chip_totals = lax.dynamic_slice_in_dim(
-        totals[:, 0] + totals[:, 1], c_idx * half + z_idx * quarter, quarter, 1
+    per_chip = chip_skip.shape[0]
+    extra = jnp.concatenate(
+        [
+            split3((t_first + t_second).reshape(n_z, quarter)),
+            jnp.broadcast_to(
+                split3(chip_skip.reshape(quarter, per_chip // quarter)).reshape(1, quarter, -1),
+                (n_z, quarter, 3 * per_chip // quarter),
+            ),
+        ],
+        axis=-1,
     )
-    run = jnp.zeros((quarter, state, width), f32)
-    before = jnp.zeros((quarter,), f32)
-    starts, lead = [], []
-    for chip in range(n_z):
-        starts.append(run)
-        lead.append(before)
-        run = jnp.exp(chip_totals[chip])[:, None, None] * run + rows[chip]
-        before = before + chip_totals[chip]
+    extra = jnp.pad(extra, ((0, 0), (0, 0), (0, width - extra.shape[-1])))
+    message = jnp.concatenate([pair, extra[:, :, None, :]], axis=2)
+    rows = lax.all_to_all(message, "z", 0, 0, tiled=True)
+    chip_totals = join3(rows[:, :, state, 0:3])
+    skip = join3(
+        rows[:, :, state, 3 : 3 + 3 * per_chip // quarter].reshape(n_z, quarter, -1, 3)
+    ).reshape(heads)
+    scan = jnp.einsum(
+        "hab,bhnp->ahnp",
+        decay_matrix(chip_totals, n_z + 1),
+        rows[:, :, :state].astype(f32),
+        precision=lax.Precision.HIGHEST,
+    )
+    leads = jnp.einsum(
+        "am,mh->ah", lower_mask(n_z + 1, n_z), chip_totals, precision=lax.Precision.HIGHEST
+    )
+    starts, run = scan[:n_z], scan[n_z]
+    lead, before = leads[:n_z], leads[n_z]
 
     piece = state // n_seq
     packed = jnp.concatenate(
@@ -78,20 +126,14 @@
     gathered = lax.all_to_all(packed, "seq", 0, 0, tiled=True)
     row_state = gathered[:, :, :piece]
     row_total = gathered[:, :, piece, 0]
-    order = jnp.arange(n_seq)
-    between = (order[None, None, :] > order[None, :, None]) & (order[None, None, :] < order[:, None, None])
-    exponent = jnp.einsum(
-        "abi,ih->hab", between.astype(f32), row_total, precision=lax.Precision.HIGHEST
-    )
-    earlier = (order[None, :] < order[:, None])[None]
-    decay = jnp.where(earlier, jnp.exp(jnp.where(earlier, exponent, 0.0)), 0.0)
     entering = jnp.einsum(
-        "hab,bhrw->ahrw", decay, row_state, precision=lax.Precision.HIGHEST
+        "hab,bhrw->ahrw", decay_matrix(row_total, n_seq), row_state,
+        precision=lax.Precision.HIGHEST,
     )
     acc_s = lax.all_to_all(entering, "seq", 0, 0, tiled=True)
     acc_s = acc_s.transpose(1, 0, 2, 3).reshape(quarter, state, width)
 
-    chip_in = jnp.stack(starts) + jnp.exp(jnp.stack(lead))[:, :, None, None] * acc_s[None]
+    chip_in = starts + jnp.exp(lead)[:, :, None, None] * acc_s[None]
     back = lax.all_to_all(chip_in.astype(bf16), "z", 0, 0, tiled=True)
     entry = back.astype(f32).reshape(half, state, width)
 

time: 234 us -> 199 us (0.85)
  local copies, waits for them, and re-layouts: 40.9 us -> 26.1 us
  blocking collectives: 45.8 us -> 31.5 us
  other arithmetic: 35.8 us -> 21.8 us
  waiting for transfers between devices: 61.8 us -> 70.9 us
    unnamed x1 -> x0, blocking collectives: 45.8 us -> none
    all_to_all x0 -> x1, blocking collectives: none -> 31.5 us  [local(): back = lax.all_to_all(chip_in.astype(bf16), 'z', 0, 0, tiled=True)]
    slice x14 -> x7, local copies, waits for them, and re-layouts: 17.2 us -> 3.81 us  [the longest x1 1.33 us: local(): rows[:, :, :state].astype(f32)]
    unnamed x8 -> x1, other arithmetic: 7.93 us -> 0.05 us
    all_to_all x1, waiting for transfers between devices: 4.87 us -> 10.2 us  [local(): acc_s = lax.all_to_all(entering, 'seq', 0, 0, tiled=True)]
    all_to_all x2 -> x1, starting transfers between devices: 8.14 us -> 4.66 us  [local(): rows = lax.all_to_all(message, 'z', 0, 0, tiled=True)]
    all_to_all x1, waiting for transfers between devices: 7.21 us -> 10.7 us  [local(): gathered = lax.all_to_all(packed, 'seq', 0, 0, tiled=True)]
    add x3 -> x1, other arithmetic: 2.81 us -> 0.01 us  [join3(): return parts[..., 0] + parts[..., 1] + parts[..., 2]]
  transfers between devices with their start and end apart: 6 -> 6, of which waited for: 4 -> 4; matrix products, arithmetic and copies ran while one was open for 9% -> 6% of each run, Pallas kernels for 0% -> 0%
where the time goes in v3:
time: 199 us; the launch traced here: 198 us
  waiting for transfers between devices  70.9 us (36%)
  starting transfers between devices  35.3 us (18%)
  blocking collectives  31.5 us (16%)
  local copies, waits for them, and re-layouts  26.1 us (13%)
  other arithmetic  21.8 us (11%)
  matrix products  11.7 us (6%)
    all_to_all x1, waiting for transfers between devices, local(): rows = lax.all_to_all(message, 'z', 0, 0, tiled=True)  48.4 us
    all_to_all x1, blocking collectives, local(): back = lax.all_to_all(chip_in.astype(bf16), 'z', 0, 0, tiled=True)  31.5 us
    ppermute x3, starting transfers between devices, swap(): return lax.ppermute(value, 'core', [(0, 1), (1, 0)])  16.5 us
    unnamed x26, local copies, waits for them, and re-layouts  11.4 us
    all_to_all x1, waiting for transfers between devices, local(): gathered = lax.all_to_all(packed, 'seq', 0, 0, tiled=True)  10.7 us
    all_to_all x1, waiting for transfers between devices, local(): acc_s = lax.all_to_all(entering, 'seq', 0, 0, tiled=True)  10.2 us
    all_to_all x1, starting transfers between devices, local(): gathered = lax.all_to_all(packed, 'seq', 0, 0, tiled=True)  9.67 us
    all_to_all x1, starting transfers between devices, local(): rows = lax.all_to_all(message, 'z', 0, 0, tiled=True)  4.66 us
  transfers between devices with their start and end apart: 6, of which 4 were waited for; matrix products, arithmetic and copies ran while one was open for 6% of the time, Pallas kernels for 0%

profile of v3, /device:TPU:1, one launch (start us, length us, event | category | flops | bytes accessed | tf_op | source)
XLA Modules:
  0.0 197.8 jit_solution(17303160758807033774)
XLA Ops:
  1.8 3.3 %copy.99 = bf16[128,8192]{0,1:T(8,128)(2,1)S(1)} copy(bf16[128,8192]{1,0:T(8,128)(2,1)} %param.6) | data formatting | bytes 4194304 | tf_op args[0]
  5.9 1.6 constant_dynamic-slice_fusion
  8.6 8.8 %collective-permute-start.1 = (f32[64,128,64]{1,2,0:T(8,128)}, f32[64,128,64]{1,2,0:T(8,128)}, u32[]{:S(2)}, u32[]{:S(2)}) collective-permute-start(f32[64,128,64]{1,2,0:T(8,128)} %constant_dynamic-slice_fusion), channel_id=1, source_target_pairs={{0,1},{1,0},{2,3},{3,2},{4,5},{5,4},{6,7},{7,6},{8,9},{9,8},{10,11... | collective-permute-start | bytes 6291464 | tf_op jit(solution)/shard_map/ppermute | solution.py:12
  17.4 1.9 collective-permute-start
  19.5 1.6 collective-permute-done
  22.8 2.6 %add_convert_fusion = bf16[64,128,64]{1,2,0:T(8,128)(2,1)S(1)} fusion(f32[64,128,64]{1,2,0:T(8,128)} %collective-permute-done.1, f32[128,128,64]{1,2,0:T(8,128)} %bitcast.106, s32[]{:T(128)S(6)} %select_n.103, f32[64]{0:T(128)S(1)} %get-tuple-element.20, pred[]{:T(512)S(6)} %eq.2), kind=kLoop, calls=%fused_computation.21 | loop fusion | flops 2621440 | bytes 5243141 | tf_op jit(solution)/shard_map/convert_element_type | solution.py:87
  25.5 2.0 %pad_maximum_fusion = bf16[8,8,129,64]{2,3,1,0:T(8,128)(2,1)} fusion(bf16[8,8,1,64]{2,3,1,0:T(8,128)(2,1)S(1)} %copy.113, bf16[8,8,128,64]{2,3,1,0:T(8,128)(2,1)S(1)} %bitcast.112), kind=kLoop, calls=%fused_computation.19 | loop fusion | flops 2113536 | bytes 2113536 | tf_op jit(solution)/shard_map/concatenate | solution.py:100
  27.5 4.7 %all-to-all-start = ((bf16[8,8,129,64]{2,3,1,0:T(8,128)(2,1)}), bf16[8,8,129,64]{2,3,1,0:T(8,128)(2,1)}, u32[]{:S(2)}, u32[]{:S(2)}) async-start(bf16[8,8,129,64]{2,3,1,0:T(8,128)(2,1)} %pad_maximum_fusion), calls=%async_computation | async-start | bytes 4194304 | tf_op jit(solution)/shard_map/all_to_all | solution.py:101
  32.2 48.4 %all-to-all-done = bf16[8,8,129,64]{2,3,1,0:T(8,128)(2,1)} async-done(((bf16[8,8,129,64]{2,3,1,0:T(8,128)(2,1)}), bf16[8,8,129,64]{2,3,1,0:T(8,128)(2,1)}, u32[]{:S(2)}, u32[]{:S(2)}) %all-to-all-start) | async-done | bytes 1056800 | tf_op jit(solution)/shard_map/all_to_all | solution.py:101
  83.5 2.1 %convolution_bitcast_fusion = f32[9,8,128,64]{2,0,3,1:T(8,128)S(1)} fusion(bf16[8,8,128,64]{2,3,1,0:T(8,128)(2,1)S(1)} %slice.83, f32[8,9,8,1]{1,0,2,3:T(8,128)S(1)} %fusion.18), kind=kOutput, calls=%fused_computation.12 | convolution fusion | flops 56623104 | bytes 3410176 | tf_op jit(solution)/shard_map/hab,bhnp->ahnp/dot_general | solution.py:106
  85.6 2.0 copy-done.3
  89.4 9.7 %all-to-all-start.1 = ((f32[32,1,2560]{2,1,0:T(1,128)}), f32[32,1,2560]{2,1,0:T(1,128)S(1)}, u32[]{:S(2)}, u32[]{:S(2)}) async-start(f32[32,1,2560]{2,1,0:T(1,128)} %reshape.395), calls=%async_computation.1 | async-start | bytes 655360 | tf_op jit(solution)/shard_map/all_to_all | solution.py:126
  99.1 10.7 %all-to-all-done.1 = f32[32,1,2560]{2,1,0:T(1,128)S(1)} async-done(((f32[32,1,2560]{2,1,0:T(1,128)}), f32[32,1,2560]{2,1,0:T(1,128)S(1)}, u32[]{:S(2)}, u32[]{:S(2)}) %all-to-all-start.1) | async-done | bytes 327712 | tf_op jit(solution)/shard_map/all_to_all | solution.py:126
  115.6 4.4 %all-to-all-start.2 = ((f32[32,1,2048]{2,1,0:T(1,128)}), f32[32,1,2048]{2,1,0:T(1,128)S(1)}, u32[]{:S(2)}, u32[]{:S(2)}) async-start(f32[32,1,2048]{2,1,0:T(1,128)} %reshape.397), calls=%async_computation.2 | async-start | bytes 524288 | tf_op jit(solution)/shard_map/all_to_all | solution.py:133
  120.1 10.2 %all-to-all-done.2 = f32[32,1,2048]{2,1,0:T(1,128)S(1)} async-done(((f32[32,1,2048]{2,1,0:T(1,128)}), f32[32,1,2048]{2,1,0:T(1,128)S(1)}, u32[]{:S(2)}, u32[]{:S(2)}) %all-to-all-start.2) | async-done | bytes 262176 | tf_op jit(solution)/shard_map/all_to_all | solution.py:133
  132.1 1.9 fusion.11
  134.3 31.5 %all_to_all.20 = bf16[8,8,128,64]{2,3,1,0:T(8,128)(2,1)S(1)} all-to-all(bf16[8,8,128,64]{2,3,1,0:T(8,128)(2,1)S(1)} %copy.125), channel_id=1, replica_groups=mesh['seq'=32,'z'=8,'core'=2] {'z'}, dimensions={0} | all-to-all | bytes 2097152 | tf_op jit(solution)/shard_map/all_to_all | solution.py:137
  165.8 3.3 %fusion.7 = (bf16[64,128,64]{1,2,0:T(8,128)(2,1)S(1)}, bf16[64,128,64]{1,2,0:T(8,128)(2,1)}) fusion(bf16[8,8,128,64]{2,3,1,0:T(8,128)(2,1)S(1)} %all_to_all.20, f32[64]{0:T(128)S(1)} %get-tuple-element.18, pred[]{:T(512)S(6)} %eq.2, f32[64,128,64]{1,2,0:T(8,128)} %collective-permute-done.1, f32[128,128,64]{1,2,0:T(8,128)S(1)} %bitcast.107, s32[]{:T(128)S(6)} %select_n.103), kind=kLoop, calls=%fused_computation.14 | loop fusion | flops 4194304 | bytes 7340293 | tf_op jit(solution)/shard_map/convert_element_type | solution.py:141
  169.1 5.8 %collective-permute-start.2 = (bf16[64,128,64]{1,2,0:T(8,128)(2,1)}, bf16[64,128,64]{1,2,0:T(8,128)(2,1)}, u32[]{:S(2)}, u32[]{:S(2)}) collective-permute-start(bf16[64,128,64]{1,2,0:T(8,128)(2,1)} %get-tuple-element.8), channel_id=1, source_target_pairs={{0,1},{1,0},{2,3},{3,2},{4,5},{5,4},{6,7},{7,6},{8,9},{9,8},{10,11... | collective-permute-start | bytes 3145736 | tf_op jit(solution)/shard_map/ppermute | solution.py:12
  179.5 4.0 %fusion.1 = bf16[128,128,128]{2,1,0:T(8,128)(2,1)} fusion(f32[128,128]{1,0:T(8,128)S(1)} %copy.98, f32[128,128]{1,0:T(8,128)S(1)} %copy.96, f32[8,128,128]{2,1,0:T(8,128)S(1)} %fusion.22, pred[128,128]{1,0:T(8,128)(4,1)S(1)} %iota_compare_fusion), kind=kLoop, calls=%fused_computation.2 | loop fusion | flops 12582912 | bytes 4866048 | tf_op jit(solution)/shard_map/convert_element_type | solution.py:156
  185.2 1.9 maximum_select_fusion
  187.8 1.5 copy-done.2
  189.2 4.5 %fusion.4 = bf16[128,128,64]{0,2,1:T(8,128)(2,1)} fusion(f32[8,16,64,128]{3,2,1,0:T(8,128)S(1)} %fusion.27, bf16[128,128,64]{0,2,1:T(8,128)(2,1)S(1)} %bitcast.109, bf16[128,128,128]{2,1,0:T(8,128)(2,1)S(1)} %copy-done.2, f32[128]{0:T(128)S(1)} %add.68, f32[128,128]{0,1:T(8,128)S(1)} %copy-done.6), kind=kOutput, calls=%fused_computation.6 | convolution fusion | flops 274726912 | bytes 12648960 | tf_op jit(solution)/shard_map/hts,shp->thp/dot_general | solution.py:157
  193.7 4.1 %copy.129 = bf16[128,8192]{1,0:T(8,128)(2,1)} copy(bf16[128,8192]{0,1:T(8,128)(2,1)} %bitcast.110) | data formatting | bytes 4194304 | tf_op jit(solution)/shard_map/reshape | solution.py:164
  (88 shorter events, 25.1 us)
Async XLA Ops:
  1.8 3.3 %copy-start.4 = (bf16[128,1024]{1,0:T(8,128)(2,1)S(1)}, bf16[128,1024]{1,0:T(8,128)(2,1)}, u32[]{:S(2)}) copy-start(bf16[128,1024]{1,0:T(8,128)(2,1)} %param.9) | copy-start | bytes 786436
  5.9 2.7 %copy-start = (f32[8,16,64,128]{3,2,1,0:T(8,128)}, f32[8,16,64,128]{3,2,1,0:T(8,128)S(1)}, u32[]{:S(2)}) copy-start(f32[8,16,64,128]{3,2,1,0:T(8,128)S(1)} %fusion.9) | copy-start | bytes 12582916
  5.9 11.5 %copy-start.7 = (f32[8]{0:T(128)S(1)}, f32[8]{0:T(128)}, u32[]{:S(2)}) copy-start(f32[8]{0:T(128)} %param.11) | copy-start | bytes 100
  8.6 14.3 %collective-permute-start.1 = (f32[64,128,64]{1,2,0:T(8,128)}, f32[64,128,64]{1,2,0:T(8,128)}, u32[]{:S(2)}, u32[]{:S(2)}) collective-permute-start(f32[64,128,64]{1,2,0:T(8,128)} %constant_dynamic-slice_fusion), channel_id=1, source_target_pairs={{0,1},{1,0},{2,3},{3,2},{4,5},{5,4},{6,7},{7,6},{8,9},{9,8},{10,11... | collective-permute-start | bytes 6291464 | tf_op jit(solution)/shard_map/ppermute | solution.py:12
  17.4 3.7 %collective-permute-start = (f32[136]{0:T(256)S(1)}, f32[136]{0:T(256)S(1)}, u32[]{:S(2)}, u32[]{:S(2)}) collective-permute-start(f32[136]{0:T(256)S(1)} %pad_maximum_fusion.2), channel_id=1, source_target_pairs={{0,1},{1,0},{2,3},{3,2},{4,5},{5,4},{6,7},{7,6},{8,9},{9,8},{10,11... | collective-permute-start | bytes 1640 | tf_op jit(solution)/shard_map/ppermute | solution.py:12
  27.5 53.1 %all-to-all-start = ((bf16[8,8,129,64]{2,3,1,0:T(8,128)(2,1)}), bf16[8,8,129,64]{2,3,1,0:T(8,128)(2,1)}, u32[]{:S(2)}, u32[]{:S(2)}) async-start(bf16[8,8,129,64]{2,3,1,0:T(8,128)(2,1)} %pad_maximum_fusion), calls=%async_computation | async-start | bytes 4194304 | tf_op jit(solution)/shard_map/all_to_all | solution.py:101
  85.6 2.0 copy-start.3
  89.4 20.4 %all-to-all-start.1 = ((f32[32,1,2560]{2,1,0:T(1,128)}), f32[32,1,2560]{2,1,0:T(1,128)S(1)}, u32[]{:S(2)}, u32[]{:S(2)}) async-start(f32[32,1,2560]{2,1,0:T(1,128)} %reshape.395), calls=%async_computation.1 | async-start | bytes 655360 | tf_op jit(solution)/shard_map/all_to_all | solution.py:126
  115.6 14.7 %all-to-all-start.2 = ((f32[32,1,2048]{2,1,0:T(1,128)}), f32[32,1,2048]{2,1,0:T(1,128)S(1)}, u32[]{:S(2)}, u32[]{:S(2)}) async-start(f32[32,1,2048]{2,1,0:T(1,128)} %reshape.397), calls=%async_computation.2 | async-start | bytes 524288 | tf_op jit(solution)/shard_map/all_to_all | solution.py:133
  134.0 31.8 %copy-start.1 = (f32[8,16,64,128]{3,2,1,0:T(8,128)S(1)}, f32[8,16,64,128]{3,2,1,0:T(8,128)}, u32[]{:S(2)}) copy-start(f32[8,16,64,128]{3,2,1,0:T(8,128)} %copy-done) | copy-start | bytes 12582916
  165.8 9.1 %copy-start.5 = (bf16[128,1024]{1,0:T(8,128)(2,1)S(1)}, bf16[128,1024]{1,0:T(8,128)(2,1)}, u32[]{:S(2)}) copy-start(bf16[128,1024]{1,0:T(8,128)(2,1)} %param.10) | copy-start | bytes 786436
  169.1 16.1 %collective-permute-start.2 = (bf16[64,128,64]{1,2,0:T(8,128)(2,1)}, bf16[64,128,64]{1,2,0:T(8,128)(2,1)}, u32[]{:S(2)}, u32[]{:S(2)}) collective-permute-start(bf16[64,128,64]{1,2,0:T(8,128)(2,1)} %get-tuple-element.8), channel_id=1, source_target_pairs={{0,1},{1,0},{2,3},{3,2},{4,5},{5,4},{6,7},{7,6},{8,9},{9,8},{10,11... | collective-permute-start | bytes 3145736 | tf_op jit(solution)/shard_map/ppermute | solution.py:12
  187.0 2.2 %copy-start.2 = (bf16[128,128,128]{2,1,0:T(8,128)(2,1)S(1)}, bf16[128,128,128]{2,1,0:T(8,128)(2,1)}, u32[]{:S(2)}) copy-start(bf16[128,128,128]{2,1,0:T(8,128)(2,1)} %fusion.1) | copy-start | bytes 12582916
  187.0 2.2 %copy-start.6 = (f32[128,128]{0,1:T(8,128)S(1)}, f32[128,128]{0,1:T(8,128)}, u32[]{:S(2)}) copy-start(f32[128,128]{0,1:T(8,128)} %copy.100) | copy-start | bytes 196612

commit v4 on v3

--- a/solution.py
+++ b/solution.py
@@ -99,6 +99,16 @@
     extra = jnp.pad(extra, ((0, 0), (0, 0), (0, width - extra.shape[-1])))
     message = jnp.concatenate([pair, extra[:, :, None, :]], axis=2)
     rows = lax.all_to_all(message, "z", 0, 0, tiled=True)
+    scores = jnp.einsum("tgn,sgn->gts", c, b, preferred_element_type=f32)
+    scores = jnp.repeat(scores, per_group, axis=0)
+    causal = (jnp.arange(tokens)[:, None] >= jnp.arange(tokens)[None, :])[None]
+    w_t = within.T
+    gap = w_t[:, :, None] - w_t[:, None, :]
+    damping = jnp.where(causal, jnp.exp(jnp.where(causal, gap, 0.0)), 0.0)
+    weight = (scores * damping * step.T[:, None, :]).astype(bf16)
+    inside = jnp.einsum("hts,shp->thp", weight, x, preferred_element_type=f32)
+
+    inside, rows = lax.optimization_barrier((inside, rows))
     chip_totals = join3(rows[:, :, state, 0:3])
     skip = join3(
         rows[:, :, state, 3 : 3 + 3 * per_chip // quarter].reshape(n_z, quarter, -1, 3)
@@ -147,15 +157,6 @@
         jnp.concatenate([other, keep], axis=0),
     )
 
-    scores = jnp.einsum("tgn,sgn->gts", c, b, preferred_element_type=f32)
-    scores = jnp.repeat(scores, per_group, axis=0)
-    causal = (jnp.arange(tokens)[:, None] >= jnp.arange(tokens)[None, :])[None]
-    w_t = within.T
-    gap = w_t[:, :, None] - w_t[:, None, :]
-    damping = jnp.where(causal, jnp.exp(jnp.where(causal, gap, 0.0)), 0.0)
-    weight = (scores * damping * step.T[:, None, :]).astype(bf16)
-    inside = jnp.einsum("hts,shp->thp", weight, x, preferred_element_type=f32)
-
     outside = jnp.einsum(
         "tgn,ghnp->tghp", c, carried_in.reshape(G, per_group, state, width),
         preferred_element_type=f32,

time: 199 us -> 248 us (1.25)
  local copies, waits for them, and re-layouts: 26.1 us -> 81.9 us
  waiting for transfers between devices: 70.9 us -> 63.2 us
    optimization_barrier x0 -> x2, local copies, waits for them, and re-layouts: none -> 58.7 us  [local(): inside, rows = lax.optimization_barrier((inside, rows))]
    all_to_all x1, waiting for transfers between devices: 48.4 us -> 40.2 us  [local(): rows = lax.all_to_all(message, 'z', 0, 0, tiled=True)]
  transfers between devices with their start and end apart: 6 -> 6, of which waited for: 4 -> 5; matrix products, arithmetic and copies ran while one was open for 6% -> 5% of each run, Pallas kernels for 0% -> 0%
where the time goes in v4:
time: 248 us; the launch traced here: 247 us
  local copies, waits for them, and re-layouts  81.9 us (33%)
  waiting for transfers between devices  63.2 us (25%)
  starting transfers between devices  35.5 us (14%)
  blocking collectives  31.5 us (13%)
  other arithmetic  22.5 us (9%)
  matrix products  12.2 us (5%)
    optimization_barrier x2, local copies, waits for them, and re-layouts, local(): inside, rows = lax.optimization_barrier((inside, rows))  58.7 us
    all_to_all x1, waiting for transfers between devices, local(): rows = lax.all_to_all(message, 'z', 0, 0, tiled=True)  40.2 us
    all_to_all x1, blocking collectives, local(): back = lax.all_to_all(chip_in.astype(bf16), 'z', 0, 0, tiled=True)  31.5 us
    ppermute x3, starting transfers between devices, swap(): return lax.ppermute(value, 'core', [(0, 1), (1, 0)])  16.6 us
    unnamed x26, local copies, waits for them, and re-layouts  12.7 us
    all_to_all x1, waiting for transfers between devices, local(): gathered = lax.all_to_all(packed, 'seq', 0, 0, tiled=True)  10.5 us
    all_to_all x1, waiting for transfers between devices, local(): acc_s = lax.all_to_all(entering, 'seq', 0, 0, tiled=True)  10.4 us
    all_to_all x1, starting transfers between devices, local(): gathered = lax.all_to_all(packed, 'seq', 0, 0, tiled=True)  9.89 us
  transfers between devices with their start and end apart: 6, of which 5 were waited for; matrix products, arithmetic and copies ran while one was open for 5% of the time, Pallas kernels for 0%

profile of v4, /device:TPU:1, one launch (start us, length us, event | category | flops | bytes accessed | tf_op | source)
XLA Modules:
  0.0 247.2 jit_solution(18181773240149280860)
XLA Ops:
  3.4 3.2 %copy.99 = bf16[128,8192]{0,1:T(8,128)(2,1)S(1)} copy(bf16[128,8192]{1,0:T(8,128)(2,1)} %param.6) | data formatting | bytes 4194304 | tf_op args[0]
  10.0 8.8 %collective-permute-start.1 = (f32[64,128,64]{1,2,0:T(8,128)}, f32[64,128,64]{1,2,0:T(8,128)}, u32[]{:S(2)}, u32[]{:S(2)}) collective-permute-start(f32[64,128,64]{1,2,0:T(8,128)} %constant_dynamic-slice_fusion), channel_id=1, source_target_pairs={{0,1},{1,0},{2,3},{3,2},{4,5},{5,4},{6,7},{7,6},{8,9},{9,8},{10,11... | collective-permute-start | bytes 6291464 | tf_op jit(solution)/shard_map/ppermute | solution.py:12
  18.8 1.9 collective-permute-start
  24.3 2.6 %add_convert_fusion = bf16[64,128,64]{1,2,0:T(8,128)(2,1)S(1)} fusion(f32[64,128,64]{1,2,0:T(8,128)} %collective-permute-done.1, f32[128,128,64]{1,2,0:T(8,128)} %bitcast.111, s32[]{:T(128)S(6)} %select_n.101, f32[64]{0:T(128)S(1)} %get-tuple-element.24, pred[]{:T(512)S(6)} %eq.2), kind=kLoop, calls=%fused_computation.22 | loop fusion | flops 2621440 | bytes 5243141 | tf_op jit(solution)/shard_map/convert_element_type | solution.py:87
  26.9 2.0 pad_maximum_fusion
  28.9 4.8 %all-to-all-start = ((bf16[8,8,129,64]{2,3,1,0:T(8,128)(2,1)}), bf16[8,8,129,64]{2,3,1,0:T(8,128)(2,1)}, u32[]{:S(2)}, u32[]{:S(2)}) async-start(bf16[8,8,129,64]{2,3,1,0:T(8,128)(2,1)} %pad_maximum_fusion), calls=%async_computation | async-start | bytes 4194304 | tf_op jit(solution)/shard_map/all_to_all | solution.py:101
  34.3 2.7 %fusion.1 = bf16[128,128,128]{2,1,0:T(8,128)(2,1)S(1)} fusion(f32[128,128]{1,0:T(8,128)S(1)} %copy.98, f32[128,128]{1,0:T(8,128)S(1)} %copy.96, f32[8,128,128]{2,1,0:T(8,128)S(1)} %fusion.22, pred[128,128]{1,0:T(8,128)(4,1)S(1)} %iota_compare_fusion), kind=kLoop, calls=%fused_computation.2 | loop fusion | flops 12582912 | bytes 4866048 | tf_op jit(solution)/shard_map/convert_element_type | solution.py:108
  37.0 4.9 %convolution_bitcast_fusion.1 = f32[128,128,64]{0,2,1:T(8,128)} fusion(bf16[128,128,128]{2,1,0:T(8,128)(2,1)S(1)} %fusion.1, bf16[128,128,64]{0,2,1:T(8,128)(2,1)S(1)} %bitcast.108), kind=kOutput, calls=%fused_computation.13 | convolution fusion | flops 268435456 | bytes 10485760 | tf_op jit(solution)/shard_map/hts,shp->thp/dot_general | solution.py:109
  41.9 40.2 %all-to-all-done = bf16[8,8,129,64]{2,3,1,0:T(8,128)(2,1)} async-done(((bf16[8,8,129,64]{2,3,1,0:T(8,128)(2,1)}), bf16[8,8,129,64]{2,3,1,0:T(8,128)(2,1)}, u32[]{:S(2)}, u32[]{:S(2)}) %all-to-all-start) | async-done | bytes 1056800 | tf_op jit(solution)/shard_map/all_to_all | solution.py:101
  82.2 4.2 %copy.114 = bf16[8,8,129,64]{2,0,3,1:T(8,128)(2,1)} copy(bf16[8,8,129,64]{2,3,1,0:T(8,128)(2,1)} %all-to-all-done) | data formatting | bytes 2113536 | tf_op jit(solution)/shard_map/optimization_barrier | solution.py:111
  86.3 54.5 %copy.115 = bf16[8,8,129,64]{1,0,3,2:T(8,128)(2,1)} copy(bf16[8,8,129,64]{2,3,1,0:T(8,128)(2,1)} %all-to-all-done) | data formatting | bytes 2113536 | tf_op jit(solution)/shard_map/optimization_barrier | solution.py:111
  142.1 3.1 %convolution_bitcast_fusion = f32[9,8,128,64]{2,0,3,1:T(8,128)S(1)} fusion(bf16[8,8,129,64]{2,0,3,1:T(8,128)(2,1)} %copy.114, f32[8,9,8,1]{1,0,2,3:T(8,128)S(1)} %fusion.18), kind=kOutput, calls=%fused_computation.12 | convolution fusion | flops 56623104 | bytes 3410176 | tf_op jit(solution)/shard_map/hab,bhnp->ahnp/dot_general | solution.py:116
  145.3 2.0 copy-done.3
  148.9 9.9 %all-to-all-start.1 = ((f32[32,1,2560]{2,1,0:T(1,128)}), f32[32,1,2560]{2,1,0:T(1,128)S(1)}, u32[]{:S(2)}, u32[]{:S(2)}) async-start(f32[32,1,2560]{2,1,0:T(1,128)} %reshape.395), calls=%async_computation.1 | async-start | bytes 655360 | tf_op jit(solution)/shard_map/all_to_all | solution.py:136
  158.8 10.5 %all-to-all-done.1 = f32[32,1,2560]{2,1,0:T(1,128)S(1)} async-done(((f32[32,1,2560]{2,1,0:T(1,128)}), f32[32,1,2560]{2,1,0:T(1,128)S(1)}, u32[]{:S(2)}, u32[]{:S(2)}) %all-to-all-start.1) | async-done | bytes 327712 | tf_op jit(solution)/shard_map/all_to_all | solution.py:136
  175.1 4.2 %all-to-all-start.2 = ((f32[32,1,2048]{2,1,0:T(1,128)}), f32[32,1,2048]{2,1,0:T(1,128)S(1)}, u32[]{:S(2)}, u32[]{:S(2)}) async-start(f32[32,1,2048]{2,1,0:T(1,128)} %reshape.397), calls=%async_computation.2 | async-start | bytes 524288 | tf_op jit(solution)/shard_map/all_to_all | solution.py:143
  179.3 10.4 %all-to-all-done.2 = f32[32,1,2048]{2,1,0:T(1,128)S(1)} async-done(((f32[32,1,2048]{2,1,0:T(1,128)}), f32[32,1,2048]{2,1,0:T(1,128)S(1)}, u32[]{:S(2)}, u32[]{:S(2)}) %all-to-all-start.2) | async-done | bytes 262176 | tf_op jit(solution)/shard_map/all_to_all | solution.py:143
  191.5 1.9 fusion.11
  193.7 31.5 %all_to_all.20 = bf16[8,8,128,64]{2,3,1,0:T(8,128)(2,1)S(1)} all-to-all(bf16[8,8,128,64]{2,3,1,0:T(8,128)(2,1)S(1)} %copy.125), channel_id=1, replica_groups=mesh['seq'=32,'z'=8,'core'=2] {'z'}, dimensions={0} | all-to-all | bytes 2097152 | tf_op jit(solution)/shard_map/all_to_all | solution.py:147
  225.2 3.2 %fusion.7 = (bf16[64,128,64]{1,2,0:T(8,128)(2,1)S(1)}, bf16[64,128,64]{1,2,0:T(8,128)(2,1)}) fusion(bf16[8,8,128,64]{2,3,1,0:T(8,128)(2,1)S(1)} %all_to_all.20, f32[64]{0:T(128)S(1)} %get-tuple-element.22, pred[]{:T(512)S(6)} %eq.2, f32[64,128,64]{1,2,0:T(8,128)} %collective-permute-done.1, f32[128,128,64]{1,2,0:T(8,128)S(1)} %bitcast.112, s32[]{:T(128)S(6)} %select_n.101), kind=kLoop, calls=%fused_computation.15 | loop fusion | flops 4194304 | bytes 7340293 | tf_op jit(solution)/shard_map/convert_element_type | solution.py:151
  228.4 5.9 %collective-permute-start.2 = (bf16[64,128,64]{1,2,0:T(8,128)(2,1)}, bf16[64,128,64]{1,2,0:T(8,128)(2,1)}, u32[]{:S(2)}, u32[]{:S(2)}) collective-permute-start(bf16[64,128,64]{1,2,0:T(8,128)(2,1)} %get-tuple-element.12), channel_id=1, source_target_pairs={{0,1},{1,0},{2,3},{3,2},{4,5},{5,4},{6,7},{7,6},{8,9},{9,8},{10,11... | collective-permute-start | bytes 3145736 | tf_op jit(solution)/shard_map/ppermute | solution.py:12
  236.9 1.9 maximum_select_fusion
  240.9 2.2 fusion.4
  243.1 4.1 %copy.129 = bf16[128,8192]{1,0:T(8,128)(2,1)} copy(bf16[128,8192]{0,1:T(8,128)(2,1)} %bitcast.113) | data formatting | bytes 4194304 | tf_op jit(solution)/shard_map/reshape | solution.py:165
  (89 shorter events, 26.3 us)
Async XLA Ops:
  7.4 2.6 %copy-start = (f32[8,16,64,128]{3,2,1,0:T(8,128)}, f32[8,16,64,128]{3,2,1,0:T(8,128)S(1)}, u32[]{:S(2)}) copy-start(f32[8,16,64,128]{3,2,1,0:T(8,128)S(1)} %fusion.9) | copy-start | bytes 12582916
  7.4 11.4 %copy-start.8 = (f32[8]{0:T(128)S(1)}, f32[8]{0:T(128)}, u32[]{:S(2)}) copy-start(f32[8]{0:T(128)} %param.11) | copy-start | bytes 100
  10.0 14.3 %collective-permute-start.1 = (f32[64,128,64]{1,2,0:T(8,128)}, f32[64,128,64]{1,2,0:T(8,128)}, u32[]{:S(2)}, u32[]{:S(2)}) collective-permute-start(f32[64,128,64]{1,2,0:T(8,128)} %constant_dynamic-slice_fusion), channel_id=1, source_target_pairs={{0,1},{1,0},{2,3},{3,2},{4,5},{5,4},{6,7},{7,6},{8,9},{9,8},{10,11... | collective-permute-start | bytes 6291464 | tf_op jit(solution)/shard_map/ppermute | solution.py:12
  18.8 3.7 %collective-permute-start = (f32[136]{0:T(256)S(1)}, f32[136]{0:T(256)S(1)}, u32[]{:S(2)}, u32[]{:S(2)}) collective-permute-start(f32[136]{0:T(256)S(1)} %pad_maximum_fusion.2), channel_id=1, source_target_pairs={{0,1},{1,0},{2,3},{3,2},{4,5},{5,4},{6,7},{7,6},{8,9},{9,8},{10,11... | collective-permute-start | bytes 1640 | tf_op jit(solution)/shard_map/ppermute | solution.py:12
  28.9 4.9 %copy-start.7 = (bf16[128,128]{1,0:T(8,128)(2,1)S(1)}, bf16[128,128]{1,0:T(8,128)(2,1)}, u32[]{:S(2)}) copy-start(bf16[128,128]{1,0:T(8,128)(2,1)} %param.7) | copy-start | bytes 98308
  28.9 5.0 %copy-start.4 = (bf16[128,1024]{1,0:T(8,128)(2,1)S(1)}, bf16[128,1024]{1,0:T(8,128)(2,1)}, u32[]{:S(2)}) copy-start(bf16[128,1024]{1,0:T(8,128)(2,1)} %param.9) | copy-start | bytes 786436
  28.9 5.0 %copy-start.5 = (bf16[128,1024]{1,0:T(8,128)(2,1)S(1)}, bf16[128,1024]{1,0:T(8,128)(2,1)}, u32[]{:S(2)}) copy-start(bf16[128,1024]{1,0:T(8,128)(2,1)} %param.10) | copy-start | bytes 786436
  28.9 53.2 %all-to-all-start = ((bf16[8,8,129,64]{2,3,1,0:T(8,128)(2,1)}), bf16[8,8,129,64]{2,3,1,0:T(8,128)(2,1)}, u32[]{:S(2)}, u32[]{:S(2)}) async-start(bf16[8,8,129,64]{2,3,1,0:T(8,128)(2,1)} %pad_maximum_fusion), calls=%async_computation | async-start | bytes 4194304 | tf_op jit(solution)/shard_map/all_to_all | solution.py:101
  145.3 2.0 copy-start.3
  148.9 20.4 %all-to-all-start.1 = ((f32[32,1,2560]{2,1,0:T(1,128)}), f32[32,1,2560]{2,1,0:T(1,128)S(1)}, u32[]{:S(2)}, u32[]{:S(2)}) async-start(f32[32,1,2560]{2,1,0:T(1,128)} %reshape.395), calls=%async_computation.1 | async-start | bytes 655360 | tf_op jit(solution)/shard_map/all_to_all | solution.py:136
  175.1 14.6 %all-to-all-start.2 = ((f32[32,1,2048]{2,1,0:T(1,128)}), f32[32,1,2048]{2,1,0:T(1,128)S(1)}, u32[]{:S(2)}, u32[]{:S(2)}) async-start(f32[32,1,2048]{2,1,0:T(1,128)} %reshape.397), calls=%async_computation.2 | async-start | bytes 524288 | tf_op jit(solution)/shard_map/all_to_all | solution.py:143
  193.4 31.7 %copy-start.1 = (f32[8,16,64,128]{3,2,1,0:T(8,128)S(1)}, f32[8,16,64,128]{3,2,1,0:T(8,128)}, u32[]{:S(2)}) copy-start(f32[8,16,64,128]{3,2,1,0:T(8,128)} %copy-done) | copy-start | bytes 12582916
  225.2 9.1 %copy-start.6 = (f32[128,128]{1,0:T(8,128)S(1)}, f32[128,128]{1,0:T(8,128)}, u32[]{:S(2)}) copy-start(f32[128,128]{1,0:T(8,128)} %get-tuple-element.15) | copy-start | bytes 196612
  228.4 8.5 %collective-permute-start.2 = (bf16[64,128,64]{1,2,0:T(8,128)(2,1)}, bf16[64,128,64]{1,2,0:T(8,128)(2,1)}, u32[]{:S(2)}, u32[]{:S(2)}) collective-permute-start(bf16[64,128,64]{1,2,0:T(8,128)(2,1)} %get-tuple-element.12), channel_id=1, source_target_pairs={{0,1},{1,0},{2,3},{3,2},{4,5},{5,4},{6,7},{7,6},{8,9},{9,8},{10,11... | collective-permute-start | bytes 3145736 | tf_op jit(solution)/shard_map/ppermute | solution.py:12
  238.8 2.2 copy-start.2

commit v5 on v4

--- a/solution.py
+++ b/solution.py
@@ -108,8 +108,8 @@
     weight = (scores * damping * step.T[:, None, :]).astype(bf16)
     inside = jnp.einsum("hts,shp->thp", weight, x, preferred_element_type=f32)
 
-    inside, rows = lax.optimization_barrier((inside, rows))
     chip_totals = join3(rows[:, :, state, 0:3])
+    inside, chip_totals = lax.optimization_barrier((inside, chip_totals))
     skip = join3(
         rows[:, :, state, 3 : 3 + 3 * per_chip // quarter].reshape(n_z, quarter, -1, 3)
     ).reshape(heads)

time: 248 us -> 191 us (0.77)
  local copies, waits for them, and re-layouts: 81.9 us -> 27 us
    optimization_barrier x2 -> x0, local copies, waits for them, and re-layouts: 58.7 us -> none  [local(): inside, rows = lax.optimization_barrier((inside, rows))]
    unnamed x26 -> x30, local copies, waits for them, and re-layouts: 12.7 us -> 13.2 us
  transfers between devices with their start and end apart: 6 -> 6, of which waited for: 5 -> 4; matrix products, arithmetic and copies ran while one was open for 5% -> 7% of each run, Pallas kernels for 0% -> 0%
where the time goes in v5:
time: 191 us; the launch traced here: 190 us
  waiting for transfers between devices  62.7 us (33%)
  starting transfers between devices  35.5 us (19%)
  blocking collectives  31.5 us (16%)
  local copies, waits for them, and re-layouts  27 us (14%)
  other arithmetic  21.8 us (11%)
  matrix products  11.2 us (6%)
    all_to_all x1, waiting for transfers between devices, local(): rows = lax.all_to_all(message, 'z', 0, 0, tiled=True)  40.2 us
    all_to_all x1, blocking collectives, local(): back = lax.all_to_all(chip_in.astype(bf16), 'z', 0, 0, tiled=True)  31.5 us
    ppermute x3, starting transfers between devices, swap(): return lax.ppermute(value, 'core', [(0, 1), (1, 0)])  16.6 us
    unnamed x30, local copies, waits for them, and re-layouts  13.2 us
    all_to_all x1, waiting for transfers between devices, local(): gathered = lax.all_to_all(packed, 'seq', 0, 0, tiled=True)  10.5 us
    all_to_all x1, waiting for transfers between devices, local(): acc_s = lax.all_to_all(entering, 'seq', 0, 0, tiled=True)  10.4 us
    all_to_all x1, starting transfers between devices, local(): gathered = lax.all_to_all(packed, 'seq', 0, 0, tiled=True)  9.85 us
    dot_general x1, matrix products, local(): inside = jnp.einsum('hts,shp->thp', weight, x, preferred_element_type=f32)  4.97 us
  transfers between devices with their start and end apart: 6, of which 4 were waited for; matrix products, arithmetic and copies ran while one was open for 7% of the time, Pallas kernels for 0%

profile of v5, /device:TPU:1, one launch (start us, length us, event | category | flops | bytes accessed | tf_op | source)
XLA Modules:
  0.0 190.1 jit_solution(16305084377965277507)
XLA Ops:
  3.4 3.2 %copy.99 = bf16[128,8192]{0,1:T(8,128)(2,1)S(1)} copy(bf16[128,8192]{1,0:T(8,128)(2,1)} %param.6) | data formatting | bytes 4194304 | tf_op args[0]
  7.4 1.6 constant_dynamic-slice_fusion
  10.0 8.8 %collective-permute-start.1 = (f32[64,128,64]{1,2,0:T(8,128)}, f32[64,128,64]{1,2,0:T(8,128)}, u32[]{:S(2)}, u32[]{:S(2)}) collective-permute-start(f32[64,128,64]{1,2,0:T(8,128)} %constant_dynamic-slice_fusion), channel_id=1, source_target_pairs={{0,1},{1,0},{2,3},{3,2},{4,5},{5,4},{6,7},{7,6},{8,9},{9,8},{10,11... | collective-permute-start | bytes 6291464 | tf_op jit(solution)/shard_map/ppermute | solution.py:12
  18.8 1.9 %collective-permute-start = (f32[136]{0:T(256)S(1)}, f32[136]{0:T(256)S(1)}, u32[]{:S(2)}, u32[]{:S(2)}) collective-permute-start(f32[136]{0:T(256)S(1)} %pad_maximum_fusion.2), channel_id=1, source_target_pairs={{0,1},{1,0},{2,3},{3,2},{4,5},{5,4},{6,7},{7,6},{8,9},{9,8},{10,11... | collective-permute-start | bytes 1640 | tf_op jit(solution)/shard_map/ppermute | solution.py:12
  20.9 1.6 collective-permute-done
  24.2 2.6 %add_convert_fusion = bf16[64,128,64]{1,2,0:T(8,128)(2,1)S(1)} fusion(f32[64,128,64]{1,2,0:T(8,128)} %collective-permute-done.1, f32[128,128,64]{1,2,0:T(8,128)} %bitcast.110, s32[]{:T(128)S(6)} %select_n.101, f32[64]{0:T(128)S(1)} %get-tuple-element.24, pred[]{:T(512)S(6)} %eq.2), kind=kLoop, calls=%fused_computation.22 | loop fusion | flops 2621440 | bytes 5243141 | tf_op jit(solution)/shard_map/convert_element_type | solution.py:87
  26.9 2.0 %pad_maximum_fusion = bf16[8,8,129,64]{2,3,1,0:T(8,128)(2,1)} fusion(bf16[8,8,1,64]{2,3,1,0:T(8,128)(2,1)S(1)} %copy.112, bf16[8,8,128,64]{2,3,1,0:T(8,128)(2,1)S(1)} %bitcast.114), kind=kLoop, calls=%fused_computation.20 | loop fusion | flops 2113536 | bytes 2113536 | tf_op jit(solution)/shard_map/concatenate | solution.py:100
  28.9 4.8 %all-to-all-start = ((bf16[8,8,129,64]{2,3,1,0:T(8,128)(2,1)}), bf16[8,8,129,64]{2,3,1,0:T(8,128)(2,1)}, u32[]{:S(2)}, u32[]{:S(2)}) async-start(bf16[8,8,129,64]{2,3,1,0:T(8,128)(2,1)} %pad_maximum_fusion), calls=%async_computation | async-start | bytes 4194304 | tf_op jit(solution)/shard_map/all_to_all | solution.py:101
  34.2 2.7 %fusion.1 = bf16[128,128,128]{2,1,0:T(8,128)(2,1)S(1)} fusion(f32[128,128]{1,0:T(8,128)S(1)} %copy.98, f32[128,128]{1,0:T(8,128)S(1)} %copy.96, f32[8,128,128]{2,1,0:T(8,128)S(1)} %fusion.22, pred[128,128]{1,0:T(8,128)(4,1)S(1)} %iota_compare_fusion), kind=kLoop, calls=%fused_computation.2 | loop fusion | flops 12582912 | bytes 4866048 | tf_op jit(solution)/shard_map/convert_element_type | solution.py:108
  36.9 5.0 %convolution_bitcast_fusion.1 = f32[128,128,64]{0,2,1:T(8,128)} fusion(bf16[128,128,128]{2,1,0:T(8,128)(2,1)S(1)} %fusion.1, bf16[128,128,64]{0,2,1:T(8,128)(2,1)S(1)} %bitcast.107), kind=kOutput, calls=%fused_computation.13 | convolution fusion | flops 268435456 | bytes 10485760 | tf_op jit(solution)/shard_map/hts,shp->thp/dot_general | solution.py:109
  41.9 40.2 %all-to-all-done = bf16[8,8,129,64]{2,3,1,0:T(8,128)(2,1)} async-done(((bf16[8,8,129,64]{2,3,1,0:T(8,128)(2,1)}), bf16[8,8,129,64]{2,3,1,0:T(8,128)(2,1)}, u32[]{:S(2)}, u32[]{:S(2)}) %all-to-all-start) | async-done | bytes 1056800 | tf_op jit(solution)/shard_map/all_to_all | solution.py:101
  85.2 2.1 %convolution_bitcast_fusion = f32[9,8,128,64]{2,0,3,1:T(8,128)S(1)} fusion(bf16[8,8,128,64]{2,3,1,0:T(8,128)(2,1)S(1)} %slice.87, f32[8,9,8,1]{1,0,2,3:T(8,128)S(1)} %fusion.18), kind=kOutput, calls=%fused_computation.12 | convolution fusion | flops 56623104 | bytes 3410176 | tf_op jit(solution)/shard_map/hab,bhnp->ahnp/dot_general | solution.py:116
  87.3 2.0 %copy-done.3 = f32[9,8,128,64]{2,0,3,1:T(8,128)} copy-done((f32[9,8,128,64]{2,0,3,1:T(8,128)}, f32[9,8,128,64]{2,0,3,1:T(8,128)S(1)}, u32[]{:S(2)}) %copy-start.3) | copy-done | bytes 2359320
  90.9 9.9 %all-to-all-start.1 = ((f32[32,1,2560]{2,1,0:T(1,128)}), f32[32,1,2560]{2,1,0:T(1,128)S(1)}, u32[]{:S(2)}, u32[]{:S(2)}) async-start(f32[32,1,2560]{2,1,0:T(1,128)} %reshape.395), calls=%async_computation.1 | async-start | bytes 655360 | tf_op jit(solution)/shard_map/all_to_all | solution.py:136
  100.8 10.5 %all-to-all-done.1 = f32[32,1,2560]{2,1,0:T(1,128)S(1)} async-done(((f32[32,1,2560]{2,1,0:T(1,128)}), f32[32,1,2560]{2,1,0:T(1,128)S(1)}, u32[]{:S(2)}, u32[]{:S(2)}) %all-to-all-start.1) | async-done | bytes 327712 | tf_op jit(solution)/shard_map/all_to_all | solution.py:136
  117.1 4.2 %all-to-all-start.2 = ((f32[32,1,2048]{2,1,0:T(1,128)}), f32[32,1,2048]{2,1,0:T(1,128)S(1)}, u32[]{:S(2)}, u32[]{:S(2)}) async-start(f32[32,1,2048]{2,1,0:T(1,128)} %reshape.397), calls=%async_computation.2 | async-start | bytes 524288 | tf_op jit(solution)/shard_map/all_to_all | solution.py:143
  121.4 10.4 %all-to-all-done.2 = f32[32,1,2048]{2,1,0:T(1,128)S(1)} async-done(((f32[32,1,2048]{2,1,0:T(1,128)}), f32[32,1,2048]{2,1,0:T(1,128)S(1)}, u32[]{:S(2)}, u32[]{:S(2)}) %all-to-all-start.2) | async-done | bytes 262176 | tf_op jit(solution)/shard_map/all_to_all | solution.py:143
  133.5 1.9 %fusion.11 = bf16[8,8,128,64]{2,0,3,1:T(8,128)(2,1)S(1)} fusion(f32[9,8,128,64]{2,0,3,1:T(8,128)} %copy-done.3, f32[8,128,64]{1,2,0:T(8,128)S(1)} %copy.124, f32[8,8]{0,1:T(8,128)S(1)} %slice_exponential_fusion), kind=kLoop, calls=%fused_computation.19 | loop fusion | flops 1572864 | bytes 3408128 | tf_op jit(solution)/shard_map/convert_element_type | solution.py:147
  135.7 31.5 %all_to_all.20 = bf16[8,8,128,64]{2,3,1,0:T(8,128)(2,1)S(1)} all-to-all(bf16[8,8,128,64]{2,3,1,0:T(8,128)(2,1)S(1)} %copy.125), channel_id=1, replica_groups=mesh['seq'=32,'z'=8,'core'=2] {'z'}, dimensions={0} | all-to-all | bytes 2097152 | tf_op jit(solution)/shard_map/all_to_all | solution.py:147
  167.2 3.2 %fusion.7 = (bf16[64,128,64]{1,2,0:T(8,128)(2,1)S(1)}, bf16[64,128,64]{1,2,0:T(8,128)(2,1)}) fusion(bf16[8,8,128,64]{2,3,1,0:T(8,128)(2,1)S(1)} %all_to_all.20, f32[64]{0:T(128)S(1)} %get-tuple-element.22, pred[]{:T(512)S(6)} %eq.2, f32[64,128,64]{1,2,0:T(8,128)} %collective-permute-done.1, f32[128,128,64]{1,2,0:T(8,128)S(1)} %bitcast.111, s32[]{:T(128)S(6)} %select_n.101), kind=kLoop, calls=%fused_computation.15 | loop fusion | flops 4194304 | bytes 7340293 | tf_op jit(solution)/shard_map/convert_element_type | solution.py:151
  170.4 5.9 %collective-permute-start.2 = (bf16[64,128,64]{1,2,0:T(8,128)(2,1)}, bf16[64,128,64]{1,2,0:T(8,128)(2,1)}, u32[]{:S(2)}, u32[]{:S(2)}) collective-permute-start(bf16[64,128,64]{1,2,0:T(8,128)(2,1)} %get-tuple-element.12), channel_id=1, source_target_pairs={{0,1},{1,0},{2,3},{3,2},{4,5},{5,4},{6,7},{7,6},{8,9},{9,8},{10,11... | collective-permute-start | bytes 3145736 | tf_op jit(solution)/shard_map/ppermute | solution.py:12
  179.7 1.9 maximum_select_fusion
  183.8 2.2 %fusion.4 = bf16[128,128,64]{0,2,1:T(8,128)(2,1)} fusion(f32[128,128,64]{0,2,1:T(8,128)S(1)} %copy-done.2, f32[8,16,64,128]{3,2,1,0:T(8,128)S(1)} %fusion.27, bf16[128,128,64]{0,2,1:T(8,128)(2,1)S(1)} %bitcast.108, f32[128]{0:T(128)S(1)} %add.68, f32[128,128]{0,1:T(8,128)S(1)} %copy-done.6), kind=kLoop, calls=%fused_computation.6 | loop fusion | flops 6291456 | bytes 12648960 | tf_op jit(solution)/shard_map/convert_element_type | solution.py:165
  186.0 4.1 %copy.129 = bf16[128,8192]{1,0:T(8,128)(2,1)} copy(bf16[128,8192]{0,1:T(8,128)(2,1)} %bitcast.112) | data formatting | bytes 4194304 | tf_op jit(solution)/shard_map/reshape | solution.py:165
  (94 shorter events, 25.6 us)
Async XLA Ops:
  7.4 2.6 %copy-start = (f32[8,16,64,128]{3,2,1,0:T(8,128)}, f32[8,16,64,128]{3,2,1,0:T(8,128)S(1)}, u32[]{:S(2)}) copy-start(f32[8,16,64,128]{3,2,1,0:T(8,128)S(1)} %fusion.9) | copy-start | bytes 12582916
  7.4 11.4 %copy-start.9 = (f32[8]{0:T(128)S(1)}, f32[8]{0:T(128)}, u32[]{:S(2)}) copy-start(f32[8]{0:T(128)} %param.11) | copy-start | bytes 100
  10.0 14.3 %collective-permute-start.1 = (f32[64,128,64]{1,2,0:T(8,128)}, f32[64,128,64]{1,2,0:T(8,128)}, u32[]{:S(2)}, u32[]{:S(2)}) collective-permute-start(f32[64,128,64]{1,2,0:T(8,128)} %constant_dynamic-slice_fusion), channel_id=1, source_target_pairs={{0,1},{1,0},{2,3},{3,2},{4,5},{5,4},{6,7},{7,6},{8,9},{9,8},{10,11... | collective-permute-start | bytes 6291464 | tf_op jit(solution)/shard_map/ppermute | solution.py:12
  18.8 3.7 %collective-permute-start = (f32[136]{0:T(256)S(1)}, f32[136]{0:T(256)S(1)}, u32[]{:S(2)}, u32[]{:S(2)}) collective-permute-start(f32[136]{0:T(256)S(1)} %pad_maximum_fusion.2), channel_id=1, source_target_pairs={{0,1},{1,0},{2,3},{3,2},{4,5},{5,4},{6,7},{7,6},{8,9},{9,8},{10,11... | collective-permute-start | bytes 1640 | tf_op jit(solution)/shard_map/ppermute | solution.py:12
  28.9 4.9 %copy-start.8 = (bf16[128,128]{1,0:T(8,128)(2,1)S(1)}, bf16[128,128]{1,0:T(8,128)(2,1)}, u32[]{:S(2)}) copy-start(bf16[128,128]{1,0:T(8,128)(2,1)} %param.7) | copy-start | bytes 98308
  28.9 5.0 %copy-start.4 = (bf16[128,1024]{1,0:T(8,128)(2,1)S(1)}, bf16[128,1024]{1,0:T(8,128)(2,1)}, u32[]{:S(2)}) copy-start(bf16[128,1024]{1,0:T(8,128)(2,1)} %param.9) | copy-start | bytes 786436
  28.9 5.0 %copy-start.5 = (bf16[128,1024]{1,0:T(8,128)(2,1)S(1)}, bf16[128,1024]{1,0:T(8,128)(2,1)}, u32[]{:S(2)}) copy-start(bf16[128,1024]{1,0:T(8,128)(2,1)} %param.10) | copy-start | bytes 786436
  28.9 53.2 %all-to-all-start = ((bf16[8,8,129,64]{2,3,1,0:T(8,128)(2,1)}), bf16[8,8,129,64]{2,3,1,0:T(8,128)(2,1)}, u32[]{:S(2)}, u32[]{:S(2)}) async-start(bf16[8,8,129,64]{2,3,1,0:T(8,128)(2,1)} %pad_maximum_fusion), calls=%async_computation | async-start | bytes 4194304 | tf_op jit(solution)/shard_map/all_to_all | solution.py:101
  87.3 2.0 %copy-start.3 = (f32[9,8,128,64]{2,0,3,1:T(8,128)}, f32[9,8,128,64]{2,0,3,1:T(8,128)S(1)}, u32[]{:S(2)}) copy-start(f32[9,8,128,64]{2,0,3,1:T(8,128)S(1)} %convolution_bitcast_fusion) | copy-start | bytes 7077892
  90.9 20.4 %all-to-all-start.1 = ((f32[32,1,2560]{2,1,0:T(1,128)}), f32[32,1,2560]{2,1,0:T(1,128)S(1)}, u32[]{:S(2)}, u32[]{:S(2)}) async-start(f32[32,1,2560]{2,1,0:T(1,128)} %reshape.395), calls=%async_computation.1 | async-start | bytes 655360 | tf_op jit(solution)/shard_map/all_to_all | solution.py:136
  117.1 14.6 %all-to-all-start.2 = ((f32[32,1,2048]{2,1,0:T(1,128)}), f32[32,1,2048]{2,1,0:T(1,128)S(1)}, u32[]{:S(2)}, u32[]{:S(2)}) async-start(f32[32,1,2048]{2,1,0:T(1,128)} %reshape.397), calls=%async_computation.2 | async-start | bytes 524288 | tf_op jit(solution)/shard_map/all_to_all | solution.py:143
  135.5 31.7 %copy-start.1 = (f32[8,16,64,128]{3,2,1,0:T(8,128)S(1)}, f32[8,16,64,128]{3,2,1,0:T(8,128)}, u32[]{:S(2)}) copy-start(f32[8,16,64,128]{3,2,1,0:T(8,128)} %copy-done) | copy-start | bytes 12582916
  167.2 9.1 %copy-start.7 = (f32[128,128]{1,0:T(8,128)S(1)}, f32[128,128]{1,0:T(8,128)}, u32[]{:S(2)}) copy-start(f32[128,128]{1,0:T(8,128)} %get-tuple-element.15) | copy-start | bytes 196612
  170.4 9.3 %collective-permute-start.2 = (bf16[64,128,64]{1,2,0:T(8,128)(2,1)}, bf16[64,128,64]{1,2,0:T(8,128)(2,1)}, u32[]{:S(2)}, u32[]{:S(2)}) collective-permute-start(bf16[64,128,64]{1,2,0:T(8,128)(2,1)} %get-tuple-element.12), channel_id=1, source_target_pairs={{0,1},{1,0},{2,3},{3,2},{4,5},{5,4},{6,7},{7,6},{8,9},{9,8},{10,11... | collective-permute-start | bytes 3145736 | tf_op jit(solution)/shard_map/ppermute | solution.py:12
  181.6 2.2 %copy-start.2 = (f32[128,128,64]{0,2,1:T(8,128)S(1)}, f32[128,128,64]{0,2,1:T(8,128)}, u32[]{:S(2)}) copy-start(f32[128,128,64]{0,2,1:T(8,128)} %convolution_bitcast_fusion.1) | copy-start | bytes 12582916
  181.6 2.2 %copy-start.6 = (f32[128,128]{0,1:T(8,128)S(1)}, f32[128,128]{0,1:T(8,128)}, u32[]{:S(2)}) copy-start(f32[128,128]{0,1:T(8,128)} %copy.114) | copy-start | bytes 196612

commit v6 on v5

--- a/solution.py
+++ b/solution.py
@@ -72,19 +72,29 @@
     factor = jnp.exp(total[None, :] - within) * step
     scaled = (x * factor[..., None]).astype(bf16)
     update = jnp.einsum(
-        "sgn,sghp->ghnp", b, scaled.reshape(tokens, G, per_group, width),
+        "sgn,sgk->gnk", b, scaled.reshape(tokens, G, per_group * width),
         preferred_element_type=f32,
-    ).reshape(heads, state, width)
+    )
 
-    own = lax.dynamic_slice_in_dim(update, c_idx * half, half, 0)
-    got = swap(lax.dynamic_slice_in_dim(update, (1 - c_idx) * half, half, 0))
+    groups = G // n_core
+    own = lax.dynamic_slice_in_dim(update, c_idx * groups, groups, 0)
+    got = swap(lax.dynamic_slice_in_dim(update, (1 - c_idx) * groups, groups, 0))
     first = jnp.where(c_idx == 0, own, got)
     second = jnp.where(c_idx == 0, got, own)
     t_first = lax.dynamic_slice_in_dim(t_first, c_idx * half, half)
     t_second = lax.dynamic_slice_in_dim(t_second, c_idx * half, half)
-    pair = jnp.exp(t_second)[:, None, None] * first + second
+    def spread(v):
+        return jnp.repeat(v.reshape(groups, 1, per_group), width, axis=2)
 
-    pair = pair.astype(bf16).reshape(n_z, quarter, state, width)
+    pair = spread(jnp.exp(t_second)) * first + second
+
+    split = per_group // quarter
+    pair = (
+        pair.astype(bf16)
+        .reshape(groups, state, split, quarter, width)
+        .transpose(0, 2, 3, 1, 4)
+        .reshape(n_z, quarter, state, width)
+    )
     per_chip = chip_skip.shape[0]
     extra = jnp.concatenate(
         [
@@ -145,9 +155,14 @@
 
     chip_in = starts + jnp.exp(lead)[:, :, None, None] * acc_s[None]
     back = lax.all_to_all(chip_in.astype(bf16), "z", 0, 0, tiled=True)
-    entry = back.astype(f32).reshape(half, state, width)
+    entry = (
+        back.astype(f32)
+        .reshape(groups, split, quarter, state, width)
+        .transpose(0, 3, 1, 2, 4)
+        .reshape(groups, state, per_group * width)
+    )
 
-    into_second = jnp.exp(t_first)[:, None, None] * entry + first
+    into_second = spread(jnp.exp(t_first)) * entry + first
     keep = jnp.where(c_idx == 0, entry, into_second).astype(bf16)
     send = jnp.where(c_idx == 0, into_second, entry).astype(bf16)
     other = swap(send)
@@ -158,8 +173,7 @@
     )
 
     outside = jnp.einsum(
-        "tgn,ghnp->tghp", c, carried_in.reshape(G, per_group, state, width),
-        preferred_element_type=f32,
+        "tgn,gnk->tgk", c, carried_in, preferred_element_type=f32
     ).reshape(tokens, heads, width)
     mixed = inside + jnp.exp(within)[..., None] * outside + skip[None, :, None] * x.astype(f32)
     return mixed.astype(bf16).reshape(tokens, heads * width)

time: 191 us -> 197 us (1.031)
  blocking collectives: 31.5 us -> 0 us
  waiting for transfers between devices: 62.7 us -> 85.9 us
  starting transfers between devices: 35.5 us -> 41.9 us
  local copies, waits for them, and re-layouts: 27 us -> 33 us
  matrix products: 11.2 us -> 13.6 us
    all_to_all x1 -> x0, blocking collectives: 31.5 us -> none  [local(): back = lax.all_to_all(chip_in.astype(bf16), 'z', 0, 0, tiled=True)]
    all_to_all x0 -> x1, waiting for transfers between devices: none -> 25.6 us  [local(): back = lax.all_to_all(chip_in.astype(bf16), 'z', 0, 0, tiled=True)]
    all_to_all x0 -> x1, starting transfers between devices: none -> 7.29 us  [local(): back = lax.all_to_all(chip_in.astype(bf16), 'z', 0, 0, tiled=True)]
    convert_element_type x0 -> x1, local copies, waits for them, and re-layouts: none -> 4.32 us  [local(): scaled = (x * factor[..., None]).astype(bf16)]
    all_to_all x1, waiting for transfers between devices: 40.2 us -> 36.9 us  [local(): rows = lax.all_to_all(message, 'z', 0, 0, tiled=True)]
    dot_general x2, matrix products: 1.41 us -> 3.78 us  [the longest x1 3.09 us: local(): jnp.einsum('tgn,gnk->tgk', c, carried_in, preferred_element_type=f32)]
    unnamed x30 -> x28, local copies, waits for them, and re-layouts: 13.2 us -> 13.1 us
  transfers between devices with their start and end apart: 6 -> 7, of which waited for: 4 -> 6; matrix products, arithmetic and copies ran while one was open for 7% -> 8% of each run, Pallas kernels for 0% -> 0%
where the time goes in v6:
time: 197 us; the launch traced here: 196 us
  waiting for transfers between devices  85.9 us (44%)
  starting transfers between devices  41.9 us (21%)
  local copies, waits for them, and re-layouts  33 us (17%)
  other arithmetic  20.9 us (11%)
  matrix products  13.6 us (7%)
    all_to_all x1, waiting for transfers between devices, local(): rows = lax.all_to_all(message, 'z', 0, 0, tiled=True)  36.9 us
    all_to_all x1, waiting for transfers between devices, local(): back = lax.all_to_all(chip_in.astype(bf16), 'z', 0, 0, tiled=True)  25.6 us
    ppermute x3, starting transfers between devices, swap(): return lax.ppermute(value, 'core', [(0, 1), (1, 0)])  15.9 us
    unnamed x28, local copies, waits for them, and re-layouts  13.1 us
    all_to_all x1, waiting for transfers between devices, local(): gathered = lax.all_to_all(packed, 'seq', 0, 0, tiled=True)  10.5 us
    all_to_all x1, waiting for transfers between devices, local(): acc_s = lax.all_to_all(entering, 'seq', 0, 0, tiled=True)  10.4 us
    all_to_all x1, starting transfers between devices, local(): gathered = lax.all_to_all(packed, 'seq', 0, 0, tiled=True)  9.85 us
    all_to_all x1, starting transfers between devices, local(): back = lax.all_to_all(chip_in.astype(bf16), 'z', 0, 0, tiled=True)  7.29 us
  transfers between devices with their start and end apart: 7, of which 6 were waited for; matrix products, arithmetic and copies ran while one was open for 8% of the time, Pallas kernels for 0%

profile of v6, /device:TPU:1, one launch (start us, length us, event | category | flops | bytes accessed | tf_op | source)
XLA Modules:
  0.0 195.7 jit_solution(15205494305785920827)
XLA Ops:
  2.5 4.3 %copy.135 = f32[128,8192]{0,1:T(8,128)} copy(bf16[128,8192]{1,0:T(8,128)(2,1)} %param.6) | data formatting | bytes 6291456 | tf_op jit(solution)/shard_map/convert_element_type | solution.py:73
  12.7 8.8 %collective-permute-start.1 = (f32[4,128,1024]{1,2,0:T(8,128)}, f32[4,128,1024]{1,2,0:T(8,128)S(1)}, u32[]{:S(2)}, u32[]{:S(2)}) collective-permute-start(f32[4,128,1024]{1,2,0:T(8,128)} %dynamic-slice_bitcast_fusion), channel_id=1, source_target_pairs={{0,1},{1,0},{2,3},{3,2},{4,5},{5,4},{6,7},{7,6},{8,9},{9,8},{10,11... | collective-permute-start | bytes 6291464 | tf_op jit(solution)/shard_map/ppermute | solution.py:12
  21.5 1.9 collective-permute-start
  27.3 2.7 %fusion.14 = bf16[4,128,1024]{1,2,0:T(8,128)(2,1)S(1)} fusion(f32[4,128,1024]{1,2,0:T(8,128)S(1)} %collective-permute-done.1, f32[8,1024,128]{2,1,0:T(8,128)} %copy-done.1, s32[]{:T(128)S(6)} %select_n.101, f32[4,1024]{1,0:T(4,128)S(1)} %broadcast_in_dim.103, pred[]{:T(512)S(6)} %eq.2), kind=kLoop, calls=%fused_computation.27 | loop fusion | flops 2621440 | bytes 5259269 | tf_op jit(solution)/shard_map/convert_element_type | solution.py:93
  30.0 1.9 pad_maximum_fusion
  31.9 4.7 %all-to-all-start = ((bf16[8,8,129,64]{2,3,1,0:T(8,128)(2,1)}), bf16[8,8,129,64]{2,3,1,0:T(8,128)(2,1)}, u32[]{:S(2)}, u32[]{:S(2)}) async-start(bf16[8,8,129,64]{2,3,1,0:T(8,128)(2,1)} %pad_maximum_fusion), calls=%async_computation | async-start | bytes 4194304 | tf_op jit(solution)/shard_map/all_to_all | solution.py:111
  36.6 3.3 %copy.101 = bf16[128,8192]{0,1:T(8,128)(2,1)S(1)} copy(bf16[128,8192]{1,0:T(8,128)(2,1)} %param.6) | data formatting | bytes 4194304 | tf_op args[0]
  40.4 2.7 %fusion.1 = bf16[128,128,128]{2,1,0:T(8,128)(2,1)S(1)} fusion(f32[128,128]{1,0:T(8,128)S(1)} %copy.100, f32[128,128]{1,0:T(8,128)S(1)} %copy.98, f32[8,128,128]{2,1,0:T(8,128)S(1)} %fusion.27, pred[128,128]{1,0:T(8,128)(4,1)S(1)} %iota_compare_fusion), kind=kLoop, calls=%fused_computation.2 | loop fusion | flops 12582912 | bytes 4866048 | tf_op jit(solution)/shard_map/convert_element_type | solution.py:118
  43.2 5.0 %convolution_bitcast_fusion.1 = f32[128,128,64]{0,2,1:T(8,128)} fusion(bf16[128,128,128]{2,1,0:T(8,128)(2,1)S(1)} %fusion.1, bf16[128,128,64]{0,2,1:T(8,128)(2,1)S(1)} %bitcast.133), kind=kOutput, calls=%fused_computation.7 | convolution fusion | flops 268435456 | bytes 10485760 | tf_op jit(solution)/shard_map/hts,shp->thp/dot_general | solution.py:119
  48.1 36.9 %all-to-all-done = bf16[8,8,129,64]{2,3,1,0:T(8,128)(2,1)} async-done(((bf16[8,8,129,64]{2,3,1,0:T(8,128)(2,1)}), bf16[8,8,129,64]{2,3,1,0:T(8,128)(2,1)}, u32[]{:S(2)}, u32[]{:S(2)}) %all-to-all-start) | async-done | bytes 1056800 | tf_op jit(solution)/shard_map/all_to_all | solution.py:111
  88.2 2.1 %convolution_bitcast_fusion = f32[9,8,128,64]{2,0,3,1:T(8,128)S(1)} fusion(bf16[8,8,128,64]{2,3,1,0:T(8,128)(2,1)S(1)} %slice.87, f32[8,9,8,1]{1,0,2,3:T(8,128)S(1)} %fusion.21), kind=kOutput, calls=%fused_computation.6 | convolution fusion | flops 56623104 | bytes 3410176 | tf_op jit(solution)/shard_map/hab,bhnp->ahnp/dot_general | solution.py:126
  90.2 2.0 %copy-done.4 = f32[9,8,128,64]{2,0,3,1:T(8,128)} copy-done((f32[9,8,128,64]{2,0,3,1:T(8,128)}, f32[9,8,128,64]{2,0,3,1:T(8,128)S(1)}, u32[]{:S(2)}) %copy-start.4) | copy-done | bytes 2359320
  93.9 9.9 %all-to-all-start.1 = ((f32[32,1,2560]{2,1,0:T(1,128)}), f32[32,1,2560]{2,1,0:T(1,128)S(1)}, u32[]{:S(2)}, u32[]{:S(2)}) async-start(f32[32,1,2560]{2,1,0:T(1,128)} %reshape.413), calls=%async_computation.1 | async-start | bytes 655360 | tf_op jit(solution)/shard_map/all_to_all | solution.py:146
  103.7 10.5 %all-to-all-done.1 = f32[32,1,2560]{2,1,0:T(1,128)S(1)} async-done(((f32[32,1,2560]{2,1,0:T(1,128)}), f32[32,1,2560]{2,1,0:T(1,128)S(1)}, u32[]{:S(2)}, u32[]{:S(2)}) %all-to-all-start.1) | async-done | bytes 327712 | tf_op jit(solution)/shard_map/all_to_all | solution.py:146
  121.7 4.2 %all-to-all-start.2 = ((f32[32,1,2048]{2,1,0:T(1,128)}), f32[32,1,2048]{2,1,0:T(1,128)S(1)}, u32[]{:S(2)}, u32[]{:S(2)}) async-start(f32[32,1,2048]{2,1,0:T(1,128)} %reshape.415), calls=%async_computation.2 | async-start | bytes 524288 | tf_op jit(solution)/shard_map/all_to_all | solution.py:153
  126.0 10.4 %all-to-all-done.2 = f32[32,1,2048]{2,1,0:T(1,128)S(1)} async-done(((f32[32,1,2048]{2,1,0:T(1,128)}), f32[32,1,2048]{2,1,0:T(1,128)S(1)}, u32[]{:S(2)}, u32[]{:S(2)}) %all-to-all-start.2) | async-done | bytes 262176 | tf_op jit(solution)/shard_map/all_to_all | solution.py:153
  138.2 1.9 fusion.3
  141.3 7.3 %all-to-all-start.3 = ((bf16[8,8,128,64]{2,3,1,0:T(8,128)(2,1)}), bf16[8,8,128,64]{2,3,1,0:T(8,128)(2,1)S(1)}, u32[]{:S(2)}, u32[]{:S(2)}) async-start(bf16[8,8,128,64]{2,3,1,0:T(8,128)(2,1)} %copy.127), calls=%async_computation.3 | async-start | bytes 2097152 | tf_op jit(solution)/shard_map/all_to_all | solution.py:157
  148.9 25.6 %all-to-all-done.3 = bf16[8,8,128,64]{2,3,1,0:T(8,128)(2,1)S(1)} async-done(((bf16[8,8,128,64]{2,3,1,0:T(8,128)(2,1)}), bf16[8,8,128,64]{2,3,1,0:T(8,128)(2,1)S(1)}, u32[]{:S(2)}, u32[]{:S(2)}) %all-to-all-start.3) | async-done | bytes 1048608 | tf_op jit(solution)/shard_map/all_to_all | solution.py:157
  174.5 3.6 %fusion.11 = (bf16[4,128,1024]{1,2,0:T(8,128)(2,1)}, bf16[4,128,1024]{1,2,0:T(8,128)(2,1)}) fusion(bf16[4,2,8,128,64]{3,4,2,1,0:T(8,128)(2,1)S(1)} %bitcast.139, f32[4,1024]{1,0:T(4,128)S(1)} %broadcast_in_dim.113, pred[]{:T(512)S(6)} %eq.2, f32[4,128,1024]{1,2,0:T(8,128)} %copy-done.5, f32[8,1024,128]{2,1,0:T(8,128)} %copy-done.1, s32[]{:T(128)S(6)} %select_n.101), kind=kLoop, calls=%fused_computation.22 | loop fusion | flops 4194304 | bytes 7356421 | tf_op jit(solution)/shard_map/convert_element_type | solution.py:166
  178.1 5.2 %collective-permute-start.2 = (bf16[4,128,1024]{1,2,0:T(8,128)(2,1)}, bf16[4,128,1024]{1,2,0:T(8,128)(2,1)}, u32[]{:S(2)}, u32[]{:S(2)}) collective-permute-start(bf16[4,128,1024]{1,2,0:T(8,128)(2,1)} %get-tuple-element.12), channel_id=1, source_target_pairs={{0,1},{1,0},{2,3},{3,2},{4,5},{5,4},{6,7},{7,6},{8,9},{9,8},{10,11... | collective-permute-start | bytes 3145736 | tf_op jit(solution)/shard_map/ppermute | solution.py:12
  185.9 3.1 %fusion.4 = f32[8,1024,128]{2,1,0:T(8,128)S(1)} fusion(bf16[4,128,1024]{1,2,0:T(8,128)(2,1)} %collective-permute-done.2, bf16[4,128,1024]{1,2,0:T(8,128)(2,1)} %get-tuple-element.11, pred[]{:T(512)S(6)} %eq.2, bf16[128,1024]{1,0:T(8,128)(2,1)} %param.10), kind=kOutput, calls=%fused_computation.12 | convolution fusion | flops 271581184 | bytes 6553601 | tf_op jit(solution)/shard_map/tgn,gnk->tgk/dot_general | solution.py:175
  189.4 2.2 %add_convert_fusion = bf16[128,128,64]{0,2,1:T(8,128)(2,1)} fusion(bf16[128,128,64]{0,2,1:T(8,128)(2,1)S(1)} %bitcast.134, f32[128,128,64]{0,2,1:T(8,128)S(1)} %copy-done.2, f32[128,128,64]{0,2,1:T(8,128)S(1)} %bitcast.138, f32[128]{0:T(128)S(1)} %add.71, f32[128,128]{0,1:T(8,128)S(1)} %copy.116), kind=kLoop, calls=%fused_computation.5 | loop fusion | flops 6291456 | bytes 12648960 | tf_op jit(solution)/shard_map/convert_element_type | solution.py:179
  191.6 4.1 %copy.131 = bf16[128,8192]{1,0:T(8,128)(2,1)} copy(bf16[128,8192]{0,1:T(8,128)(2,1)} %bitcast.137) | data formatting | bytes 4194304 | tf_op jit(solution)/shard_map/reshape | solution.py:179
  (101 shorter events, 31.1 us)
Async XLA Ops:
  0.0 9.4 %copy-start = (bf16[128,1024]{1,0:T(8,128)(2,1)S(1)}, bf16[128,1024]{1,0:T(8,128)(2,1)}, u32[]{:S(2)}) copy-start(bf16[128,1024]{1,0:T(8,128)(2,1)} %param.9) | copy-start | bytes 786436
  6.8 2.2 %copy-start.3 = (f32[128,8192]{0,1:T(8,128)S(1)}, f32[128,8192]{0,1:T(8,128)}, u32[]{:S(2)}) copy-start(f32[128,8192]{0,1:T(8,128)} %copy.135) | copy-start | bytes 12582916
  10.1 2.6 %copy-start.1 = (f32[8,1024,128]{2,1,0:T(8,128)}, f32[8,1024,128]{2,1,0:T(8,128)S(1)}, u32[]{:S(2)}) copy-start(f32[8,1024,128]{2,1,0:T(8,128)S(1)} %fusion.25) | copy-start | bytes 12582916
  10.1 11.4 %copy-start.9 = (f32[8]{0:T(128)S(1)}, f32[8]{0:T(128)}, u32[]{:S(2)}) copy-start(f32[8]{0:T(128)} %param.11) | copy-start | bytes 100
  12.7 14.5 %collective-permute-start.1 = (f32[4,128,1024]{1,2,0:T(8,128)}, f32[4,128,1024]{1,2,0:T(8,128)S(1)}, u32[]{:S(2)}, u32[]{:S(2)}) collective-permute-start(f32[4,128,1024]{1,2,0:T(8,128)} %dynamic-slice_bitcast_fusion), channel_id=1, source_target_pairs={{0,1},{1,0},{2,3},{3,2},{4,5},{5,4},{6,7},{7,6},{8,9},{9,8},{10,11... | collective-permute-start | bytes 6291464 | tf_op jit(solution)/shard_map/ppermute | solution.py:12
  21.5 3.7 %collective-permute-start = (f32[136]{0:T(256)S(1)}, f32[136]{0:T(256)S(1)}, u32[]{:S(2)}, u32[]{:S(2)}) collective-permute-start(f32[136]{0:T(256)S(1)} %pad_maximum_fusion.2), channel_id=1, source_target_pairs={{0,1},{1,0},{2,3},{3,2},{4,5},{5,4},{6,7},{7,6},{8,9},{9,8},{10,11... | collective-permute-start | bytes 1640 | tf_op jit(solution)/shard_map/ppermute | solution.py:12
  27.2 2.7 %copy-start.5 = (f32[4,128,1024]{1,2,0:T(8,128)}, f32[4,128,1024]{1,2,0:T(8,128)S(1)}, u32[]{:S(2)}) copy-start(f32[4,128,1024]{1,2,0:T(8,128)S(1)} %collective-permute-done.1) | copy-start | bytes 6291460
  31.9 53.1 %all-to-all-start = ((bf16[8,8,129,64]{2,3,1,0:T(8,128)(2,1)}), bf16[8,8,129,64]{2,3,1,0:T(8,128)(2,1)}, u32[]{:S(2)}, u32[]{:S(2)}) async-start(bf16[8,8,129,64]{2,3,1,0:T(8,128)(2,1)} %pad_maximum_fusion), calls=%async_computation | async-start | bytes 4194304 | tf_op jit(solution)/shard_map/all_to_all | solution.py:111
  36.6 3.4 %copy-start.8 = (bf16[128,128]{1,0:T(8,128)(2,1)S(1)}, bf16[128,128]{1,0:T(8,128)(2,1)}, u32[]{:S(2)}) copy-start(bf16[128,128]{1,0:T(8,128)(2,1)} %param.7) | copy-start | bytes 98308
  36.6 3.5 %copy-start.7 = (bf16[128,1024]{1,0:T(8,128)(2,1)S(1)}, bf16[128,1024]{1,0:T(8,128)(2,1)}, u32[]{:S(2)}) copy-start(bf16[128,1024]{1,0:T(8,128)(2,1)} %param.10) | copy-start | bytes 786436
  90.2 2.0 %copy-start.4 = (f32[9,8,128,64]{2,0,3,1:T(8,128)}, f32[9,8,128,64]{2,0,3,1:T(8,128)S(1)}, u32[]{:S(2)}) copy-start(f32[9,8,128,64]{2,0,3,1:T(8,128)S(1)} %convolution_bitcast_fusion) | copy-start | bytes 7077892
  93.9 20.4 %all-to-all-start.1 = ((f32[32,1,2560]{2,1,0:T(1,128)}), f32[32,1,2560]{2,1,0:T(1,128)S(1)}, u32[]{:S(2)}, u32[]{:S(2)}) async-start(f32[32,1,2560]{2,1,0:T(1,128)} %reshape.413), calls=%async_computation.1 | async-start | bytes 655360 | tf_op jit(solution)/shard_map/all_to_all | solution.py:146
  121.7 14.6 %all-to-all-start.2 = ((f32[32,1,2048]{2,1,0:T(1,128)}), f32[32,1,2048]{2,1,0:T(1,128)S(1)}, u32[]{:S(2)}, u32[]{:S(2)}) async-start(f32[32,1,2048]{2,1,0:T(1,128)} %reshape.415), calls=%async_computation.2 | async-start | bytes 524288 | tf_op jit(solution)/shard_map/all_to_all | solution.py:153
  141.3 33.2 %all-to-all-start.3 = ((bf16[8,8,128,64]{2,3,1,0:T(8,128)(2,1)}), bf16[8,8,128,64]{2,3,1,0:T(8,128)(2,1)S(1)}, u32[]{:S(2)}, u32[]{:S(2)}) async-start(bf16[8,8,128,64]{2,3,1,0:T(8,128)(2,1)} %copy.127), calls=%async_computation.3 | async-start | bytes 2097152 | tf_op jit(solution)/shard_map/all_to_all | solution.py:157
  174.5 8.8 %copy-start.6 = (f32[128,128]{1,0:T(8,128)S(1)}, f32[128,128]{1,0:T(8,128)}, u32[]{:S(2)}) copy-start(f32[128,128]{1,0:T(8,128)} %get-tuple-element.15) | copy-start | bytes 196612
  178.1 7.8 %collective-permute-start.2 = (bf16[4,128,1024]{1,2,0:T(8,128)(2,1)}, bf16[4,128,1024]{1,2,0:T(8,128)(2,1)}, u32[]{:S(2)}, u32[]{:S(2)}) collective-permute-start(bf16[4,128,1024]{1,2,0:T(8,128)(2,1)} %get-tuple-element.12), channel_id=1, source_target_pairs={{0,1},{1,0},{2,3},{3,2},{4,5},{5,4},{6,7},{7,6},{8,9},{9,8},{10,11... | collective-permute-start | bytes 3145736 | tf_op jit(solution)/shard_map/ppermute | solution.py:12
  185.9 3.5 %copy-start.2 = (f32[128,128,64]{0,2,1:T(8,128)S(1)}, f32[128,128,64]{0,2,1:T(8,128)}, u32[]{:S(2)}) copy-start(f32[128,128,64]{0,2,1:T(8,128)} %convolution_bitcast_fusion.1) | copy-start | bytes 12582916

commit v7 on v5

--- a/solution.py
+++ b/solution.py
@@ -96,8 +96,10 @@
         ],
         axis=-1,
     )
-    extra = jnp.pad(extra, ((0, 0), (0, 0), (0, width - extra.shape[-1])))
-    message = jnp.concatenate([pair, extra[:, :, None, :]], axis=2)
+    extra = jnp.pad(
+        extra, ((0, 0), (0, state - quarter), (0, width - extra.shape[-1]))
+    )
+    message = jnp.concatenate([pair, extra[:, None]], axis=1)
     rows = lax.all_to_all(message, "z", 0, 0, tiled=True)
     scores = jnp.einsum("tgn,sgn->gts", c, b, preferred_element_type=f32)
     scores = jnp.repeat(scores, per_group, axis=0)
@@ -108,15 +110,17 @@
     weight = (scores * damping * step.T[:, None, :]).astype(bf16)
     inside = jnp.einsum("hts,shp->thp", weight, x, preferred_element_type=f32)
 
-    chip_totals = join3(rows[:, :, state, 0:3])
+    chip_totals = join3(rows[:, quarter, :quarter, 0:3])
     inside, chip_totals = lax.optimization_barrier((inside, chip_totals))
     skip = join3(
-        rows[:, :, state, 3 : 3 + 3 * per_chip // quarter].reshape(n_z, quarter, -1, 3)
+        rows[:, quarter, :quarter, 3 : 3 + 3 * per_chip // quarter].reshape(
+            n_z, quarter, -1, 3
+        )
     ).reshape(heads)
     scan = jnp.einsum(
         "hab,bhnp->ahnp",
         decay_matrix(chip_totals, n_z + 1),
-        rows[:, :, :state].astype(f32),
+        rows[:, :quarter].astype(f32),
         precision=lax.Precision.HIGHEST,
     )
     leads = jnp.einsum(

time: 191 us -> 187 us (0.979)
  waiting for transfers between devices: 62.7 us -> 42.6 us
  local copies, waits for them, and re-layouts: 27 us -> 37 us
  other arithmetic: 21.8 us -> 29 us
  blocking collectives: 31.5 us -> 26.8 us
  matrix products: 11.2 us -> 13.2 us
    all_to_all x1, waiting for transfers between devices: 40.2 us -> 17.6 us  [local(): rows = lax.all_to_all(message, 'z', 0, 0, tiled=True)]
    all_to_all x1, blocking collectives: 31.5 us -> 26.8 us  [local(): back = lax.all_to_all(chip_in.astype(bf16), 'z', 0, 0, tiled=True)]
    unnamed x30 -> x27, local copies, waits for them, and re-layouts: 13.2 us -> 17.4 us
    slice x3, local copies, waits for them, and re-layouts: 3.26 us -> 0.11 us  [the longest x1 0.09 us: local(): rows[:, :quarter].astype(f32)]
    all_to_all x1, waiting for transfers between devices: 10.5 us -> 12.5 us  [local(): gathered = lax.all_to_all(packed, 'seq', 0, 0, tiled=True)]
  transfers between devices with their start and end apart: 6 -> 6, of which waited for: 4 -> 5; matrix products, arithmetic and copies ran while one was open for 7% -> 9% of each run, Pallas kernels for 0% -> 0%
where the time goes in v7:
time: 187 us; the launch traced here: 185 us
  waiting for transfers between devices  42.6 us (23%)
  local copies, waits for them, and re-layouts  37 us (20%)
  starting transfers between devices  36.2 us (19%)
  other arithmetic  29 us (16%)
  blocking collectives  26.8 us (14%)
  matrix products  13.2 us (7%)
    all_to_all x1, blocking collectives, local(): back = lax.all_to_all(chip_in.astype(bf16), 'z', 0, 0, tiled=True)  26.8 us
    all_to_all x1, waiting for transfers between devices, local(): rows = lax.all_to_all(message, 'z', 0, 0, tiled=True)  17.6 us
    unnamed x27, local copies, waits for them, and re-layouts  17.4 us
    ppermute x3, starting transfers between devices, swap(): return lax.ppermute(value, 'core', [(0, 1), (1, 0)])  16.5 us
    all_to_all x1, waiting for transfers between devices, local(): gathered = lax.all_to_all(packed, 'seq', 0, 0, tiled=True)  12.5 us
    all_to_all x1, waiting for transfers between devices, local(): acc_s = lax.all_to_all(entering, 'seq', 0, 0, tiled=True)  10.4 us
    all_to_all x1, starting transfers between devices, local(): gathered = lax.all_to_all(packed, 'seq', 0, 0, tiled=True)  9.96 us
    all_to_all x1, starting transfers between devices, local(): acc_s = lax.all_to_all(entering, 'seq', 0, 0, tiled=True)  5 us
  transfers between devices with their start and end apart: 6, of which 5 were waited for; matrix products, arithmetic and copies ran while one was open for 9% of the time, Pallas kernels for 0%

profile of v7, /device:TPU:1, one launch (start us, length us, event | category | flops | bytes accessed | tf_op | source)
XLA Modules:
  0.0 185.3 jit_solution(2573759427683177915)
XLA Ops:
  3.5 3.2 %copy.155 = bf16[128,8192]{0,1:T(8,128)(2,1)S(1)} copy(bf16[128,8192]{1,0:T(8,128)(2,1)} %param.6) | data formatting | bytes 4194304 | tf_op args[0]
  10.1 8.8 %collective-permute-start.1 = (f32[64,128,64]{1,2,0:T(8,128)}, f32[64,128,64]{1,2,0:T(8,128)}, u32[]{:S(2)}, u32[]{:S(2)}) collective-permute-start(f32[64,128,64]{1,2,0:T(8,128)} %constant_dynamic-slice_fusion), channel_id=1, source_target_pairs={{0,1},{1,0},{2,3},{3,2},{4,5},{5,4},{6,7},{7,6},{8,9},{9,8},{10,11... | collective-permute-start | bytes 6291464 | tf_op jit(solution)/shard_map/ppermute | solution.py:12
  23.2 2.6 %add_convert_fusion = bf16[64,128,64]{1,2,0:T(8,128)(2,1)S(1)} fusion(f32[64,128,64]{1,2,0:T(8,128)} %collective-permute-done.1, f32[128,128,64]{1,2,0:T(8,128)} %bitcast.114, s32[]{:T(128)S(6)} %select_n.101, f32[64]{0:T(128)S(1)} %get-tuple-element.24, pred[]{:T(512)S(6)} %eq.2), kind=kLoop, calls=%fused_computation.21 | loop fusion | flops 2621440 | bytes 5243141 | tf_op jit(solution)/shard_map/convert_element_type | solution.py:87
  27.0 4.7 %all-to-all-start = ((bf16[8,9,128,64]{2,3,1,0:T(8,128)(2,1)}), bf16[8,9,128,64]{2,3,1,0:T(8,128)(2,1)S(1)}, u32[]{:S(2)}, u32[]{:S(2)}) async-start(bf16[8,9,128,64]{2,3,1,0:T(8,128)(2,1)} %pad_maximum_fusion), calls=%async_computation | async-start | bytes 2359296 | tf_op jit(solution)/shard_map/all_to_all | solution.py:103
  37.5 3.6 %fusion.1 = bf16[128,128,128]{2,1,0:T(8,128)(2,1)S(1)} fusion(f32[128,128]{1,0:T(8,128)} %copy.154, f32[128,128]{1,0:T(8,128)} %copy.152, f32[8,128,128]{2,1,0:T(8,128)S(1)} %fusion.22, pred[128,128]{1,0:T(8,128)(4,1)S(1)} %iota_compare_fusion.2), kind=kLoop, calls=%fused_computation.2 | loop fusion | flops 12582912 | bytes 4866048 | tf_op jit(solution)/shard_map/convert_element_type | solution.py:110
  41.2 5.0 %convolution_bitcast_fusion.1 = f32[128,128,64]{0,2,1:T(8,128)} fusion(bf16[128,128,128]{2,1,0:T(8,128)(2,1)S(1)} %fusion.1, bf16[128,128,64]{0,2,1:T(8,128)(2,1)S(1)} %bitcast.111), kind=kOutput, calls=%fused_computation.13 | convolution fusion | flops 268435456 | bytes 10485760 | tf_op jit(solution)/shard_map/hts,shp->thp/dot_general | solution.py:111
  46.1 17.6 %all-to-all-done = bf16[8,9,128,64]{2,3,1,0:T(8,128)(2,1)S(1)} async-done(((bf16[8,9,128,64]{2,3,1,0:T(8,128)(2,1)}), bf16[8,9,128,64]{2,3,1,0:T(8,128)(2,1)S(1)}, u32[]{:S(2)}, u32[]{:S(2)}) %all-to-all-start) | async-done | bytes 1179680 | tf_op jit(solution)/shard_map/all_to_all | solution.py:103
  64.5 2.1 %convolution_bitcast_fusion = f32[9,8,128,64]{2,0,3,1:T(8,128)S(1)} fusion(bf16[8,8,128,64]{2,3,1,0:T(8,128)(2,1)S(1)} %slice.87, f32[8,9,8,1]{1,0,2,3:T(8,128)S(1)} %fusion.18), kind=kOutput, calls=%fused_computation.12 | convolution fusion | flops 56623104 | bytes 3410176 | tf_op jit(solution)/shard_map/hab,bhnp->ahnp/dot_general | solution.py:120
  66.6 2.0 %copy-done.3 = f32[9,8,128,64]{2,0,3,1:T(8,128)} copy-done((f32[9,8,128,64]{2,0,3,1:T(8,128)}, f32[9,8,128,64]{2,0,3,1:T(8,128)S(1)}, u32[]{:S(2)}) %copy-start.3) | copy-done | bytes 2359320
  71.7 2.2 %reshape.394 = f32[32,1,2560]{2,1,0:T(1,128)} reshape(f32[32,5,8,64]{3,2,1,0:T(8,128)} %fusion.58) | data formatting | bytes 655360
  73.9 10.0 %all-to-all-start.1 = ((f32[32,1,2560]{2,1,0:T(1,128)}), f32[32,1,2560]{2,1,0:T(1,128)}, u32[]{:S(2)}, u32[]{:S(2)}) async-start(f32[32,1,2560]{2,1,0:T(1,128)} %reshape.394), calls=%async_computation.1 | async-start | bytes 655360 | tf_op jit(solution)/shard_map/all_to_all | solution.py:140
  83.9 12.5 %all-to-all-done.1 = f32[32,1,2560]{2,1,0:T(1,128)} async-done(((f32[32,1,2560]{2,1,0:T(1,128)}), f32[32,1,2560]{2,1,0:T(1,128)}, u32[]{:S(2)}, u32[]{:S(2)}) %all-to-all-start.1) | async-done | bytes 327712 | tf_op jit(solution)/shard_map/all_to_all | solution.py:140
  96.9 3.0 %reduce.2 = f32[32,2560]{1,0:T(8,128)} reduce(f32[32,1,2560]{2,1,0:T(1,128)} %all-to-all-done.1, f32[]{:T(128)} %broadcast.100), dimensions={1}, to_apply=%all_to_all.13.reduce_sub_computation | reduce | bytes 655364 | tf_op jit(solution)/shard_map/all_to_all | solution.py:140
  99.9 2.0 %reshape.395 = f32[32,5,8,64]{3,2,1,0:T(8,128)} reshape(f32[32,2560]{1,0:T(8,128)} %reduce.2) | data formatting | bytes 655360
  109.0 2.2 %reshape.396 = f32[32,1,2048]{2,1,0:T(1,128)} reshape(f32[32,8,4,64]{3,2,1,0:T(4,128)} %copy.176) | data formatting | bytes 524288
  111.2 5.0 %all-to-all-start.2 = ((f32[32,1,2048]{2,1,0:T(1,128)}), f32[32,1,2048]{2,1,0:T(1,128)}, u32[]{:S(2)}, u32[]{:S(2)}) async-start(f32[32,1,2048]{2,1,0:T(1,128)} %reshape.396), calls=%async_computation.2 | async-start | bytes 524288 | tf_op jit(solution)/shard_map/all_to_all | solution.py:147
  116.2 10.4 %all-to-all-done.2 = f32[32,1,2048]{2,1,0:T(1,128)} async-done(((f32[32,1,2048]{2,1,0:T(1,128)}), f32[32,1,2048]{2,1,0:T(1,128)}, u32[]{:S(2)}, u32[]{:S(2)}) %all-to-all-start.2) | async-done | bytes 262176 | tf_op jit(solution)/shard_map/all_to_all | solution.py:147
  126.6 2.1 %reduce.3 = f32[32,2048]{1,0:T(8,128)S(1)} reduce(f32[32,1,2048]{2,1,0:T(1,128)} %all-to-all-done.2, f32[]{:T(128)} %broadcast.100), dimensions={1}, to_apply=%all_to_all.14.reduce_sub_computation | reduce | bytes 524292 | tf_op jit(solution)/shard_map/all_to_all | solution.py:147
  135.1 26.8 %all_to_all.20 = bf16[8,8,128,64]{2,3,1,0:T(8,128)(2,1)S(1)} all-to-all(bf16[8,8,128,64]{2,3,1,0:T(8,128)(2,1)S(1)} %copy.179), channel_id=1, replica_groups=mesh['seq'=32,'z'=8,'core'=2] {'z'}, dimensions={0} | all-to-all | bytes 2097152 | tf_op jit(solution)/shard_map/all_to_all | solution.py:151
  162.0 3.6 %fusion.7 = (bf16[64,128,64]{1,2,0:T(8,128)(2,1)}, bf16[64,128,64]{1,2,0:T(8,128)(2,1)}) fusion(bf16[8,8,128,64]{2,3,1,0:T(8,128)(2,1)S(1)} %all_to_all.20, f32[64]{0:T(128)S(1)} %get-tuple-element.22, pred[]{:T(512)S(6)} %eq.2, f32[64,128,64]{1,2,0:T(8,128)} %collective-permute-done.1, f32[128,128,64]{1,2,0:T(8,128)S(1)} %bitcast.115, s32[]{:T(128)S(6)} %select_n.101), kind=kLoop, calls=%fused_computation.15 | loop fusion | flops 4194304 | bytes 7340293 | tf_op jit(solution)/shard_map/convert_element_type | solution.py:155
  165.6 5.8 %collective-permute-start.2 = (bf16[64,128,64]{1,2,0:T(8,128)(2,1)}, bf16[64,128,64]{1,2,0:T(8,128)(2,1)}, u32[]{:S(2)}, u32[]{:S(2)}) collective-permute-start(bf16[64,128,64]{1,2,0:T(8,128)(2,1)} %get-tuple-element.12), channel_id=1, source_target_pairs={{0,1},{1,0},{2,3},{3,2},{4,5},{5,4},{6,7},{7,6},{8,9},{9,8},{10,11... | collective-permute-start | bytes 3145736 | tf_op jit(solution)/shard_map/ppermute | solution.py:12
  174.0 2.8 %maximum_select_fusion = bf16[128,128,64]{1,2,0:T(8,128)(2,1)S(1)} fusion(bf16[64,128,64]{1,2,0:T(8,128)(2,1)} %collective-permute-done.2, bf16[64,128,64]{1,2,0:T(8,128)(2,1)} %get-tuple-element.11, pred[]{:T(512)S(6)} %eq.2), kind=kLoop, calls=%fused_computation.20 | loop fusion | flops 3145728 | bytes 4194305 | tf_op jit(solution)/shard_map/jit(_where)/select_n | solution.py:158
  179.0 2.2 %fusion.4 = bf16[128,128,64]{0,2,1:T(8,128)(2,1)} fusion(f32[128,128,64]{0,2,1:T(8,128)S(1)} %copy-done.2, f32[8,16,64,128]{3,2,1,0:T(8,128)S(1)} %fusion.32, bf16[128,128,64]{0,2,1:T(8,128)(2,1)S(1)} %bitcast.112, f32[128]{0:T(128)S(1)} %add.68, f32[128,128]{0,1:T(8,128)S(1)} %copy-done.6), kind=kLoop, calls=%fused_computation.6 | loop fusion | flops 6291456 | bytes 12648960 | tf_op jit(solution)/shard_map/convert_element_type | solution.py:169
  181.2 4.1 %copy.183 = bf16[128,8192]{1,0:T(8,128)(2,1)} copy(bf16[128,8192]{0,1:T(8,128)(2,1)} %bitcast.116) | data formatting | bytes 4194304 | tf_op jit(solution)/shard_map/reshape | solution.py:169
  (90 shorter events, 40.6 us)
Async XLA Ops:
  0.9 22.0 %copy-start.5 = (f32[128,128]{1,0:T(8,128)}, f32[128,128]{1,0:T(8,128)S(1)}, u32[]{:S(2)}) copy-start(f32[128,128]{1,0:T(8,128)S(1)} %reduce_window_sum.11) | copy-start | bytes 196612
  7.4 2.6 %copy-start = (f32[8,16,64,128]{3,2,1,0:T(8,128)}, f32[8,16,64,128]{3,2,1,0:T(8,128)S(1)}, u32[]{:S(2)}) copy-start(f32[8,16,64,128]{3,2,1,0:T(8,128)S(1)} %fusion.9) | copy-start | bytes 12582916
  7.4 11.4 %copy-start.8 = (f32[8]{0:T(128)S(1)}, f32[8]{0:T(128)}, u32[]{:S(2)}) copy-start(f32[8]{0:T(128)} %param.11) | copy-start | bytes 100
  10.1 13.2 %collective-permute-start.1 = (f32[64,128,64]{1,2,0:T(8,128)}, f32[64,128,64]{1,2,0:T(8,128)}, u32[]{:S(2)}, u32[]{:S(2)}) collective-permute-start(f32[64,128,64]{1,2,0:T(8,128)} %constant_dynamic-slice_fusion), channel_id=1, source_target_pairs={{0,1},{1,0},{2,3},{3,2},{4,5},{5,4},{6,7},{7,6},{8,9},{9,8},{10,11... | collective-permute-start | bytes 6291464 | tf_op jit(solution)/shard_map/ppermute | solution.py:12
  18.9 3.7 %collective-permute-start = (f32[136]{0:T(256)S(1)}, f32[136]{0:T(256)S(1)}, u32[]{:S(2)}, u32[]{:S(2)}) collective-permute-start(f32[136]{0:T(256)S(1)} %pad_maximum_fusion.2), channel_id=1, source_target_pairs={{0,1},{1,0},{2,3},{3,2},{4,5},{5,4},{6,7},{7,6},{8,9},{9,8},{10,11... | collective-permute-start | bytes 1640 | tf_op jit(solution)/shard_map/ppermute | solution.py:12
  25.9 10.3 %copy-start.4 = (bf16[128,1024]{1,0:T(8,128)(2,1)S(1)}, bf16[128,1024]{1,0:T(8,128)(2,1)}, u32[]{:S(2)}) copy-start(bf16[128,1024]{1,0:T(8,128)(2,1)} %param.9) | copy-start | bytes 786436
  27.0 36.8 %all-to-all-start = ((bf16[8,9,128,64]{2,3,1,0:T(8,128)(2,1)}), bf16[8,9,128,64]{2,3,1,0:T(8,128)(2,1)S(1)}, u32[]{:S(2)}, u32[]{:S(2)}) async-start(bf16[8,9,128,64]{2,3,1,0:T(8,128)(2,1)} %pad_maximum_fusion), calls=%async_computation | async-start | bytes 2359296 | tf_op jit(solution)/shard_map/all_to_all | solution.py:103
  66.6 2.0 %copy-start.3 = (f32[9,8,128,64]{2,0,3,1:T(8,128)}, f32[9,8,128,64]{2,0,3,1:T(8,128)S(1)}, u32[]{:S(2)}) copy-start(f32[9,8,128,64]{2,0,3,1:T(8,128)S(1)} %convolution_bitcast_fusion) | copy-start | bytes 7077892
  73.9 22.4 %all-to-all-start.1 = ((f32[32,1,2560]{2,1,0:T(1,128)}), f32[32,1,2560]{2,1,0:T(1,128)}, u32[]{:S(2)}, u32[]{:S(2)}) async-start(f32[32,1,2560]{2,1,0:T(1,128)} %reshape.394), calls=%async_computation.1 | async-start | bytes 655360 | tf_op jit(solution)/shard_map/all_to_all | solution.py:140
  111.2 15.4 %all-to-all-start.2 = ((f32[32,1,2048]{2,1,0:T(1,128)}), f32[32,1,2048]{2,1,0:T(1,128)}, u32[]{:S(2)}, u32[]{:S(2)}) async-start(f32[32,1,2048]{2,1,0:T(1,128)} %reshape.396), calls=%async_computation.2 | async-start | bytes 524288 | tf_op jit(solution)/shard_map/all_to_all | solution.py:147
  134.9 27.1 %copy-start.1 = (f32[8,16,64,128]{3,2,1,0:T(8,128)S(1)}, f32[8,16,64,128]{3,2,1,0:T(8,128)}, u32[]{:S(2)}) copy-start(f32[8,16,64,128]{3,2,1,0:T(8,128)} %copy-done) | copy-start | bytes 12582916
  162.0 9.4 %copy-start.7 = (f32[128,128]{1,0:T(8,128)S(1)}, f32[128,128]{1,0:T(8,128)}, u32[]{:S(2)}) copy-start(f32[128,128]{1,0:T(8,128)} %get-tuple-element.15) | copy-start | bytes 196612
  165.6 8.5 %collective-permute-start.2 = (bf16[64,128,64]{1,2,0:T(8,128)(2,1)}, bf16[64,128,64]{1,2,0:T(8,128)(2,1)}, u32[]{:S(2)}, u32[]{:S(2)}) collective-permute-start(bf16[64,128,64]{1,2,0:T(8,128)(2,1)} %get-tuple-element.12), channel_id=1, source_target_pairs={{0,1},{1,0},{2,3},{3,2},{4,5},{5,4},{6,7},{7,6},{8,9},{9,8},{10,11... | collective-permute-start | bytes 3145736 | tf_op jit(solution)/shard_map/ppermute | solution.py:12
  176.8 2.2 %copy-start.2 = (f32[128,128,64]{0,2,1:T(8,128)S(1)}, f32[128,128,64]{0,2,1:T(8,128)}, u32[]{:S(2)}) copy-start(f32[128,128,64]{0,2,1:T(8,128)} %convolution_bitcast_fusion.1) | copy-start | bytes 12582916
  176.8 2.2 %copy-start.6 = (f32[128,128]{0,1:T(8,128)S(1)}, f32[128,128]{0,1:T(8,128)}, u32[]{:S(2)}) copy-start(f32[128,128]{0,1:T(8,128)} %copy.168) | copy-start | bytes 196612

commit v8 on v7

--- a/solution.py
+++ b/solution.py
@@ -129,23 +129,21 @@
     starts, run = scan[:n_z], scan[n_z]
     lead, before = leads[:n_z], leads[n_z]
 
-    piece = state // n_seq
+    per = quarter * width // n_seq
+    chunks = run.transpose(0, 2, 1).reshape(n_seq, per, state)
+    row_totals = jnp.repeat(before, width).reshape(n_seq, per)
     packed = jnp.concatenate(
-        [
-            run.reshape(quarter, n_seq, piece, width),
-            jnp.broadcast_to(before[:, None, None, None], (quarter, n_seq, 1, width)),
-        ],
-        axis=2,
-    ).transpose(1, 0, 2, 3)
+        [chunks, jnp.pad(row_totals, ((0, 0), (0, state - per)))[:, None, :]], axis=1
+    )
     gathered = lax.all_to_all(packed, "seq", 0, 0, tiled=True)
-    row_state = gathered[:, :, :piece]
-    row_total = gathered[:, :, piece, 0]
     entering = jnp.einsum(
-        "hab,bhrw->ahrw", decay_matrix(row_total, n_seq), row_state,
+        "rab,brn->arn",
+        decay_matrix(gathered[:, per, :per], n_seq),
+        gathered[:, :per],
         precision=lax.Precision.HIGHEST,
     )
     acc_s = lax.all_to_all(entering, "seq", 0, 0, tiled=True)
-    acc_s = acc_s.transpose(1, 0, 2, 3).reshape(quarter, state, width)
+    acc_s = acc_s.reshape(quarter, width, state).transpose(0, 2, 1)
 
     chip_in = starts + jnp.exp(lead)[:, :, None, None] * acc_s[None]
     back = lax.all_to_all(chip_in.astype(bf16), "z", 0, 0, tiled=True)

time: 187 us -> 167 us (0.89)
  local copies, waits for them, and re-layouts: 37 us -> 23.7 us
  other arithmetic: 29 us -> 22.7 us
    unnamed x27 -> x22, local copies, waits for them, and re-layouts: 17.4 us -> 9.66 us
    all_to_all x2 -> x0, other arithmetic: 5.15 us -> none  [the longest x1 3.03 us: local(): gathered = lax.all_to_all(packed, 'seq', 0, 0, tiled=True)]
    transpose x2 -> x1, local copies, waits for them, and re-layouts: 3.01 us -> 0.86 us  [local(): jnp.einsum('rab,brn->arn', decay_matrix(gathered[:, per, :per], n_seq), g...]
    unnamed x1 -> x0, other arithmetic: 1.93 us -> none
  transfers between devices with their start and end apart: 6 -> 6, of which waited for: 5 -> 5; matrix products, arithmetic and copies ran while one was open for 9% -> 10% of each run, Pallas kernels for 0% -> 0%
where the time goes in v8:
time: 167 us; the launch traced here: 165 us
  waiting for transfers between devices  44 us (26%)
  starting transfers between devices  36 us (22%)
  blocking collectives  26.8 us (16%)
  local copies, waits for them, and re-layouts  23.7 us (14%)
  other arithmetic  22.7 us (14%)
  matrix products  11.8 us (7%)
    all_to_all x1, blocking collectives, local(): back = lax.all_to_all(chip_in.astype(bf16), 'z', 0, 0, tiled=True)  26.8 us
    all_to_all x1, waiting for transfers between devices, local(): rows = lax.all_to_all(message, 'z', 0, 0, tiled=True)  17.6 us
    ppermute x3, starting transfers between devices, swap(): return lax.ppermute(value, 'core', [(0, 1), (1, 0)])  16.5 us
    all_to_all x1, waiting for transfers between devices, local(): gathered = lax.all_to_all(packed, 'seq', 0, 0, tiled=True)  13.8 us
    all_to_all x1, waiting for transfers between devices, local(): acc_s = lax.all_to_all(entering, 'seq', 0, 0, tiled=True)  10.4 us
    all_to_all x1, starting transfers between devices, local(): gathered = lax.all_to_all(packed, 'seq', 0, 0, tiled=True)  9.78 us
    unnamed x22, local copies, waits for them, and re-layouts  9.66 us
    all_to_all x1, starting transfers between devices, local(): acc_s = lax.all_to_all(entering, 'seq', 0, 0, tiled=True)  5.04 us
  transfers between devices with their start and end apart: 6, of which 5 were waited for; matrix products, arithmetic and copies ran while one was open for 10% of the time, Pallas kernels for 0%

profile of v8, /device:TPU:1, one launch (start us, length us, event | category | flops | bytes accessed | tf_op | source)
XLA Modules:
  0.0 165.5 jit_solution(4616830701808440053)
XLA Ops:
  3.5 3.2 %copy.112 = bf16[128,8192]{0,1:T(8,128)(2,1)S(1)} copy(bf16[128,8192]{1,0:T(8,128)(2,1)} %param.6) | data formatting | bytes 4194304 | tf_op args[0]
  7.4 1.6 constant_dynamic-slice_fusion
  10.0 8.8 %collective-permute-start.1 = (f32[64,128,64]{1,2,0:T(8,128)}, f32[64,128,64]{1,2,0:T(8,128)}, u32[]{:S(2)}, u32[]{:S(2)}) collective-permute-start(f32[64,128,64]{1,2,0:T(8,128)} %constant_dynamic-slice_fusion), channel_id=1, source_target_pairs={{0,1},{1,0},{2,3},{3,2},{4,5},{5,4},{6,7},{7,6},{8,9},{9,8},{10,11... | collective-permute-start | bytes 6291464 | tf_op jit(solution)/shard_map/ppermute | solution.py:12
  18.8 1.9 %collective-permute-start = (f32[136]{0:T(256)S(1)}, f32[136]{0:T(256)S(1)}, u32[]{:S(2)}, u32[]{:S(2)}) collective-permute-start(f32[136]{0:T(256)S(1)} %pad_maximum_fusion.3), channel_id=1, source_target_pairs={{0,1},{1,0},{2,3},{3,2},{4,5},{5,4},{6,7},{7,6},{8,9},{9,8},{10,11... | collective-permute-start | bytes 1640 | tf_op jit(solution)/shard_map/ppermute | solution.py:12
  21.0 1.6 collective-permute-done
  23.2 2.6 %add_convert_fusion = bf16[64,128,64]{1,2,0:T(8,128)(2,1)S(1)} fusion(f32[64,128,64]{1,2,0:T(8,128)} %collective-permute-done.1, f32[128,128,64]{1,2,0:T(8,128)} %bitcast.110, s32[]{:T(128)S(6)} %select_n.101, f32[64]{0:T(128)S(1)} %get-tuple-element.24, pred[]{:T(512)S(6)} %eq.2), kind=kLoop, calls=%fused_computation.21 | loop fusion | flops 2621440 | bytes 5243141 | tf_op jit(solution)/shard_map/convert_element_type | solution.py:87
  27.0 4.7 %all-to-all-start = ((bf16[8,9,128,64]{2,3,1,0:T(8,128)(2,1)}), bf16[8,9,128,64]{2,3,1,0:T(8,128)(2,1)S(1)}, u32[]{:S(2)}, u32[]{:S(2)}) async-start(bf16[8,9,128,64]{2,3,1,0:T(8,128)(2,1)} %pad_maximum_fusion), calls=%async_computation | async-start | bytes 2359296 | tf_op jit(solution)/shard_map/all_to_all | solution.py:103
  34.6 1.6 copy.111
  37.5 3.6 %fusion.1 = bf16[128,128,128]{2,1,0:T(8,128)(2,1)S(1)} fusion(f32[128,128]{1,0:T(8,128)} %copy.111, f32[128,128]{1,0:T(8,128)} %copy.109, f32[8,128,128]{2,1,0:T(8,128)S(1)} %fusion.20, pred[128,128]{1,0:T(8,128)(4,1)S(1)} %iota_compare_fusion.2), kind=kLoop, calls=%fused_computation.2 | loop fusion | flops 12582912 | bytes 4866048 | tf_op jit(solution)/shard_map/convert_element_type | solution.py:110
  41.1 5.0 %convolution_bitcast_fusion.1 = f32[128,128,64]{0,2,1:T(8,128)} fusion(bf16[128,128,128]{2,1,0:T(8,128)(2,1)S(1)} %fusion.1, bf16[128,128,64]{0,2,1:T(8,128)(2,1)S(1)} %bitcast.107), kind=kOutput, calls=%fused_computation.13 | convolution fusion | flops 268435456 | bytes 10485760 | tf_op jit(solution)/shard_map/hts,shp->thp/dot_general | solution.py:111
  46.1 17.6 %all-to-all-done = bf16[8,9,128,64]{2,3,1,0:T(8,128)(2,1)S(1)} async-done(((bf16[8,9,128,64]{2,3,1,0:T(8,128)(2,1)}), bf16[8,9,128,64]{2,3,1,0:T(8,128)(2,1)S(1)}, u32[]{:S(2)}, u32[]{:S(2)}) %all-to-all-start) | async-done | bytes 1179680 | tf_op jit(solution)/shard_map/all_to_all | solution.py:103
  64.8 2.1 %convolution_bitcast_fusion = f32[9,8,128,64]{2,0,3,1:T(8,128)S(1)} fusion(bf16[8,8,128,64]{2,3,1,0:T(8,128)(2,1)S(1)} %slice.87, f32[8,9,8,1]{1,0,2,3:T(8,128)S(1)} %fusion.17), kind=kOutput, calls=%fused_computation.12 | convolution fusion | flops 56623104 | bytes 3410176 | tf_op jit(solution)/shard_map/hab,bhnp->ahnp/dot_general | solution.py:120
  66.8 2.0 %copy-done.3 = f32[9,8,128,64]{2,0,3,1:T(8,128)} copy-done((f32[9,8,128,64]{2,0,3,1:T(8,128)}, f32[9,8,128,64]{2,0,3,1:T(8,128)S(1)}, u32[]{:S(2)}) %copy-start.3) | copy-done | bytes 2359320
  69.7 9.8 %all-to-all-start.1 = ((f32[32,17,128]{2,1,0:T(8,128)}), f32[32,17,128]{2,1,0:T(8,128)}, u32[]{:S(2)}, u32[]{:S(2)}) async-start(f32[32,17,128]{2,1,0:T(8,128)} %pad_maximum_fusion.1), calls=%async_computation.1 | async-start | bytes 786432 | tf_op jit(solution)/shard_map/all_to_all | solution.py:138
  79.5 13.8 %all-to-all-done.1 = f32[32,17,128]{2,1,0:T(8,128)} async-done(((f32[32,17,128]{2,1,0:T(8,128)}), f32[32,17,128]{2,1,0:T(8,128)}, u32[]{:S(2)}, u32[]{:S(2)}) %all-to-all-start.1) | async-done | bytes 278560 | tf_op jit(solution)/shard_map/all_to_all | solution.py:138
  97.7 5.0 %all-to-all-start.2 = ((f32[32,16,128]{2,1,0:T(8,128)}), f32[32,16,128]{2,1,0:T(8,128)S(1)}, u32[]{:S(2)}, u32[]{:S(2)}) async-start(f32[32,16,128]{2,1,0:T(8,128)} %copy.132), calls=%async_computation.2 | async-start | bytes 524288 | tf_op jit(solution)/shard_map/all_to_all | solution.py:145
  102.8 10.4 %all-to-all-done.2 = f32[32,16,128]{2,1,0:T(8,128)S(1)} async-done(((f32[32,16,128]{2,1,0:T(8,128)}), f32[32,16,128]{2,1,0:T(8,128)S(1)}, u32[]{:S(2)}, u32[]{:S(2)}) %all-to-all-start.2) | async-done | bytes 262176 | tf_op jit(solution)/shard_map/all_to_all | solution.py:145
  113.2 1.9 %fusion.11 = bf16[8,8,128,64]{2,0,3,1:T(8,128)(2,1)S(1)} fusion(f32[9,8,128,64]{2,0,3,1:T(8,128)} %copy-done.3, f32[8,128,64]{1,2,0:T(8,128)S(1)} %bitcast.120, f32[8,8]{0,1:T(8,128)S(1)} %slice_exponential_fusion), kind=kLoop, calls=%fused_computation.19 | loop fusion | flops 1572864 | bytes 3408128 | tf_op jit(solution)/shard_map/convert_element_type | solution.py:149
  115.4 26.8 %all_to_all.20 = bf16[8,8,128,64]{2,3,1,0:T(8,128)(2,1)S(1)} all-to-all(bf16[8,8,128,64]{2,3,1,0:T(8,128)(2,1)S(1)} %copy.133), channel_id=1, replica_groups=mesh['seq'=32,'z'=8,'core'=2] {'z'}, dimensions={0} | all-to-all | bytes 2097152 | tf_op jit(solution)/shard_map/all_to_all | solution.py:149
  142.2 3.6 %fusion.7 = (bf16[64,128,64]{1,2,0:T(8,128)(2,1)}, bf16[64,128,64]{1,2,0:T(8,128)(2,1)}) fusion(bf16[8,8,128,64]{2,3,1,0:T(8,128)(2,1)S(1)} %all_to_all.20, f32[64]{0:T(128)S(1)} %get-tuple-element.22, pred[]{:T(512)S(6)} %eq.2, f32[64,128,64]{1,2,0:T(8,128)} %collective-permute-done.1, f32[128,128,64]{1,2,0:T(8,128)S(1)} %bitcast.111, s32[]{:T(128)S(6)} %select_n.101), kind=kLoop, calls=%fused_computation.15 | loop fusion | flops 4194304 | bytes 7340293 | tf_op jit(solution)/shard_map/convert_element_type | solution.py:153
  145.8 5.8 %collective-permute-start.2 = (bf16[64,128,64]{1,2,0:T(8,128)(2,1)}, bf16[64,128,64]{1,2,0:T(8,128)(2,1)}, u32[]{:S(2)}, u32[]{:S(2)}) collective-permute-start(bf16[64,128,64]{1,2,0:T(8,128)(2,1)} %get-tuple-element.12), channel_id=1, source_target_pairs={{0,1},{1,0},{2,3},{3,2},{4,5},{5,4},{6,7},{7,6},{8,9},{9,8},{10,11... | collective-permute-start | bytes 3145736 | tf_op jit(solution)/shard_map/ppermute | solution.py:12
  154.3 2.8 %maximum_select_fusion = bf16[128,128,64]{1,2,0:T(8,128)(2,1)S(1)} fusion(bf16[64,128,64]{1,2,0:T(8,128)(2,1)} %collective-permute-done.2, bf16[64,128,64]{1,2,0:T(8,128)(2,1)} %get-tuple-element.11, pred[]{:T(512)S(6)} %eq.2), kind=kLoop, calls=%fused_computation.20 | loop fusion | flops 3145728 | bytes 4194305 | tf_op jit(solution)/shard_map/jit(_where)/select_n | solution.py:156
  159.2 2.2 %fusion.4 = bf16[128,128,64]{0,2,1:T(8,128)(2,1)} fusion(f32[128,128,64]{0,2,1:T(8,128)S(1)} %copy-done.2, f32[8,16,64,128]{3,2,1,0:T(8,128)S(1)} %fusion.31, bf16[128,128,64]{0,2,1:T(8,128)(2,1)S(1)} %bitcast.108, f32[128]{0:T(128)S(1)} %add.70, f32[128,128]{0,1:T(8,128)S(1)} %copy-done.6), kind=kLoop, calls=%fused_computation.6 | loop fusion | flops 6291456 | bytes 12648960 | tf_op jit(solution)/shard_map/convert_element_type | solution.py:167
  161.4 4.1 %copy.137 = bf16[128,8192]{1,0:T(8,128)(2,1)} copy(bf16[128,8192]{0,1:T(8,128)(2,1)} %bitcast.112) | data formatting | bytes 4194304 | tf_op jit(solution)/shard_map/reshape | solution.py:167
  (82 shorter events, 22.6 us)
Async XLA Ops:
  0.9 22.0 %copy-start.5 = (f32[128,128]{1,0:T(8,128)}, f32[128,128]{1,0:T(8,128)S(1)}, u32[]{:S(2)}) copy-start(f32[128,128]{1,0:T(8,128)S(1)} %reduce_window_sum.11) | copy-start | bytes 196612
  7.4 2.6 %copy-start = (f32[8,16,64,128]{3,2,1,0:T(8,128)}, f32[8,16,64,128]{3,2,1,0:T(8,128)S(1)}, u32[]{:S(2)}) copy-start(f32[8,16,64,128]{3,2,1,0:T(8,128)S(1)} %fusion.9) | copy-start | bytes 12582916
  7.4 11.4 %copy-start.8 = (f32[8]{0:T(128)S(1)}, f32[8]{0:T(128)}, u32[]{:S(2)}) copy-start(f32[8]{0:T(128)} %param.11) | copy-start | bytes 100
  10.0 13.2 %collective-permute-start.1 = (f32[64,128,64]{1,2,0:T(8,128)}, f32[64,128,64]{1,2,0:T(8,128)}, u32[]{:S(2)}, u32[]{:S(2)}) collective-permute-start(f32[64,128,64]{1,2,0:T(8,128)} %constant_dynamic-slice_fusion), channel_id=1, source_target_pairs={{0,1},{1,0},{2,3},{3,2},{4,5},{5,4},{6,7},{7,6},{8,9},{9,8},{10,11... | collective-permute-start | bytes 6291464 | tf_op jit(solution)/shard_map/ppermute | solution.py:12
  18.8 3.7 %collective-permute-start = (f32[136]{0:T(256)S(1)}, f32[136]{0:T(256)S(1)}, u32[]{:S(2)}, u32[]{:S(2)}) collective-permute-start(f32[136]{0:T(256)S(1)} %pad_maximum_fusion.3), channel_id=1, source_target_pairs={{0,1},{1,0},{2,3},{3,2},{4,5},{5,4},{6,7},{7,6},{8,9},{9,8},{10,11... | collective-permute-start | bytes 1640 | tf_op jit(solution)/shard_map/ppermute | solution.py:12
  25.9 10.3 %copy-start.4 = (bf16[128,1024]{1,0:T(8,128)(2,1)S(1)}, bf16[128,1024]{1,0:T(8,128)(2,1)}, u32[]{:S(2)}) copy-start(bf16[128,1024]{1,0:T(8,128)(2,1)} %param.9) | copy-start | bytes 786436
  27.0 36.8 %all-to-all-start = ((bf16[8,9,128,64]{2,3,1,0:T(8,128)(2,1)}), bf16[8,9,128,64]{2,3,1,0:T(8,128)(2,1)S(1)}, u32[]{:S(2)}, u32[]{:S(2)}) async-start(bf16[8,9,128,64]{2,3,1,0:T(8,128)(2,1)} %pad_maximum_fusion), calls=%async_computation | async-start | bytes 2359296 | tf_op jit(solution)/shard_map/all_to_all | solution.py:103
  66.8 2.0 %copy-start.3 = (f32[9,8,128,64]{2,0,3,1:T(8,128)}, f32[9,8,128,64]{2,0,3,1:T(8,128)S(1)}, u32[]{:S(2)}) copy-start(f32[9,8,128,64]{2,0,3,1:T(8,128)S(1)} %convolution_bitcast_fusion) | copy-start | bytes 7077892
  69.7 23.6 %all-to-all-start.1 = ((f32[32,17,128]{2,1,0:T(8,128)}), f32[32,17,128]{2,1,0:T(8,128)}, u32[]{:S(2)}, u32[]{:S(2)}) async-start(f32[32,17,128]{2,1,0:T(8,128)} %pad_maximum_fusion.1), calls=%async_computation.1 | async-start | bytes 786432 | tf_op jit(solution)/shard_map/all_to_all | solution.py:138
  97.7 15.5 %all-to-all-start.2 = ((f32[32,16,128]{2,1,0:T(8,128)}), f32[32,16,128]{2,1,0:T(8,128)S(1)}, u32[]{:S(2)}, u32[]{:S(2)}) async-start(f32[32,16,128]{2,1,0:T(8,128)} %copy.132), calls=%async_computation.2 | async-start | bytes 524288 | tf_op jit(solution)/shard_map/all_to_all | solution.py:145
  115.1 27.1 %copy-start.1 = (f32[8,16,64,128]{3,2,1,0:T(8,128)S(1)}, f32[8,16,64,128]{3,2,1,0:T(8,128)}, u32[]{:S(2)}) copy-start(f32[8,16,64,128]{3,2,1,0:T(8,128)} %copy-done) | copy-start | bytes 12582916
  142.2 9.4 %copy-start.7 = (f32[128,128]{1,0:T(8,128)S(1)}, f32[128,128]{1,0:T(8,128)}, u32[]{:S(2)}) copy-start(f32[128,128]{1,0:T(8,128)} %get-tuple-element.15) | copy-start | bytes 196612
  145.8 8.4 %collective-permute-start.2 = (bf16[64,128,64]{1,2,0:T(8,128)(2,1)}, bf16[64,128,64]{1,2,0:T(8,128)(2,1)}, u32[]{:S(2)}, u32[]{:S(2)}) collective-permute-start(bf16[64,128,64]{1,2,0:T(8,128)(2,1)} %get-tuple-element.12), channel_id=1, source_target_pairs={{0,1},{1,0},{2,3},{3,2},{4,5},{5,4},{6,7},{7,6},{8,9},{9,8},{10,11... | collective-permute-start | bytes 3145736 | tf_op jit(solution)/shard_map/ppermute | solution.py:12
  157.0 2.2 %copy-start.2 = (f32[128,128,64]{0,2,1:T(8,128)S(1)}, f32[128,128,64]{0,2,1:T(8,128)}, u32[]{:S(2)}) copy-start(f32[128,128,64]{0,2,1:T(8,128)} %convolution_bitcast_fusion.1) | copy-start | bytes 12582916
  157.0 2.2 %copy-start.6 = (f32[128,128]{0,1:T(8,128)S(1)}, f32[128,128]{0,1:T(8,128)}, u32[]{:S(2)}) copy-start(f32[128,128]{0,1:T(8,128)} %copy.125) | copy-start | bytes 196612

commit v9 on v8

--- a/solution.py
+++ b/solution.py
@@ -153,18 +153,31 @@
     keep = jnp.where(c_idx == 0, entry, into_second).astype(bf16)
     send = jnp.where(c_idx == 0, into_second, entry).astype(bf16)
     other = swap(send)
-    carried_in = jnp.where(
+
+    groups = G // n_core
+    c_keep = lax.dynamic_slice_in_dim(c, c_idx * groups, groups, 1)
+    c_other = lax.dynamic_slice_in_dim(c, (1 - c_idx) * groups, groups, 1)
+    out_keep = jnp.einsum(
+        "tgn,ghnp->tghp", c_keep, keep.reshape(groups, per_group, state, width),
+        preferred_element_type=f32,
+    ).reshape(tokens, half * width)
+    out_other = jnp.einsum(
+        "tgn,ghnp->tghp", c_other, other.reshape(groups, per_group, state, width),
+        preferred_element_type=f32,
+    ).reshape(tokens, half * width)
+    outside = jnp.where(
         c_idx == 0,
-        jnp.concatenate([keep, other], axis=0),
-        jnp.concatenate([other, keep], axis=0),
+        jnp.concatenate([out_keep, out_other], axis=1),
+        jnp.concatenate([out_other, out_keep], axis=1),
     )
-
-    outside = jnp.einsum(
-        "tgn,ghnp->tghp", c, carried_in.reshape(G, per_group, state, width),
-        preferred_element_type=f32,
-    ).reshape(tokens, heads, width)
-    mixed = inside + jnp.exp(within)[..., None] * outside + skip[None, :, None] * x.astype(f32)
-    return mixed.astype(bf16).reshape(tokens, heads * width)
+    decay_in = jnp.repeat(jnp.exp(within), width, axis=1)
+    gain = jnp.repeat(skip, width)[None, :]
+    mixed = (
+        inside.reshape(tokens, heads * width)
+        + decay_in * outside
+        + gain * features.astype(f32)
+    )
+    return mixed.astype(bf16)
 
 
 def solution(mesh):

time: 167 us -> 168 us (level)
  matrix products: 11.8 us -> 15.3 us
    convert_element_type x0 -> x1, local copies, waits for them, and re-layouts: none -> 4.06 us  [local(): return mixed.astype(bf16)]
    reshape x1 -> x0, local copies, waits for them, and re-layouts: 4.06 us -> none  [local(): return mixed.astype(bf16).reshape(tokens, heads * width)]
    select_n x1 -> x0, other arithmetic: 2.76 us -> none  [local(): jnp.where(c_idx == 0, jnp.concatenate([keep, other], axis=0), jnp.concate...]
    dot_general x1 -> x2, matrix products: 0.71 us -> 3.45 us  [the longest x1 1.8 us: local(): jnp.einsum('tgn,ghnp->tghp', c_keep, keep.reshape(groups, per_group, stat...]
    unnamed x22 -> x18, local copies, waits for them, and re-layouts: 9.66 us -> 8.33 us
  transfers between devices with their start and end apart: 6 -> 6, of which waited for: 5 -> 4; matrix products, arithmetic and copies ran while one was open for 10% -> 11% of each run, Pallas kernels for 0% -> 0%
where the time goes in v9:
time: 168 us; the launch traced here: 167 us
  waiting for transfers between devices  44.2 us (26%)
  starting transfers between devices  36.1 us (21%)
  blocking collectives  26.8 us (16%)
  local copies, waits for them, and re-layouts  22.8 us (14%)
  other arithmetic  21.3 us (13%)
  matrix products  15.3 us (9%)
    all_to_all x1, blocking collectives, local(): back = lax.all_to_all(chip_in.astype(bf16), 'z', 0, 0, tiled=True)  26.8 us
    all_to_all x1, waiting for transfers between devices, local(): rows = lax.all_to_all(message, 'z', 0, 0, tiled=True)  18.4 us
    ppermute x3, starting transfers between devices, swap(): return lax.ppermute(value, 'core', [(0, 1), (1, 0)])  16.5 us
    all_to_all x1, waiting for transfers between devices, local(): gathered = lax.all_to_all(packed, 'seq', 0, 0, tiled=True)  13.8 us
    all_to_all x1, waiting for transfers between devices, local(): acc_s = lax.all_to_all(entering, 'seq', 0, 0, tiled=True)  10.4 us
    all_to_all x1, starting transfers between devices, local(): gathered = lax.all_to_all(packed, 'seq', 0, 0, tiled=True)  9.79 us
    unnamed x18, local copies, waits for them, and re-layouts  8.33 us
    all_to_all x1, starting transfers between devices, local(): acc_s = lax.all_to_all(entering, 'seq', 0, 0, tiled=True)  5.16 us
  transfers between devices with their start and end apart: 6, of which 4 were waited for; matrix products, arithmetic and copies ran while one was open for 11% of the time, Pallas kernels for 0%

profile of v9, /device:TPU:1, one launch (start us, length us, event | category | flops | bytes accessed | tf_op | source)
XLA Modules:
  0.0 167.0 jit_solution(4193477443967970807)
XLA Ops:
  3.4 3.2 %copy.120 = bf16[128,8192]{0,1:T(8,128)(2,1)S(1)} copy(bf16[128,8192]{1,0:T(8,128)(2,1)} %param.6) | data formatting | bytes 4194304 | tf_op args[0]
  7.4 1.6 constant_dynamic-slice_fusion
  10.0 8.8 %collective-permute-start.1 = (f32[64,128,64]{1,2,0:T(8,128)}, f32[64,128,64]{1,2,0:T(8,128)}, u32[]{:S(2)}, u32[]{:S(2)}) collective-permute-start(f32[64,128,64]{1,2,0:T(8,128)} %constant_dynamic-slice_fusion), channel_id=1, source_target_pairs={{0,1},{1,0},{2,3},{3,2},{4,5},{5,4},{6,7},{7,6},{8,9},{9,8},{10,11... | collective-permute-start | bytes 6291464 | tf_op jit(solution)/shard_map/ppermute | solution.py:12
  18.8 1.9 %collective-permute-start = (f32[136]{0:T(256)S(1)}, f32[136]{0:T(256)S(1)}, u32[]{:S(2)}, u32[]{:S(2)}) collective-permute-start(f32[136]{0:T(256)S(1)} %pad_maximum_fusion.3), channel_id=1, source_target_pairs={{0,1},{1,0},{2,3},{3,2},{4,5},{5,4},{6,7},{7,6},{8,9},{9,8},{10,11... | collective-permute-start | bytes 1640 | tf_op jit(solution)/shard_map/ppermute | solution.py:12
  20.9 1.6 collective-permute-done
  23.2 2.6 %add_convert_fusion = bf16[64,128,64]{1,2,0:T(8,128)(2,1)S(1)} fusion(f32[64,128,64]{1,2,0:T(8,128)} %collective-permute-done.1, f32[128,128,64]{1,2,0:T(8,128)} %bitcast.113, s32[]{:T(128)S(6)} %select_n.103, f32[64]{0:T(128)S(1)} %get-tuple-element.24, pred[]{:T(512)S(6)} %eq.2), kind=kLoop, calls=%fused_computation.20 | loop fusion | flops 2621440 | bytes 5243141 | tf_op jit(solution)/shard_map/convert_element_type | solution.py:87
  27.0 4.7 %all-to-all-start = ((bf16[8,9,128,64]{2,3,1,0:T(8,128)(2,1)}), bf16[8,9,128,64]{2,3,1,0:T(8,128)(2,1)S(1)}, u32[]{:S(2)}, u32[]{:S(2)}) async-start(bf16[8,9,128,64]{2,3,1,0:T(8,128)(2,1)} %pad_maximum_fusion), calls=%async_computation | async-start | bytes 2359296 | tf_op jit(solution)/shard_map/all_to_all | solution.py:103
  35.5 3.6 %fusion.1 = bf16[128,128,128]{2,1,0:T(8,128)(2,1)S(1)} fusion(f32[128,128]{1,0:T(8,128)} %copy.119, f32[128,128]{1,0:T(8,128)} %copy.117, f32[8,128,128]{2,1,0:T(8,128)S(1)} %fusion.19, pred[128,128]{1,0:T(8,128)(4,1)S(1)} %iota_compare_fusion.2), kind=kLoop, calls=%fused_computation.2 | loop fusion | flops 12582912 | bytes 4866048 | tf_op jit(solution)/shard_map/convert_element_type | solution.py:110
  40.3 5.0 %convolution_bitcast_fusion.1 = f32[128,128,64]{0,2,1:T(8,128)} fusion(bf16[128,128,128]{2,1,0:T(8,128)(2,1)S(1)} %fusion.1, bf16[128,128,64]{0,2,1:T(8,128)(2,1)S(1)} %bitcast.111), kind=kOutput, calls=%fused_computation.13 | convolution fusion | flops 268435456 | bytes 10485760 | tf_op jit(solution)/shard_map/hts,shp->thp/dot_general | solution.py:111
  45.3 18.4 %all-to-all-done = bf16[8,9,128,64]{2,3,1,0:T(8,128)(2,1)S(1)} async-done(((bf16[8,9,128,64]{2,3,1,0:T(8,128)(2,1)}), bf16[8,9,128,64]{2,3,1,0:T(8,128)(2,1)S(1)}, u32[]{:S(2)}, u32[]{:S(2)}) %all-to-all-start) | async-done | bytes 1179680 | tf_op jit(solution)/shard_map/all_to_all | solution.py:103
  66.6 2.1 %convolution_bitcast_fusion = f32[9,8,128,64]{2,0,3,1:T(8,128)S(1)} fusion(bf16[8,8,128,64]{2,3,1,0:T(8,128)(2,1)S(1)} %slice.87, f32[8,9,8,1]{1,0,2,3:T(8,128)S(1)} %fusion.16), kind=kOutput, calls=%fused_computation.12 | convolution fusion | flops 56623104 | bytes 3410176 | tf_op jit(solution)/shard_map/hab,bhnp->ahnp/dot_general | solution.py:120
  68.7 2.0 %copy-done.3 = f32[9,8,128,64]{2,0,3,1:T(8,128)} copy-done((f32[9,8,128,64]{2,0,3,1:T(8,128)}, f32[9,8,128,64]{2,0,3,1:T(8,128)S(1)}, u32[]{:S(2)}) %copy-start.3) | copy-done | bytes 2359320
  71.6 9.8 %all-to-all-start.1 = ((f32[32,17,128]{2,1,0:T(8,128)}), f32[32,17,128]{2,1,0:T(8,128)}, u32[]{:S(2)}, u32[]{:S(2)}) async-start(f32[32,17,128]{2,1,0:T(8,128)} %pad_maximum_fusion.1), calls=%async_computation.1 | async-start | bytes 786432 | tf_op jit(solution)/shard_map/all_to_all | solution.py:138
  81.4 13.8 %all-to-all-done.1 = f32[32,17,128]{2,1,0:T(8,128)} async-done(((f32[32,17,128]{2,1,0:T(8,128)}), f32[32,17,128]{2,1,0:T(8,128)}, u32[]{:S(2)}, u32[]{:S(2)}) %all-to-all-start.1) | async-done | bytes 278560 | tf_op jit(solution)/shard_map/all_to_all | solution.py:138
  99.6 5.2 %all-to-all-start.2 = ((f32[32,16,128]{2,1,0:T(8,128)}), f32[32,16,128]{2,1,0:T(8,128)}, u32[]{:S(2)}, u32[]{:S(2)}) async-start(f32[32,16,128]{2,1,0:T(8,128)} %copy.140), calls=%async_computation.2 | async-start | bytes 524288 | tf_op jit(solution)/shard_map/all_to_all | solution.py:145
  104.8 10.4 %all-to-all-done.2 = f32[32,16,128]{2,1,0:T(8,128)} async-done(((f32[32,16,128]{2,1,0:T(8,128)}), f32[32,16,128]{2,1,0:T(8,128)}, u32[]{:S(2)}, u32[]{:S(2)}) %all-to-all-start.2) | async-done | bytes 262176 | tf_op jit(solution)/shard_map/all_to_all | solution.py:145
  115.2 1.9 %fusion.10 = bf16[8,8,128,64]{2,0,3,1:T(8,128)(2,1)S(1)} fusion(f32[9,8,128,64]{2,0,3,1:T(8,128)} %copy-done.3, f32[8,128,64]{1,2,0:T(8,128)} %bitcast.31, f32[8,8]{0,1:T(8,128)S(1)} %slice_exponential_fusion), kind=kLoop, calls=%fused_computation.19 | loop fusion | flops 1572864 | bytes 3408128 | tf_op jit(solution)/shard_map/convert_element_type | solution.py:149
  117.3 26.8 %all_to_all.20 = bf16[8,8,128,64]{2,3,1,0:T(8,128)(2,1)S(1)} all-to-all(bf16[8,8,128,64]{2,3,1,0:T(8,128)(2,1)S(1)} %copy.141), channel_id=1, replica_groups=mesh['seq'=32,'z'=8,'core'=2] {'z'}, dimensions={0} | all-to-all | bytes 2097152 | tf_op jit(solution)/shard_map/all_to_all | solution.py:149
  144.2 3.6 %fusion.7 = (bf16[64,128,64]{1,2,0:T(8,128)(2,1)}, bf16[64,128,64]{1,2,0:T(8,128)(2,1)}) fusion(bf16[8,8,128,64]{2,3,1,0:T(8,128)(2,1)S(1)} %all_to_all.20, f32[64]{0:T(128)S(1)} %get-tuple-element.22, pred[]{:T(512)S(6)} %eq.2, f32[64,128,64]{1,2,0:T(8,128)} %collective-permute-done.1, f32[128,128,64]{1,2,0:T(8,128)S(1)} %bitcast.114, s32[]{:T(128)S(6)} %select_n.103), kind=kLoop, calls=%fused_computation.15 | loop fusion | flops 4194304 | bytes 7340293 | tf_op jit(solution)/shard_map/convert_element_type | solution.py:153
  147.8 5.8 %collective-permute-start.2 = (bf16[64,128,64]{1,2,0:T(8,128)(2,1)}, bf16[64,128,64]{1,2,0:T(8,128)(2,1)}, u32[]{:S(2)}, u32[]{:S(2)}) collective-permute-start(bf16[64,128,64]{1,2,0:T(8,128)(2,1)} %get-tuple-element.12), channel_id=1, source_target_pairs={{0,1},{1,0},{2,3},{3,2},{4,5},{5,4},{6,7},{7,6},{8,9},{9,8},{10,11... | collective-permute-start | bytes 3145736 | tf_op jit(solution)/shard_map/ppermute | solution.py:12
  155.7 1.8 %fusion.42 = f32[4,16,64,128]{3,2,1,0:T(8,128)S(1)} fusion(bf16[4,16,128,64]{2,3,1,0:T(8,128)(2,1)} %bitcast.117, bf16[128,8,128]{0,2,1:T(8,128)(2,1)S(1)} %bitcast.120, s32[]{:T(128)S(6)} %select_n.117), kind=kOutput, calls=%fused_computation.60 | convolution fusion | flops 134217728 | bytes 3276804 | tf_op jit(solution)/shard_map/tgn,ghnp->tghp/dot_general | solution.py:160
  157.5 1.7 fusion.40
  159.2 3.8 %fusion.5 = bf16[128,8192]{0,1:T(8,128)(2,1)} fusion(f32[128,4096]{0,1:T(8,128)S(1)} %bitcast.116, f32[128,4096]{0,1:T(8,128)S(1)} %bitcast.115, f32[128,128,64]{0,2,1:T(8,128)S(1)} %copy-done.2, f32[8192]{0:T(1024)S(1)} %mul.100, f32[128,128]{0,1:T(8,128)S(1)} %copy-done.4, pred[]{:T(512)S(6)} %eq.2, bf16[128,8192]{0,1:T(8,128)(2,1)S(1)} %copy.120), kind=kLoop, calls=%fused_computation.7 | loop fusion | flops 9437184 | bytes 12681217 | tf_op jit(solution)/shard_map/convert_element_type | solution.py:180
  163.0 4.1 %copy.146 = bf16[128,8192]{1,0:T(8,128)(2,1)} copy(bf16[128,8192]{0,1:T(8,128)(2,1)} %fusion.5) | data formatting | bytes 4194304 | tf_op jit(solution)/shard_map/convert_element_type | solution.py:180
  (80 shorter events, 22.6 us)
Async XLA Ops:
  7.4 2.6 %copy-start = (f32[8,16,64,128]{3,2,1,0:T(8,128)}, f32[8,16,64,128]{3,2,1,0:T(8,128)S(1)}, u32[]{:S(2)}) copy-start(f32[8,16,64,128]{3,2,1,0:T(8,128)S(1)} %fusion.9) | copy-start | bytes 12582916
  7.4 11.4 %copy-start.6 = (f32[8]{0:T(128)S(1)}, f32[8]{0:T(128)}, u32[]{:S(2)}) copy-start(f32[8]{0:T(128)} %param.11) | copy-start | bytes 100
  10.0 13.2 %collective-permute-start.1 = (f32[64,128,64]{1,2,0:T(8,128)}, f32[64,128,64]{1,2,0:T(8,128)}, u32[]{:S(2)}, u32[]{:S(2)}) collective-permute-start(f32[64,128,64]{1,2,0:T(8,128)} %constant_dynamic-slice_fusion), channel_id=1, source_target_pairs={{0,1},{1,0},{2,3},{3,2},{4,5},{5,4},{6,7},{7,6},{8,9},{9,8},{10,11... | collective-permute-start | bytes 6291464 | tf_op jit(solution)/shard_map/ppermute | solution.py:12
  18.8 3.7 %collective-permute-start = (f32[136]{0:T(256)S(1)}, f32[136]{0:T(256)S(1)}, u32[]{:S(2)}, u32[]{:S(2)}) collective-permute-start(f32[136]{0:T(256)S(1)} %pad_maximum_fusion.3), channel_id=1, source_target_pairs={{0,1},{1,0},{2,3},{3,2},{4,5},{5,4},{6,7},{7,6},{8,9},{9,8},{10,11... | collective-permute-start | bytes 1640 | tf_op jit(solution)/shard_map/ppermute | solution.py:12
  25.8 6.5 %copy-start.5 = (bf16[128,128]{1,0:T(8,128)(2,1)S(1)}, bf16[128,128]{1,0:T(8,128)(2,1)}, u32[]{:S(2)}) copy-start(bf16[128,128]{1,0:T(8,128)(2,1)} %param.7) | copy-start | bytes 98308
  27.0 36.8 %all-to-all-start = ((bf16[8,9,128,64]{2,3,1,0:T(8,128)(2,1)}), bf16[8,9,128,64]{2,3,1,0:T(8,128)(2,1)S(1)}, u32[]{:S(2)}, u32[]{:S(2)}) async-start(bf16[8,9,128,64]{2,3,1,0:T(8,128)(2,1)} %pad_maximum_fusion), calls=%async_computation | async-start | bytes 2359296 | tf_op jit(solution)/shard_map/all_to_all | solution.py:103
  68.7 2.0 %copy-start.3 = (f32[9,8,128,64]{2,0,3,1:T(8,128)}, f32[9,8,128,64]{2,0,3,1:T(8,128)S(1)}, u32[]{:S(2)}) copy-start(f32[9,8,128,64]{2,0,3,1:T(8,128)S(1)} %convolution_bitcast_fusion) | copy-start | bytes 7077892
  71.6 23.6 %all-to-all-start.1 = ((f32[32,17,128]{2,1,0:T(8,128)}), f32[32,17,128]{2,1,0:T(8,128)}, u32[]{:S(2)}, u32[]{:S(2)}) async-start(f32[32,17,128]{2,1,0:T(8,128)} %pad_maximum_fusion.1), calls=%async_computation.1 | async-start | bytes 786432 | tf_op jit(solution)/shard_map/all_to_all | solution.py:138
  99.6 15.5 %all-to-all-start.2 = ((f32[32,16,128]{2,1,0:T(8,128)}), f32[32,16,128]{2,1,0:T(8,128)}, u32[]{:S(2)}, u32[]{:S(2)}) async-start(f32[32,16,128]{2,1,0:T(8,128)} %copy.140), calls=%async_computation.2 | async-start | bytes 524288 | tf_op jit(solution)/shard_map/all_to_all | solution.py:145
  117.1 27.1 %copy-start.1 = (f32[8,16,64,128]{3,2,1,0:T(8,128)S(1)}, f32[8,16,64,128]{3,2,1,0:T(8,128)}, u32[]{:S(2)}) copy-start(f32[8,16,64,128]{3,2,1,0:T(8,128)} %copy-done) | copy-start | bytes 12582916
  147.8 9.7 %collective-permute-start.2 = (bf16[64,128,64]{1,2,0:T(8,128)(2,1)}, bf16[64,128,64]{1,2,0:T(8,128)(2,1)}, u32[]{:S(2)}, u32[]{:S(2)}) collective-permute-start(bf16[64,128,64]{1,2,0:T(8,128)(2,1)} %get-tuple-element.12), channel_id=1, source_target_pairs={{0,1},{1,0},{2,3},{3,2},{4,5},{5,4},{6,7},{7,6},{8,9},{9,8},{10,11... | collective-permute-start | bytes 3145736 | tf_op jit(solution)/shard_map/ppermute | solution.py:12
  155.7 3.5 %copy-start.2 = (f32[128,128,64]{0,2,1:T(8,128)S(1)}, f32[128,128,64]{0,2,1:T(8,128)}, u32[]{:S(2)}) copy-start(f32[128,128,64]{0,2,1:T(8,128)} %convolution_bitcast_fusion.1) | copy-start | bytes 12582916
  157.5 1.7 %copy-start.4 = (f32[128,128]{0,1:T(8,128)S(1)}, f32[128,128]{0,1:T(8,128)}, u32[]{:S(2)}) copy-start(f32[128,128]{0,1:T(8,128)} %copy.133) | copy-start | bytes 196612

commit v10 on v8

--- a/solution.py
+++ b/solution.py
@@ -60,7 +60,23 @@
     total = within[-1]
     b = b_matrix.reshape(tokens, G, state)
     c = c_matrix.reshape(tokens, G, state)
-    partner = swap(jnp.concatenate([total, skip_gain.astype(f32)]))
+    factor = jnp.exp(total[None, :] - within) * step
+    scaled = (x * factor[..., None]).astype(bf16)
+    update = jnp.einsum(
+        "sgn,sghp->ghnp", b, scaled.reshape(tokens, G, per_group, width),
+        preferred_element_type=f32,
+    ).reshape(heads, state, width)
+
+    own = lax.dynamic_slice_in_dim(update, c_idx * half, half, 0)
+    small = jnp.zeros((state, width), f32).at[:heads, 0].set(total)
+    small = small.at[: skip_gain.shape[0], 1].set(skip_gain.astype(f32))
+    got = swap(
+        jnp.concatenate(
+            [lax.dynamic_slice_in_dim(update, (1 - c_idx) * half, half, 0), small[None]], axis=0
+        )
+    )
+    partner = jnp.concatenate([got[half, :heads, 0], got[half, : skip_gain.shape[0], 1]])
+    got = got[:half]
     t_first = jnp.where(c_idx == 0, total, partner[:heads])
     t_second = jnp.where(c_idx == 0, partner[:heads], total)
     chip_skip = jnp.where(
@@ -69,15 +85,6 @@
         jnp.concatenate([partner[heads:], skip_gain.astype(f32)]),
     )
 
-    factor = jnp.exp(total[None, :] - within) * step
-    scaled = (x * factor[..., None]).astype(bf16)
-    update = jnp.einsum(
-        "sgn,sghp->ghnp", b, scaled.reshape(tokens, G, per_group, width),
-        preferred_element_type=f32,
-    ).reshape(heads, state, width)
-
-    own = lax.dynamic_slice_in_dim(update, c_idx * half, half, 0)
-    got = swap(lax.dynamic_slice_in_dim(update, (1 - c_idx) * half, half, 0))
     first = jnp.where(c_idx == 0, own, got)
     second = jnp.where(c_idx == 0, got, own)
     t_first = lax.dynamic_slice_in_dim(t_first, c_idx * half, half)

time: 167 us -> 177 us (1.060)
  other arithmetic: 22.7 us -> 27.8 us
  local copies, waits for them, and re-layouts: 23.7 us -> 26.4 us
  waiting for transfers between devices: 44 us -> 46.4 us
    concatenate x1, other arithmetic: 0.01 us -> 3.2 us  [local(): jnp.concatenate([lax.dynamic_slice_in_dim(update, (1 - c_idx) * half, hal...]
    ppermute x3 -> x2, waiting for transfers between devices: 2.18 us -> 4.53 us  [swap(): return lax.ppermute(value, 'core', [(0, 1), (1, 0)])]
    ppermute x3 -> x2, starting transfers between devices: 16.5 us -> 16.2 us  [swap(): return lax.ppermute(value, 'core', [(0, 1), (1, 0)])]
  transfers between devices with their start and end apart: 6 -> 5, of which waited for: 5 -> 5; matrix products, arithmetic and copies ran while one was open for 10% -> 9% of each run, Pallas kernels for 0% -> 0%
where the time goes in v10:
time: 177 us; the launch traced here: 175 us
  waiting for transfers between devices  46.4 us (26%)
  starting transfers between devices  35.7 us (20%)
  other arithmetic  27.8 us (16%)
  blocking collectives  26.8 us (15%)
  local copies, waits for them, and re-layouts  26.4 us (15%)
  matrix products  11.8 us (7%)
    all_to_all x1, blocking collectives, local(): back = lax.all_to_all(chip_in.astype(bf16), 'z', 0, 0, tiled=True)  26.8 us
    all_to_all x1, waiting for transfers between devices, local(): rows = lax.all_to_all(message, 'z', 0, 0, tiled=True)  17.7 us
    ppermute x2, starting transfers between devices, swap(): return lax.ppermute(value, 'core', [(0, 1), (1, 0)])  16.2 us
    all_to_all x1, waiting for transfers between devices, local(): gathered = lax.all_to_all(packed, 'seq', 0, 0, tiled=True)  13.8 us
    all_to_all x1, waiting for transfers between devices, local(): acc_s = lax.all_to_all(entering, 'seq', 0, 0, tiled=True)  10.4 us
    all_to_all x1, starting transfers between devices, local(): gathered = lax.all_to_all(packed, 'seq', 0, 0, tiled=True)  9.78 us
    unnamed x22, local copies, waits for them, and re-layouts  9.65 us
    all_to_all x1, starting transfers between devices, local(): acc_s = lax.all_to_all(entering, 'seq', 0, 0, tiled=True)  5.03 us
  transfers between devices with their start and end apart: 5, of which 5 were waited for; matrix products, arithmetic and copies ran while one was open for 9% of the time, Pallas kernels for 0%

profile of v10, /device:TPU:1, one launch (start us, length us, event | category | flops | bytes accessed | tf_op | source)
XLA Modules:
  0.0 175.3 jit_solution(15679364447760589305)
XLA Ops:
  5.4 3.2 %copy.112 = bf16[128,8192]{0,1:T(8,128)(2,1)S(1)} copy(bf16[128,8192]{1,0:T(8,128)(2,1)} %param.10) | data formatting | bytes 4194304 | tf_op args[0]
  9.3 1.6 constant_dynamic-slice_fusion
  13.3 3.2 %pad_maximum_fusion = f32[65,128,64]{1,2,0:T(8,128)} fusion(f32[1,128,64]{1,2,0:T(8,128)S(1)} %scatter.9, f32[64,128,64]{1,2,0:T(8,128)} %constant_dynamic-slice_fusion), kind=kLoop, calls=%fused_computation.14 | loop fusion | flops 532480 | bytes 4259840 | tf_op jit(solution)/shard_map/concatenate | solution.py:74
  16.5 8.8 %collective-permute-start = (f32[65,128,64]{1,2,0:T(8,128)}, f32[65,128,64]{1,2,0:T(8,128)}, u32[]{:S(2)}, u32[]{:S(2)}) collective-permute-start(f32[65,128,64]{1,2,0:T(8,128)} %pad_maximum_fusion), channel_id=1, source_target_pairs={{0,1},{1,0},{2,3},{3,2},{4,5},{5,4},{6,7},{7,6},{8,9},{9,8},{10,11... | collective-permute-start | bytes 6389768 | tf_op jit(solution)/shard_map/ppermute | solution.py:12
  25.5 4.0 %collective-permute-done = f32[65,128,64]{1,2,0:T(8,128)} collective-permute-done((f32[65,128,64]{1,2,0:T(8,128)}, f32[65,128,64]{1,2,0:T(8,128)}, u32[]{:S(2)}, u32[]{:S(2)}) %collective-permute-start) | collective-permute-done | bytes 2129952 | tf_op jit(solution)/shard_map/ppermute | solution.py:12
  31.4 2.6 %add_convert_fusion = bf16[64,128,64]{1,2,0:T(8,128)(2,1)S(1)} fusion(f32[65,128,64]{1,2,0:T(8,128)} %collective-permute-done, f32[128,128,64]{1,2,0:T(8,128)} %bitcast.123, s32[]{:T(128)S(6)} %select_n.102, f32[64]{0:T(128)S(1)} %get-tuple-element.50, pred[]{:T(512)S(6)} %eq.2), kind=kLoop, calls=%fused_computation.22 | loop fusion | flops 2621440 | bytes 5243141 | tf_op jit(solution)/shard_map/convert_element_type | solution.py:94
  35.2 4.7 %all-to-all-start = ((bf16[8,9,128,64]{2,3,1,0:T(8,128)(2,1)}), bf16[8,9,128,64]{2,3,1,0:T(8,128)(2,1)S(1)}, u32[]{:S(2)}, u32[]{:S(2)}) async-start(bf16[8,9,128,64]{2,3,1,0:T(8,128)(2,1)} %pad_maximum_fusion.1), calls=%async_computation | async-start | bytes 2359296 | tf_op jit(solution)/shard_map/all_to_all | solution.py:110
  39.9 1.6 copy.109
  45.7 3.6 %fusion.1 = bf16[128,128,128]{2,1,0:T(8,128)(2,1)S(1)} fusion(f32[128,128]{1,0:T(8,128)} %copy.111, f32[128,128]{1,0:T(8,128)} %copy.109, f32[8,128,128]{2,1,0:T(8,128)S(1)} %fusion.20, pred[128,128]{1,0:T(8,128)(4,1)S(1)} %iota_compare_fusion.2), kind=kLoop, calls=%fused_computation.2 | loop fusion | flops 12582912 | bytes 4866048 | tf_op jit(solution)/shard_map/convert_element_type | solution.py:117
  49.3 5.0 %convolution_bitcast_fusion.1 = f32[128,128,64]{0,2,1:T(8,128)} fusion(bf16[128,128,128]{2,1,0:T(8,128)(2,1)S(1)} %fusion.1, bf16[128,128,64]{0,2,1:T(8,128)(2,1)S(1)} %bitcast.120), kind=kOutput, calls=%fused_computation.13 | convolution fusion | flops 268435456 | bytes 10485760 | tf_op jit(solution)/shard_map/hts,shp->thp/dot_general | solution.py:118
  54.3 17.7 %all-to-all-done = bf16[8,9,128,64]{2,3,1,0:T(8,128)(2,1)S(1)} async-done(((bf16[8,9,128,64]{2,3,1,0:T(8,128)(2,1)}), bf16[8,9,128,64]{2,3,1,0:T(8,128)(2,1)S(1)}, u32[]{:S(2)}, u32[]{:S(2)}) %all-to-all-start) | async-done | bytes 1179680 | tf_op jit(solution)/shard_map/all_to_all | solution.py:110
  73.0 2.0 %convolution_bitcast_fusion = f32[9,8,128,64]{2,0,3,1:T(8,128)S(1)} fusion(bf16[8,8,128,64]{2,3,1,0:T(8,128)(2,1)S(1)} %slice.121, f32[8,9,8,1]{1,0,2,3:T(8,128)S(1)} %fusion.17), kind=kOutput, calls=%fused_computation.12 | convolution fusion | flops 56623104 | bytes 3410176 | tf_op jit(solution)/shard_map/hab,bhnp->ahnp/dot_general | solution.py:127
  75.0 2.0 %copy-done.3 = f32[9,8,128,64]{2,0,3,1:T(8,128)} copy-done((f32[9,8,128,64]{2,0,3,1:T(8,128)}, f32[9,8,128,64]{2,0,3,1:T(8,128)S(1)}, u32[]{:S(2)}) %copy-start.3) | copy-done | bytes 2359320
  77.9 9.8 %all-to-all-start.1 = ((f32[32,17,128]{2,1,0:T(8,128)}), f32[32,17,128]{2,1,0:T(8,128)}, u32[]{:S(2)}, u32[]{:S(2)}) async-start(f32[32,17,128]{2,1,0:T(8,128)} %pad_maximum_fusion.2), calls=%async_computation.1 | async-start | bytes 786432 | tf_op jit(solution)/shard_map/all_to_all | solution.py:145
  87.7 13.8 %all-to-all-done.1 = f32[32,17,128]{2,1,0:T(8,128)} async-done(((f32[32,17,128]{2,1,0:T(8,128)}), f32[32,17,128]{2,1,0:T(8,128)}, u32[]{:S(2)}, u32[]{:S(2)}) %all-to-all-start.1) | async-done | bytes 278560 | tf_op jit(solution)/shard_map/all_to_all | solution.py:145
  105.9 5.0 %all-to-all-start.2 = ((f32[32,16,128]{2,1,0:T(8,128)}), f32[32,16,128]{2,1,0:T(8,128)S(1)}, u32[]{:S(2)}, u32[]{:S(2)}) async-start(f32[32,16,128]{2,1,0:T(8,128)} %copy.132), calls=%async_computation.2 | async-start | bytes 524288 | tf_op jit(solution)/shard_map/all_to_all | solution.py:152
  111.0 10.4 %all-to-all-done.2 = f32[32,16,128]{2,1,0:T(8,128)S(1)} async-done(((f32[32,16,128]{2,1,0:T(8,128)}), f32[32,16,128]{2,1,0:T(8,128)S(1)}, u32[]{:S(2)}, u32[]{:S(2)}) %all-to-all-start.2) | async-done | bytes 262176 | tf_op jit(solution)/shard_map/all_to_all | solution.py:152
  121.4 1.9 %fusion.11 = bf16[8,8,128,64]{2,0,3,1:T(8,128)(2,1)S(1)} fusion(f32[9,8,128,64]{2,0,3,1:T(8,128)} %copy-done.3, f32[8,128,64]{1,2,0:T(8,128)S(1)} %bitcast.133, f32[8,8]{0,1:T(8,128)S(1)} %slice_exponential_fusion), kind=kLoop, calls=%fused_computation.20 | loop fusion | flops 1572864 | bytes 3408128 | tf_op jit(solution)/shard_map/convert_element_type | solution.py:156
  123.6 26.8 %all_to_all.20 = bf16[8,8,128,64]{2,3,1,0:T(8,128)(2,1)S(1)} all-to-all(bf16[8,8,128,64]{2,3,1,0:T(8,128)(2,1)S(1)} %copy.133), channel_id=1, replica_groups=mesh['seq'=32,'z'=8,'core'=2] {'z'}, dimensions={0} | all-to-all | bytes 2097152 | tf_op jit(solution)/shard_map/all_to_all | solution.py:156
  150.4 3.6 %fusion.7 = (bf16[64,128,64]{1,2,0:T(8,128)(2,1)}, bf16[64,128,64]{1,2,0:T(8,128)(2,1)}) fusion(bf16[8,8,128,64]{2,3,1,0:T(8,128)(2,1)S(1)} %all_to_all.20, f32[64]{0:T(128)S(1)} %get-tuple-element.48, pred[]{:T(512)S(6)} %eq.2, f32[65,128,64]{1,2,0:T(8,128)} %collective-permute-done, f32[128,128,64]{1,2,0:T(8,128)S(1)} %bitcast.124, s32[]{:T(128)S(6)} %select_n.102), kind=kLoop, calls=%fused_computation.16 | loop fusion | flops 4194304 | bytes 7340293 | tf_op jit(solution)/shard_map/convert_element_type | solution.py:160
  154.0 7.4 %collective-permute-start.1 = (bf16[64,128,64]{1,2,0:T(8,128)(2,1)}, bf16[64,128,64]{1,2,0:T(8,128)(2,1)}, u32[]{:S(2)}, u32[]{:S(2)}) collective-permute-start(bf16[64,128,64]{1,2,0:T(8,128)(2,1)} %get-tuple-element.36), channel_id=1, source_target_pairs={{0,1},{1,0},{2,3},{3,2},{4,5},{5,4},{6,7},{7,6},{8,9},{9,8},{10,11... | collective-permute-start | bytes 3145736 | tf_op jit(solution)/shard_map/ppermute | solution.py:12
  164.0 2.8 %maximum_select_fusion = bf16[128,128,64]{1,2,0:T(8,128)(2,1)S(1)} fusion(bf16[64,128,64]{1,2,0:T(8,128)(2,1)} %collective-permute-done.1, bf16[64,128,64]{1,2,0:T(8,128)(2,1)} %get-tuple-element.35, pred[]{:T(512)S(6)} %eq.2), kind=kLoop, calls=%fused_computation.21 | loop fusion | flops 3145728 | bytes 4194305 | tf_op jit(solution)/shard_map/jit(_where)/select_n | solution.py:163
  169.0 2.2 %fusion.4 = bf16[128,128,64]{0,2,1:T(8,128)(2,1)} fusion(f32[128,128,64]{0,2,1:T(8,128)S(1)} %copy-done.2, f32[8,16,64,128]{3,2,1,0:T(8,128)S(1)} %fusion.31, bf16[128,128,64]{0,2,1:T(8,128)(2,1)S(1)} %bitcast.121, f32[128]{0:T(128)S(1)} %add.76, f32[128,128]{0,1:T(8,128)S(1)} %copy-done.6), kind=kLoop, calls=%fused_computation.6 | loop fusion | flops 6291456 | bytes 12648960 | tf_op jit(solution)/shard_map/convert_element_type | solution.py:174
  171.2 4.1 %copy.137 = bf16[128,8192]{1,0:T(8,128)(2,1)} copy(bf16[128,8192]{0,1:T(8,128)(2,1)} %bitcast.125) | data formatting | bytes 4194304 | tf_op jit(solution)/shard_map/reshape | solution.py:174
  (85 shorter events, 27.1 us)
Async XLA Ops:
  2.2 28.3 %copy-start.5 = (f32[128,128]{1,0:T(8,128)}, f32[128,128]{1,0:T(8,128)S(1)}, u32[]{:S(2)}) copy-start(f32[128,128]{1,0:T(8,128)S(1)} %reduce_window_sum.11) | copy-start | bytes 196612
  9.3 2.6 %copy-start = (f32[8,16,64,128]{3,2,1,0:T(8,128)}, f32[8,16,64,128]{3,2,1,0:T(8,128)S(1)}, u32[]{:S(2)}) copy-start(f32[8,16,64,128]{3,2,1,0:T(8,128)S(1)} %fusion.9) | copy-start | bytes 12582916
  9.3 2.6 %copy-start.8 = (f32[8]{0:T(128)S(1)}, f32[8]{0:T(128)}, u32[]{:S(2)}) copy-start(f32[8]{0:T(128)} %param.15) | copy-start | bytes 100
  16.5 12.9 %collective-permute-start = (f32[65,128,64]{1,2,0:T(8,128)}, f32[65,128,64]{1,2,0:T(8,128)}, u32[]{:S(2)}, u32[]{:S(2)}) collective-permute-start(f32[65,128,64]{1,2,0:T(8,128)} %pad_maximum_fusion), channel_id=1, source_target_pairs={{0,1},{1,0},{2,3},{3,2},{4,5},{5,4},{6,7},{7,6},{8,9},{9,8},{10,11... | collective-permute-start | bytes 6389768 | tf_op jit(solution)/shard_map/ppermute | solution.py:12
  34.1 10.3 %copy-start.4 = (bf16[128,1024]{1,0:T(8,128)(2,1)S(1)}, bf16[128,1024]{1,0:T(8,128)(2,1)}, u32[]{:S(2)}) copy-start(bf16[128,1024]{1,0:T(8,128)(2,1)} %param.13) | copy-start | bytes 786436
  35.2 36.8 %all-to-all-start = ((bf16[8,9,128,64]{2,3,1,0:T(8,128)(2,1)}), bf16[8,9,128,64]{2,3,1,0:T(8,128)(2,1)S(1)}, u32[]{:S(2)}, u32[]{:S(2)}) async-start(bf16[8,9,128,64]{2,3,1,0:T(8,128)(2,1)} %pad_maximum_fusion.1), calls=%async_computation | async-start | bytes 2359296 | tf_op jit(solution)/shard_map/all_to_all | solution.py:110
  75.0 2.0 %copy-start.3 = (f32[9,8,128,64]{2,0,3,1:T(8,128)}, f32[9,8,128,64]{2,0,3,1:T(8,128)S(1)}, u32[]{:S(2)}) copy-start(f32[9,8,128,64]{2,0,3,1:T(8,128)S(1)} %convolution_bitcast_fusion) | copy-start | bytes 7077892
  77.9 23.6 %all-to-all-start.1 = ((f32[32,17,128]{2,1,0:T(8,128)}), f32[32,17,128]{2,1,0:T(8,128)}, u32[]{:S(2)}, u32[]{:S(2)}) async-start(f32[32,17,128]{2,1,0:T(8,128)} %pad_maximum_fusion.2), calls=%async_computation.1 | async-start | bytes 786432 | tf_op jit(solution)/shard_map/all_to_all | solution.py:145
  105.9 15.4 %all-to-all-start.2 = ((f32[32,16,128]{2,1,0:T(8,128)}), f32[32,16,128]{2,1,0:T(8,128)S(1)}, u32[]{:S(2)}, u32[]{:S(2)}) async-start(f32[32,16,128]{2,1,0:T(8,128)} %copy.132), calls=%async_computation.2 | async-start | bytes 524288 | tf_op jit(solution)/shard_map/all_to_all | solution.py:152
  123.3 27.1 %copy-start.1 = (f32[8,16,64,128]{3,2,1,0:T(8,128)S(1)}, f32[8,16,64,128]{3,2,1,0:T(8,128)}, u32[]{:S(2)}) copy-start(f32[8,16,64,128]{3,2,1,0:T(8,128)} %copy-done) | copy-start | bytes 12582916
  150.4 11.0 %copy-start.7 = (f32[128,128]{1,0:T(8,128)S(1)}, f32[128,128]{1,0:T(8,128)}, u32[]{:S(2)}) copy-start(f32[128,128]{1,0:T(8,128)} %get-tuple-element.39) | copy-start | bytes 196612
  154.0 10.0 %collective-permute-start.1 = (bf16[64,128,64]{1,2,0:T(8,128)(2,1)}, bf16[64,128,64]{1,2,0:T(8,128)(2,1)}, u32[]{:S(2)}, u32[]{:S(2)}) collective-permute-start(bf16[64,128,64]{1,2,0:T(8,128)(2,1)} %get-tuple-element.36), channel_id=1, source_target_pairs={{0,1},{1,0},{2,3},{3,2},{4,5},{5,4},{6,7},{7,6},{8,9},{9,8},{10,11... | collective-permute-start | bytes 3145736 | tf_op jit(solution)/shard_map/ppermute | solution.py:12
  166.8 2.2 %copy-start.2 = (f32[128,128,64]{0,2,1:T(8,128)S(1)}, f32[128,128,64]{0,2,1:T(8,128)}, u32[]{:S(2)}) copy-start(f32[128,128,64]{0,2,1:T(8,128)} %convolution_bitcast_fusion.1) | copy-start | bytes 12582916
  166.9 2.2 %copy-start.6 = (f32[128,128]{0,1:T(8,128)S(1)}, f32[128,128]{0,1:T(8,128)}, u32[]{:S(2)}) copy-start(f32[128,128]{0,1:T(8,128)} %copy.125) | copy-start | bytes 196612

commit v11 on v8

--- a/solution.py
+++ b/solution.py
@@ -77,7 +77,9 @@
     ).reshape(heads, state, width)
 
     own = lax.dynamic_slice_in_dim(update, c_idx * half, half, 0)
-    got = swap(lax.dynamic_slice_in_dim(update, (1 - c_idx) * half, half, 0))
+    got = swap(
+        lax.dynamic_slice_in_dim(update, (1 - c_idx) * half, half, 0).astype(bf16)
+    ).astype(f32)
     first = jnp.where(c_idx == 0, own, got)
     second = jnp.where(c_idx == 0, got, own)
     t_first = lax.dynamic_slice_in_dim(t_first, c_idx * half, half)
@@ -121,7 +123,7 @@
         "hab,bhnp->ahnp",
         decay_matrix(chip_totals, n_z + 1),
         rows[:, :quarter].astype(f32),
-        precision=lax.Precision.HIGHEST,
+        precision=lax.Precision.HIGH,
     )
     leads = jnp.einsum(
         "am,mh->ah", lower_mask(n_z + 1, n_z), chip_totals, precision=lax.Precision.HIGHEST
@@ -140,7 +142,7 @@
         "rab,brn->arn",
         decay_matrix(gathered[:, per, :per], n_seq),
         gathered[:, :per],
-        precision=lax.Precision.HIGHEST,
+        precision=lax.Precision.HIGH,
     )
     acc_s = lax.all_to_all(entering, "seq", 0, 0, tiled=True)
     acc_s = acc_s.reshape(quarter, width, state).transpose(0, 2, 1)

time: 167 us -> 167 us (level)
    unnamed x22 -> x26, local copies, waits for them, and re-layouts: 9.66 us -> 10.6 us
  transfers between devices with their start and end apart: 6 -> 6, of which waited for: 5 -> 5; matrix products, arithmetic and copies ran while one was open for 10% -> 15% of each run, Pallas kernels for 0% -> 0%
where the time goes in v11:
time: 167 us; the launch traced here: 166 us
  waiting for transfers between devices  44.3 us (27%)
  starting transfers between devices  37.6 us (23%)
  blocking collectives  26.9 us (16%)
  local copies, waits for them, and re-layouts  24.2 us (14%)
  other arithmetic  21.7 us (13%)
  matrix products  11.1 us (7%)
    all_to_all x1, blocking collectives, local(): back = lax.all_to_all(chip_in.astype(bf16), 'z', 0, 0, tiled=True)  26.9 us
    ppermute x3, starting transfers between devices, swap(): return lax.ppermute(value, 'core', [(0, 1), (1, 0)])  18.1 us
    all_to_all x1, waiting for transfers between devices, local(): rows = lax.all_to_all(message, 'z', 0, 0, tiled=True)  17.6 us
    all_to_all x1, waiting for transfers between devices, local(): gathered = lax.all_to_all(packed, 'seq', 0, 0, tiled=True)  13.8 us
    unnamed x26, local copies, waits for them, and re-layouts  10.6 us
    all_to_all x1, waiting for transfers between devices, local(): acc_s = lax.all_to_all(entering, 'seq', 0, 0, tiled=True)  10.4 us
    all_to_all x1, starting transfers between devices, local(): gathered = lax.all_to_all(packed, 'seq', 0, 0, tiled=True)  9.79 us
    all_to_all x1, starting transfers between devices, local(): acc_s = lax.all_to_all(entering, 'seq', 0, 0, tiled=True)  5.04 us
  transfers between devices with their start and end apart: 6, of which 5 were waited for; matrix products, arithmetic and copies ran while one was open for 15% of the time, Pallas kernels for 0%

profile of v11, /device:TPU:1, one launch (start us, length us, event | category | flops | bytes accessed | tf_op | source)
XLA Modules:
  0.0 166.2 jit_solution(14597231645628361245)
XLA Ops:
  1.6 8.8 %collective-permute-start = (f32[136]{0:T(256)S(1)}, f32[136]{0:T(256)S(1)}, u32[]{:S(2)}, u32[]{:S(2)}) collective-permute-start(f32[136]{0:T(256)S(1)} %pad_maximum_fusion.3), channel_id=1, source_target_pairs={{0,1},{1,0},{2,3},{3,2},{4,5},{5,4},{6,7},{7,6},{8,9},{9,8},{10,11... | collective-permute-start | bytes 1640 | tf_op jit(solution)/shard_map/ppermute | solution.py:12
  12.9 3.2 %copy.112 = bf16[128,8192]{0,1:T(8,128)(2,1)S(1)} copy(bf16[128,8192]{1,0:T(8,128)(2,1)} %param.6) | data formatting | bytes 4194304 | tf_op args[0]
  16.9 1.9 %copy-done = f32[8,16,64,128]{3,2,1,0:T(8,128)} copy-done((f32[8,16,64,128]{3,2,1,0:T(8,128)}, f32[8,16,64,128]{3,2,1,0:T(8,128)S(1)}, u32[]{:S(2)}) %copy-start) | copy-done | bytes 4194328
  20.0 1.9 %collective-permute-start.1 = (bf16[64,128,64]{1,2,0:T(8,128)(2,1)}, bf16[64,128,64]{1,2,0:T(8,128)(2,1)S(1)}, u32[]{:S(2)}, u32[]{:S(2)}) collective-permute-start(bf16[64,128,64]{1,2,0:T(8,128)(2,1)} %dynamic-slice_convert_fusion), channel_id=1, source_target_pairs={{0,1},{1,0},{2,3},{3,2},{4,5},{5,4},{6,7},{7,6},{8,9},{9,8},{10,11... | collective-permute-start | bytes 3145736 | tf_op jit(solution)/shard_map/ppermute | solution.py:12
  22.7 2.0 %collective-permute-done.1 = bf16[64,128,64]{1,2,0:T(8,128)(2,1)S(1)} collective-permute-done((bf16[64,128,64]{1,2,0:T(8,128)(2,1)}, bf16[64,128,64]{1,2,0:T(8,128)(2,1)S(1)}, u32[]{:S(2)}, u32[]{:S(2)}) %collective-permute-start.1) | collective-permute-done | bytes 1048608 | tf_op jit(solution)/shard_map/ppermute | solution.py:12
  24.7 2.4 %fusion.7 = bf16[64,128,64]{1,2,0:T(8,128)(2,1)S(1)} fusion(bf16[64,128,64]{1,2,0:T(8,128)(2,1)S(1)} %collective-permute-done.1, f32[128,128,64]{1,2,0:T(8,128)} %bitcast.110, s32[]{:T(128)S(6)} %select_n.101, f32[64]{0:T(128)S(1)} %get-tuple-element.24, pred[]{:T(512)S(6)} %eq.2), kind=kLoop, calls=%fused_computation.17 | loop fusion | flops 3145728 | bytes 4194565 | tf_op jit(solution)/shard_map/convert_element_type | solution.py:89
  28.3 4.7 %all-to-all-start = ((bf16[8,9,128,64]{2,3,1,0:T(8,128)(2,1)}), bf16[8,9,128,64]{2,3,1,0:T(8,128)(2,1)S(1)}, u32[]{:S(2)}, u32[]{:S(2)}) async-start(bf16[8,9,128,64]{2,3,1,0:T(8,128)(2,1)} %pad_maximum_fusion), calls=%async_computation | async-start | bytes 2359296 | tf_op jit(solution)/shard_map/all_to_all | solution.py:105
  33.0 1.6 copy.109
  35.9 1.6 copy.111
  38.8 3.6 %fusion.1 = bf16[128,128,128]{2,1,0:T(8,128)(2,1)S(1)} fusion(f32[128,128]{1,0:T(8,128)} %copy.111, f32[128,128]{1,0:T(8,128)} %copy.109, f32[8,128,128]{2,1,0:T(8,128)S(1)} %fusion.22, pred[128,128]{1,0:T(8,128)(4,1)S(1)} %iota_compare_fusion.2), kind=kLoop, calls=%fused_computation.2 | loop fusion | flops 12582912 | bytes 4866048 | tf_op jit(solution)/shard_map/convert_element_type | solution.py:112
  42.4 5.0 %convolution_bitcast_fusion.1 = f32[128,128,64]{0,2,1:T(8,128)} fusion(bf16[128,128,128]{2,1,0:T(8,128)(2,1)S(1)} %fusion.1, bf16[128,128,64]{0,2,1:T(8,128)(2,1)S(1)} %bitcast.107), kind=kOutput, calls=%fused_computation.15 | convolution fusion | flops 268435456 | bytes 10485760 | tf_op jit(solution)/shard_map/hts,shp->thp/dot_general | solution.py:113
  47.5 17.6 %all-to-all-done = bf16[8,9,128,64]{2,3,1,0:T(8,128)(2,1)S(1)} async-done(((bf16[8,9,128,64]{2,3,1,0:T(8,128)(2,1)}), bf16[8,9,128,64]{2,3,1,0:T(8,128)(2,1)S(1)}, u32[]{:S(2)}, u32[]{:S(2)}) %all-to-all-start) | async-done | bytes 1179680 | tf_op jit(solution)/shard_map/all_to_all | solution.py:105
  67.5 2.0 %copy-done.3 = f32[9,8,128,64]{2,0,3,1:T(8,128)} copy-done((f32[9,8,128,64]{2,0,3,1:T(8,128)}, f32[9,8,128,64]{2,0,3,1:T(8,128)S(1)}, u32[]{:S(2)}) %copy-start.3) | copy-done | bytes 2359320
  70.4 9.8 %all-to-all-start.1 = ((f32[32,17,128]{2,1,0:T(8,128)}), f32[32,17,128]{2,1,0:T(8,128)}, u32[]{:S(2)}, u32[]{:S(2)}) async-start(f32[32,17,128]{2,1,0:T(8,128)} %pad_maximum_fusion.1), calls=%async_computation.1 | async-start | bytes 786432 | tf_op jit(solution)/shard_map/all_to_all | solution.py:140
  80.2 13.8 %all-to-all-done.1 = f32[32,17,128]{2,1,0:T(8,128)} async-done(((f32[32,17,128]{2,1,0:T(8,128)}), f32[32,17,128]{2,1,0:T(8,128)}, u32[]{:S(2)}, u32[]{:S(2)}) %all-to-all-start.1) | async-done | bytes 278560 | tf_op jit(solution)/shard_map/all_to_all | solution.py:140
  98.3 5.0 %all-to-all-start.2 = ((f32[32,16,128]{2,1,0:T(8,128)}), f32[32,16,128]{2,1,0:T(8,128)S(1)}, u32[]{:S(2)}, u32[]{:S(2)}) async-start(f32[32,16,128]{2,1,0:T(8,128)} %copy.132), calls=%async_computation.2 | async-start | bytes 524288 | tf_op jit(solution)/shard_map/all_to_all | solution.py:147
  103.4 10.4 %all-to-all-done.2 = f32[32,16,128]{2,1,0:T(8,128)S(1)} async-done(((f32[32,16,128]{2,1,0:T(8,128)}), f32[32,16,128]{2,1,0:T(8,128)S(1)}, u32[]{:S(2)}, u32[]{:S(2)}) %all-to-all-start.2) | async-done | bytes 262176 | tf_op jit(solution)/shard_map/all_to_all | solution.py:147
  113.8 2.0 %fusion.13 = bf16[8,8,128,64]{2,0,3,1:T(8,128)(2,1)S(1)} fusion(f32[9,8,128,64]{2,0,3,1:T(8,128)} %copy-done.3, f32[8,128,64]{1,2,0:T(8,128)S(1)} %bitcast.120, f32[8,8]{0,1:T(8,128)S(1)} %slice_exponential_fusion), kind=kLoop, calls=%fused_computation.23 | loop fusion | flops 1572864 | bytes 3408128 | tf_op jit(solution)/shard_map/convert_element_type | solution.py:151
  116.0 26.9 %all_to_all.20 = bf16[8,8,128,64]{2,3,1,0:T(8,128)(2,1)S(1)} all-to-all(bf16[8,8,128,64]{2,3,1,0:T(8,128)(2,1)S(1)} %copy.133), channel_id=1, replica_groups=mesh['seq'=32,'z'=8,'core'=2] {'z'}, dimensions={0} | all-to-all | bytes 2097152 | tf_op jit(solution)/shard_map/all_to_all | solution.py:151
  142.9 2.2 %fusion.9 = (bf16[64,128,64]{1,2,0:T(8,128)(2,1)}, bf16[64,128,64]{1,2,0:T(8,128)(2,1)}) fusion(bf16[64,128,64]{1,2,0:T(8,128)(2,1)S(1)} %copy-done.5, f32[128,128,64]{1,2,0:T(8,128)S(1)} %bitcast.111, s32[]{:T(128)S(6)} %select_n.101, bf16[8,8,128,64]{2,3,1,0:T(8,128)(2,1)S(1)} %all_to_all.20, f32[64]{0:T(128)S(1)} %get-tuple-element.22, pred[]{:T(512)S(6)} %eq.2), kind=kLoop, calls=%fused_computation.19 | loop fusion | flops 4718592 | bytes 6291717 | tf_op jit(solution)/shard_map/convert_element_type | solution.py:155
  145.1 7.4 %collective-permute-start.2 = (bf16[64,128,64]{1,2,0:T(8,128)(2,1)}, bf16[64,128,64]{1,2,0:T(8,128)(2,1)}, u32[]{:S(2)}, u32[]{:S(2)}) collective-permute-start(bf16[64,128,64]{1,2,0:T(8,128)(2,1)} %get-tuple-element.12), channel_id=1, source_target_pairs={{0,1},{1,0},{2,3},{3,2},{4,5},{5,4},{6,7},{7,6},{8,9},{9,8},{10,11... | collective-permute-start | bytes 3145736 | tf_op jit(solution)/shard_map/ppermute | solution.py:12
  155.2 2.6 %maximum_select_fusion = bf16[128,128,64]{1,2,0:T(8,128)(2,1)S(1)} fusion(bf16[64,128,64]{1,2,0:T(8,128)(2,1)} %collective-permute-done.2, bf16[64,128,64]{1,2,0:T(8,128)(2,1)} %get-tuple-element.11, pred[]{:T(512)S(6)} %eq.2), kind=kLoop, calls=%fused_computation.24 | loop fusion | flops 3145728 | bytes 4194305 | tf_op jit(solution)/shard_map/jit(_where)/select_n | solution.py:158
  160.0 2.2 %fusion.4 = bf16[128,128,64]{0,2,1:T(8,128)(2,1)} fusion(f32[128,128,64]{0,2,1:T(8,128)S(1)} %copy-done.2, f32[8,16,64,128]{3,2,1,0:T(8,128)S(1)} %fusion.33, bf16[128,128,64]{0,2,1:T(8,128)(2,1)S(1)} %bitcast.108, f32[128]{0:T(128)S(1)} %add.70, f32[128,128]{0,1:T(8,128)S(1)} %copy-done.8), kind=kLoop, calls=%fused_computation.6 | loop fusion | flops 6291456 | bytes 12648960 | tf_op jit(solution)/shard_map/convert_element_type | solution.py:169
  162.1 4.1 %copy.137 = bf16[128,8192]{1,0:T(8,128)(2,1)} copy(bf16[128,8192]{0,1:T(8,128)(2,1)} %bitcast.112) | data formatting | bytes 4194304 | tf_op jit(solution)/shard_map/reshape | solution.py:169
  (86 shorter events, 23.2 us)
Async XLA Ops:
  0.9 21.5 %copy-start.7 = (f32[128,128]{1,0:T(8,128)}, f32[128,128]{1,0:T(8,128)S(1)}, u32[]{:S(2)}) copy-start(f32[128,128]{1,0:T(8,128)S(1)} %reduce_window_sum.11) | copy-start | bytes 196612
  1.6 20.5 %collective-permute-start = (f32[136]{0:T(256)S(1)}, f32[136]{0:T(256)S(1)}, u32[]{:S(2)}, u32[]{:S(2)}) collective-permute-start(f32[136]{0:T(256)S(1)} %pad_maximum_fusion.3), channel_id=1, source_target_pairs={{0,1},{1,0},{2,3},{3,2},{4,5},{5,4},{6,7},{7,6},{8,9},{9,8},{10,11... | collective-permute-start | bytes 1640 | tf_op jit(solution)/shard_map/ppermute | solution.py:12
  16.9 1.9 %copy-start = (f32[8,16,64,128]{3,2,1,0:T(8,128)}, f32[8,16,64,128]{3,2,1,0:T(8,128)S(1)}, u32[]{:S(2)}) copy-start(f32[8,16,64,128]{3,2,1,0:T(8,128)S(1)} %fusion.11) | copy-start | bytes 12582916
  16.9 5.0 %copy-start.10 = (f32[8]{0:T(128)S(1)}, f32[8]{0:T(128)}, u32[]{:S(2)}) copy-start(f32[8]{0:T(128)} %param.11) | copy-start | bytes 100
  20.0 4.8 %collective-permute-start.1 = (bf16[64,128,64]{1,2,0:T(8,128)(2,1)}, bf16[64,128,64]{1,2,0:T(8,128)(2,1)S(1)}, u32[]{:S(2)}, u32[]{:S(2)}) collective-permute-start(bf16[64,128,64]{1,2,0:T(8,128)(2,1)} %dynamic-slice_convert_fusion), channel_id=1, source_target_pairs={{0,1},{1,0},{2,3},{3,2},{4,5},{5,4},{6,7},{7,6},{8,9},{9,8},{10,11... | collective-permute-start | bytes 3145736 | tf_op jit(solution)/shard_map/ppermute | solution.py:12
  24.7 2.4 %copy-start.4 = (bf16[64,128,64]{1,2,0:T(8,128)(2,1)}, bf16[64,128,64]{1,2,0:T(8,128)(2,1)S(1)}, u32[]{:S(2)}) copy-start(bf16[64,128,64]{1,2,0:T(8,128)(2,1)S(1)} %collective-permute-done.1) | copy-start | bytes 3145732
  27.2 10.4 %copy-start.6 = (bf16[128,1024]{1,0:T(8,128)(2,1)S(1)}, bf16[128,1024]{1,0:T(8,128)(2,1)}, u32[]{:S(2)}) copy-start(bf16[128,1024]{1,0:T(8,128)(2,1)} %param.9) | copy-start | bytes 786436
  28.3 36.7 %all-to-all-start = ((bf16[8,9,128,64]{2,3,1,0:T(8,128)(2,1)}), bf16[8,9,128,64]{2,3,1,0:T(8,128)(2,1)S(1)}, u32[]{:S(2)}, u32[]{:S(2)}) async-start(bf16[8,9,128,64]{2,3,1,0:T(8,128)(2,1)} %pad_maximum_fusion), calls=%async_computation | async-start | bytes 2359296 | tf_op jit(solution)/shard_map/all_to_all | solution.py:105
  67.5 2.0 %copy-start.3 = (f32[9,8,128,64]{2,0,3,1:T(8,128)}, f32[9,8,128,64]{2,0,3,1:T(8,128)S(1)}, u32[]{:S(2)}) copy-start(f32[9,8,128,64]{2,0,3,1:T(8,128)S(1)} %convolution_bitcast_fusion) | copy-start | bytes 7077892
  70.4 23.6 %all-to-all-start.1 = ((f32[32,17,128]{2,1,0:T(8,128)}), f32[32,17,128]{2,1,0:T(8,128)}, u32[]{:S(2)}, u32[]{:S(2)}) async-start(f32[32,17,128]{2,1,0:T(8,128)} %pad_maximum_fusion.1), calls=%async_computation.1 | async-start | bytes 786432 | tf_op jit(solution)/shard_map/all_to_all | solution.py:140
  98.3 15.4 %all-to-all-start.2 = ((f32[32,16,128]{2,1,0:T(8,128)}), f32[32,16,128]{2,1,0:T(8,128)S(1)}, u32[]{:S(2)}, u32[]{:S(2)}) async-start(f32[32,16,128]{2,1,0:T(8,128)} %copy.132), calls=%async_computation.2 | async-start | bytes 524288 | tf_op jit(solution)/shard_map/all_to_all | solution.py:147
  113.8 29.1 %copy-start.5 = (bf16[64,128,64]{1,2,0:T(8,128)(2,1)S(1)}, bf16[64,128,64]{1,2,0:T(8,128)(2,1)}, u32[]{:S(2)}) copy-start(bf16[64,128,64]{1,2,0:T(8,128)(2,1)} %copy-done.4) | copy-start | bytes 3145732
  115.8 27.1 %copy-start.1 = (f32[8,16,64,128]{3,2,1,0:T(8,128)S(1)}, f32[8,16,64,128]{3,2,1,0:T(8,128)}, u32[]{:S(2)}) copy-start(f32[8,16,64,128]{3,2,1,0:T(8,128)} %copy-done) | copy-start | bytes 12582916
  142.9 9.7 %copy-start.9 = (f32[128,128]{1,0:T(8,128)S(1)}, f32[128,128]{1,0:T(8,128)}, u32[]{:S(2)}) copy-start(f32[128,128]{1,0:T(8,128)} %get-tuple-element.15) | copy-start | bytes 196612
  145.1 10.0 %collective-permute-start.2 = (bf16[64,128,64]{1,2,0:T(8,128)(2,1)}, bf16[64,128,64]{1,2,0:T(8,128)(2,1)}, u32[]{:S(2)}, u32[]{:S(2)}) collective-permute-start(bf16[64,128,64]{1,2,0:T(8,128)(2,1)} %get-tuple-element.12), channel_id=1, source_target_pairs={{0,1},{1,0},{2,3},{3,2},{4,5},{5,4},{6,7},{7,6},{8,9},{9,8},{10,11... | collective-permute-start | bytes 3145736 | tf_op jit(solution)/shard_map/ppermute | solution.py:12
  157.8 2.2 %copy-start.2 = (f32[128,128,64]{0,2,1:T(8,128)S(1)}, f32[128,128,64]{0,2,1:T(8,128)}, u32[]{:S(2)}) copy-start(f32[128,128,64]{0,2,1:T(8,128)} %convolution_bitcast_fusion.1) | copy-start | bytes 12582916
  157.8 2.2 %copy-start.8 = (f32[128,128]{0,1:T(8,128)S(1)}, f32[128,128]{0,1:T(8,128)}, u32[]{:S(2)}) copy-start(f32[128,128]{0,1:T(8,128)} %copy.125) | copy-start | bytes 196612

commit v12 on v8

--- a/solution.py
+++ b/solution.py
@@ -135,6 +135,7 @@
     packed = jnp.concatenate(
         [chunks, jnp.pad(row_totals, ((0, 0), (0, state - per)))[:, None, :]], axis=1
     )
+    packed = jnp.pad(packed, ((0, 0), (0, -(per + 1) % 8), (0, 0)))
     gathered = lax.all_to_all(packed, "seq", 0, 0, tiled=True)
     entering = jnp.einsum(
         "rab,brn->arn",

time: 167 us -> 167 us (level)
  no operation moved by 1% of the time
where the time goes in v12:
time: 167 us; the launch traced here: 165 us
  waiting for transfers between devices  44 us (26%)
  starting transfers between devices  36 us (22%)
  blocking collectives  26.8 us (16%)
  local copies, waits for them, and re-layouts  23.7 us (14%)
  other arithmetic  22.7 us (14%)
  matrix products  11.8 us (7%)
    all_to_all x1, blocking collectives, local(): back = lax.all_to_all(chip_in.astype(bf16), 'z', 0, 0, tiled=True)  26.8 us
    all_to_all x1, waiting for transfers between devices, local(): rows = lax.all_to_all(message, 'z', 0, 0, tiled=True)  17.6 us
    ppermute x3, starting transfers between devices, swap(): return lax.ppermute(value, 'core', [(0, 1), (1, 0)])  16.5 us
    all_to_all x1, waiting for transfers between devices, local(): gathered = lax.all_to_all(packed, 'seq', 0, 0, tiled=True)  13.8 us
    all_to_all x1, waiting for transfers between devices, local(): acc_s = lax.all_to_all(entering, 'seq', 0, 0, tiled=True)  10.4 us
    all_to_all x1, starting transfers between devices, local(): gathered = lax.all_to_all(packed, 'seq', 0, 0, tiled=True)  9.78 us
    unnamed x22, local copies, waits for them, and re-layouts  9.66 us
    all_to_all x1, starting transfers between devices, local(): acc_s = lax.all_to_all(entering, 'seq', 0, 0, tiled=True)  5.04 us
  transfers between devices with their start and end apart: 6, of which 5 were waited for; matrix products, arithmetic and copies ran while one was open for 10% of the time, Pallas kernels for 0%

profile of v12, /device:TPU:1, one launch (start us, length us, event | category | flops | bytes accessed | tf_op | source)
XLA Modules:
  0.0 165.5 jit_solution(5356429337143800479)
XLA Ops:
  3.5 3.2 %copy.112 = bf16[128,8192]{0,1:T(8,128)(2,1)S(1)} copy(bf16[128,8192]{1,0:T(8,128)(2,1)} %param.6) | data formatting | bytes 4194304 | tf_op args[0]
  7.4 1.6 constant_dynamic-slice_fusion
  10.0 8.8 %collective-permute-start.1 = (f32[64,128,64]{1,2,0:T(8,128)}, f32[64,128,64]{1,2,0:T(8,128)}, u32[]{:S(2)}, u32[]{:S(2)}) collective-permute-start(f32[64,128,64]{1,2,0:T(8,128)} %constant_dynamic-slice_fusion), channel_id=1, source_target_pairs={{0,1},{1,0},{2,3},{3,2},{4,5},{5,4},{6,7},{7,6},{8,9},{9,8},{10,11... | collective-permute-start | bytes 6291464 | tf_op jit(solution)/shard_map/ppermute | solution.py:12
  18.8 1.9 %collective-permute-start = (f32[136]{0:T(256)S(1)}, f32[136]{0:T(256)S(1)}, u32[]{:S(2)}, u32[]{:S(2)}) collective-permute-start(f32[136]{0:T(256)S(1)} %pad_maximum_fusion.2), channel_id=1, source_target_pairs={{0,1},{1,0},{2,3},{3,2},{4,5},{5,4},{6,7},{7,6},{8,9},{9,8},{10,11... | collective-permute-start | bytes 1640 | tf_op jit(solution)/shard_map/ppermute | solution.py:12
  21.0 1.6 collective-permute-done
  23.2 2.6 %add_convert_fusion = bf16[64,128,64]{1,2,0:T(8,128)(2,1)S(1)} fusion(f32[64,128,64]{1,2,0:T(8,128)} %collective-permute-done.1, f32[128,128,64]{1,2,0:T(8,128)} %bitcast.110, s32[]{:T(128)S(6)} %select_n.101, f32[64]{0:T(128)S(1)} %get-tuple-element.24, pred[]{:T(512)S(6)} %eq.2), kind=kLoop, calls=%fused_computation.21 | loop fusion | flops 2621440 | bytes 5243141 | tf_op jit(solution)/shard_map/convert_element_type | solution.py:87
  27.0 4.7 %all-to-all-start = ((bf16[8,9,128,64]{2,3,1,0:T(8,128)(2,1)}), bf16[8,9,128,64]{2,3,1,0:T(8,128)(2,1)S(1)}, u32[]{:S(2)}, u32[]{:S(2)}) async-start(bf16[8,9,128,64]{2,3,1,0:T(8,128)(2,1)} %pad_maximum_fusion), calls=%async_computation | async-start | bytes 2359296 | tf_op jit(solution)/shard_map/all_to_all | solution.py:103
  34.6 1.6 copy.111
  37.5 3.6 %fusion.1 = bf16[128,128,128]{2,1,0:T(8,128)(2,1)S(1)} fusion(f32[128,128]{1,0:T(8,128)} %copy.111, f32[128,128]{1,0:T(8,128)} %copy.109, f32[8,128,128]{2,1,0:T(8,128)S(1)} %fusion.20, pred[128,128]{1,0:T(8,128)(4,1)S(1)} %iota_compare_fusion.3), kind=kLoop, calls=%fused_computation.2 | loop fusion | flops 12582912 | bytes 4866048 | tf_op jit(solution)/shard_map/convert_element_type | solution.py:110
  41.1 5.0 %convolution_bitcast_fusion.1 = f32[128,128,64]{0,2,1:T(8,128)} fusion(bf16[128,128,128]{2,1,0:T(8,128)(2,1)S(1)} %fusion.1, bf16[128,128,64]{0,2,1:T(8,128)(2,1)S(1)} %bitcast.107), kind=kOutput, calls=%fused_computation.13 | convolution fusion | flops 268435456 | bytes 10485760 | tf_op jit(solution)/shard_map/hts,shp->thp/dot_general | solution.py:111
  46.1 17.6 %all-to-all-done = bf16[8,9,128,64]{2,3,1,0:T(8,128)(2,1)S(1)} async-done(((bf16[8,9,128,64]{2,3,1,0:T(8,128)(2,1)}), bf16[8,9,128,64]{2,3,1,0:T(8,128)(2,1)S(1)}, u32[]{:S(2)}, u32[]{:S(2)}) %all-to-all-start) | async-done | bytes 1179680 | tf_op jit(solution)/shard_map/all_to_all | solution.py:103
  64.8 2.1 %convolution_bitcast_fusion = f32[9,8,128,64]{2,0,3,1:T(8,128)S(1)} fusion(bf16[8,8,128,64]{2,3,1,0:T(8,128)(2,1)S(1)} %slice.87, f32[8,9,8,1]{1,0,2,3:T(8,128)S(1)} %fusion.17), kind=kOutput, calls=%fused_computation.12 | convolution fusion | flops 56623104 | bytes 3410176 | tf_op jit(solution)/shard_map/hab,bhnp->ahnp/dot_general | solution.py:120
  66.8 2.0 %copy-done.3 = f32[9,8,128,64]{2,0,3,1:T(8,128)} copy-done((f32[9,8,128,64]{2,0,3,1:T(8,128)}, f32[9,8,128,64]{2,0,3,1:T(8,128)S(1)}, u32[]{:S(2)}) %copy-start.3) | copy-done | bytes 2359320
  69.7 9.8 %all-to-all-start.1 = ((f32[32,24,128]{2,1,0:T(8,128)}), f32[32,24,128]{2,1,0:T(8,128)}, u32[]{:S(2)}, u32[]{:S(2)}) async-start(f32[32,24,128]{2,1,0:T(8,128)} %select_maximum_fusion), calls=%async_computation.1 | async-start | bytes 786432 | tf_op jit(solution)/shard_map/all_to_all | solution.py:139
  79.5 13.8 %all-to-all-done.1 = f32[32,24,128]{2,1,0:T(8,128)} async-done(((f32[32,24,128]{2,1,0:T(8,128)}), f32[32,24,128]{2,1,0:T(8,128)}, u32[]{:S(2)}, u32[]{:S(2)}) %all-to-all-start.1) | async-done | bytes 393248 | tf_op jit(solution)/shard_map/all_to_all | solution.py:139
  97.7 5.0 %all-to-all-start.2 = ((f32[32,16,128]{2,1,0:T(8,128)}), f32[32,16,128]{2,1,0:T(8,128)S(1)}, u32[]{:S(2)}, u32[]{:S(2)}) async-start(f32[32,16,128]{2,1,0:T(8,128)} %copy.132), calls=%async_computation.2 | async-start | bytes 524288 | tf_op jit(solution)/shard_map/all_to_all | solution.py:146
  102.8 10.4 %all-to-all-done.2 = f32[32,16,128]{2,1,0:T(8,128)S(1)} async-done(((f32[32,16,128]{2,1,0:T(8,128)}), f32[32,16,128]{2,1,0:T(8,128)S(1)}, u32[]{:S(2)}, u32[]{:S(2)}) %all-to-all-start.2) | async-done | bytes 262176 | tf_op jit(solution)/shard_map/all_to_all | solution.py:146
  113.2 1.9 %fusion.11 = bf16[8,8,128,64]{2,0,3,1:T(8,128)(2,1)S(1)} fusion(f32[9,8,128,64]{2,0,3,1:T(8,128)} %copy-done.3, f32[8,128,64]{1,2,0:T(8,128)S(1)} %bitcast.120, f32[8,8]{0,1:T(8,128)S(1)} %slice_exponential_fusion), kind=kLoop, calls=%fused_computation.19 | loop fusion | flops 1572864 | bytes 3408128 | tf_op jit(solution)/shard_map/convert_element_type | solution.py:150
  115.4 26.8 %all_to_all.20 = bf16[8,8,128,64]{2,3,1,0:T(8,128)(2,1)S(1)} all-to-all(bf16[8,8,128,64]{2,3,1,0:T(8,128)(2,1)S(1)} %copy.133), channel_id=1, replica_groups=mesh['seq'=32,'z'=8,'core'=2] {'z'}, dimensions={0} | all-to-all | bytes 2097152 | tf_op jit(solution)/shard_map/all_to_all | solution.py:150
  142.2 3.6 %fusion.7 = (bf16[64,128,64]{1,2,0:T(8,128)(2,1)}, bf16[64,128,64]{1,2,0:T(8,128)(2,1)}) fusion(bf16[8,8,128,64]{2,3,1,0:T(8,128)(2,1)S(1)} %all_to_all.20, f32[64]{0:T(128)S(1)} %get-tuple-element.22, pred[]{:T(512)S(6)} %eq.2, f32[64,128,64]{1,2,0:T(8,128)} %collective-permute-done.1, f32[128,128,64]{1,2,0:T(8,128)S(1)} %bitcast.111, s32[]{:T(128)S(6)} %select_n.101), kind=kLoop, calls=%fused_computation.15 | loop fusion | flops 4194304 | bytes 7340293 | tf_op jit(solution)/shard_map/convert_element_type | solution.py:154
  145.8 5.8 %collective-permute-start.2 = (bf16[64,128,64]{1,2,0:T(8,128)(2,1)}, bf16[64,128,64]{1,2,0:T(8,128)(2,1)}, u32[]{:S(2)}, u32[]{:S(2)}) collective-permute-start(bf16[64,128,64]{1,2,0:T(8,128)(2,1)} %get-tuple-element.12), channel_id=1, source_target_pairs={{0,1},{1,0},{2,3},{3,2},{4,5},{5,4},{6,7},{7,6},{8,9},{9,8},{10,11... | collective-permute-start | bytes 3145736 | tf_op jit(solution)/shard_map/ppermute | solution.py:12
  154.3 2.8 %maximum_select_fusion = bf16[128,128,64]{1,2,0:T(8,128)(2,1)S(1)} fusion(bf16[64,128,64]{1,2,0:T(8,128)(2,1)} %collective-permute-done.2, bf16[64,128,64]{1,2,0:T(8,128)(2,1)} %get-tuple-element.11, pred[]{:T(512)S(6)} %eq.2), kind=kLoop, calls=%fused_computation.20 | loop fusion | flops 3145728 | bytes 4194305 | tf_op jit(solution)/shard_map/jit(_where)/select_n | solution.py:157
  159.2 2.2 %fusion.4 = bf16[128,128,64]{0,2,1:T(8,128)(2,1)} fusion(f32[128,128,64]{0,2,1:T(8,128)S(1)} %copy-done.2, f32[8,16,64,128]{3,2,1,0:T(8,128)S(1)} %fusion.31, bf16[128,128,64]{0,2,1:T(8,128)(2,1)S(1)} %bitcast.108, f32[128]{0:T(128)S(1)} %add.72, f32[128,128]{0,1:T(8,128)S(1)} %copy-done.6), kind=kLoop, calls=%fused_computation.6 | loop fusion | flops 6291456 | bytes 12648960 | tf_op jit(solution)/shard_map/convert_element_type | solution.py:168
  161.4 4.1 %copy.137 = bf16[128,8192]{1,0:T(8,128)(2,1)} copy(bf16[128,8192]{0,1:T(8,128)(2,1)} %bitcast.112) | data formatting | bytes 4194304 | tf_op jit(solution)/shard_map/reshape | solution.py:168
  (82 shorter events, 22.6 us)
Async XLA Ops:
  0.9 22.0 %copy-start.5 = (f32[128,128]{1,0:T(8,128)}, f32[128,128]{1,0:T(8,128)S(1)}, u32[]{:S(2)}) copy-start(f32[128,128]{1,0:T(8,128)S(1)} %reduce_window_sum.11) | copy-start | bytes 196612
  7.4 2.6 %copy-start = (f32[8,16,64,128]{3,2,1,0:T(8,128)}, f32[8,16,64,128]{3,2,1,0:T(8,128)S(1)}, u32[]{:S(2)}) copy-start(f32[8,16,64,128]{3,2,1,0:T(8,128)S(1)} %fusion.9) | copy-start | bytes 12582916
  7.4 11.4 %copy-start.8 = (f32[8]{0:T(128)S(1)}, f32[8]{0:T(128)}, u32[]{:S(2)}) copy-start(f32[8]{0:T(128)} %param.11) | copy-start | bytes 100
  10.0 13.2 %collective-permute-start.1 = (f32[64,128,64]{1,2,0:T(8,128)}, f32[64,128,64]{1,2,0:T(8,128)}, u32[]{:S(2)}, u32[]{:S(2)}) collective-permute-start(f32[64,128,64]{1,2,0:T(8,128)} %constant_dynamic-slice_fusion), channel_id=1, source_target_pairs={{0,1},{1,0},{2,3},{3,2},{4,5},{5,4},{6,7},{7,6},{8,9},{9,8},{10,11... | collective-permute-start | bytes 6291464 | tf_op jit(solution)/shard_map/ppermute | solution.py:12
  18.8 3.7 %collective-permute-start = (f32[136]{0:T(256)S(1)}, f32[136]{0:T(256)S(1)}, u32[]{:S(2)}, u32[]{:S(2)}) collective-permute-start(f32[136]{0:T(256)S(1)} %pad_maximum_fusion.2), channel_id=1, source_target_pairs={{0,1},{1,0},{2,3},{3,2},{4,5},{5,4},{6,7},{7,6},{8,9},{9,8},{10,11... | collective-permute-start | bytes 1640 | tf_op jit(solution)/shard_map/ppermute | solution.py:12
  25.9 10.3 %copy-start.4 = (bf16[128,1024]{1,0:T(8,128)(2,1)S(1)}, bf16[128,1024]{1,0:T(8,128)(2,1)}, u32[]{:S(2)}) copy-start(bf16[128,1024]{1,0:T(8,128)(2,1)} %param.9) | copy-start | bytes 786436
  27.0 36.8 %all-to-all-start = ((bf16[8,9,128,64]{2,3,1,0:T(8,128)(2,1)}), bf16[8,9,128,64]{2,3,1,0:T(8,128)(2,1)S(1)}, u32[]{:S(2)}, u32[]{:S(2)}) async-start(bf16[8,9,128,64]{2,3,1,0:T(8,128)(2,1)} %pad_maximum_fusion), calls=%async_computation | async-start | bytes 2359296 | tf_op jit(solution)/shard_map/all_to_all | solution.py:103
  66.8 2.0 %copy-start.3 = (f32[9,8,128,64]{2,0,3,1:T(8,128)}, f32[9,8,128,64]{2,0,3,1:T(8,128)S(1)}, u32[]{:S(2)}) copy-start(f32[9,8,128,64]{2,0,3,1:T(8,128)S(1)} %convolution_bitcast_fusion) | copy-start | bytes 7077892
  69.7 23.6 %all-to-all-start.1 = ((f32[32,24,128]{2,1,0:T(8,128)}), f32[32,24,128]{2,1,0:T(8,128)}, u32[]{:S(2)}, u32[]{:S(2)}) async-start(f32[32,24,128]{2,1,0:T(8,128)} %select_maximum_fusion), calls=%async_computation.1 | async-start | bytes 786432 | tf_op jit(solution)/shard_map/all_to_all | solution.py:139
  97.7 15.5 %all-to-all-start.2 = ((f32[32,16,128]{2,1,0:T(8,128)}), f32[32,16,128]{2,1,0:T(8,128)S(1)}, u32[]{:S(2)}, u32[]{:S(2)}) async-start(f32[32,16,128]{2,1,0:T(8,128)} %copy.132), calls=%async_computation.2 | async-start | bytes 524288 | tf_op jit(solution)/shard_map/all_to_all | solution.py:146
  115.1 27.1 %copy-start.1 = (f32[8,16,64,128]{3,2,1,0:T(8,128)S(1)}, f32[8,16,64,128]{3,2,1,0:T(8,128)}, u32[]{:S(2)}) copy-start(f32[8,16,64,128]{3,2,1,0:T(8,128)} %copy-done) | copy-start | bytes 12582916
  142.2 9.4 %copy-start.7 = (f32[128,128]{1,0:T(8,128)S(1)}, f32[128,128]{1,0:T(8,128)}, u32[]{:S(2)}) copy-start(f32[128,128]{1,0:T(8,128)} %get-tuple-element.15) | copy-start | bytes 196612
  145.8 8.4 %collective-permute-start.2 = (bf16[64,128,64]{1,2,0:T(8,128)(2,1)}, bf16[64,128,64]{1,2,0:T(8,128)(2,1)}, u32[]{:S(2)}, u32[]{:S(2)}) collective-permute-start(bf16[64,128,64]{1,2,0:T(8,128)(2,1)} %get-tuple-element.12), channel_id=1, source_target_pairs={{0,1},{1,0},{2,3},{3,2},{4,5},{5,4},{6,7},{7,6},{8,9},{9,8},{10,11... | collective-permute-start | bytes 3145736 | tf_op jit(solution)/shard_map/ppermute | solution.py:12
  157.0 2.2 %copy-start.2 = (f32[128,128,64]{0,2,1:T(8,128)S(1)}, f32[128,128,64]{0,2,1:T(8,128)}, u32[]{:S(2)}) copy-start(f32[128,128,64]{0,2,1:T(8,128)} %convolution_bitcast_fusion.1) | copy-start | bytes 12582916
  157.0 2.2 %copy-start.6 = (f32[128,128]{0,1:T(8,128)S(1)}, f32[128,128]{0,1:T(8,128)}, u32[]{:S(2)}) copy-start(f32[128,128]{0,1:T(8,128)} %copy.125) | copy-start | bytes 196612

commit v13 on v12

--- a/solution.py
+++ b/solution.py
@@ -71,13 +71,19 @@
 
     factor = jnp.exp(total[None, :] - within) * step
     scaled = (x * factor[..., None]).astype(bf16)
-    update = jnp.einsum(
-        "sgn,sghp->ghnp", b, scaled.reshape(tokens, G, per_group, width),
-        preferred_element_type=f32,
-    ).reshape(heads, state, width)
+    scaled = scaled.reshape(tokens, G, per_group, width)
+    groups = G // n_core
 
-    own = lax.dynamic_slice_in_dim(update, c_idx * half, half, 0)
-    got = swap(lax.dynamic_slice_in_dim(update, (1 - c_idx) * half, half, 0))
+    def update_of(core):
+        return jnp.einsum(
+            "sgn,sghp->ghnp",
+            lax.dynamic_slice_in_dim(b, core * groups, groups, 1),
+            lax.dynamic_slice_in_dim(scaled, core * groups, groups, 1),
+            preferred_element_type=f32,
+        ).reshape(half, state, width)
+
+    own = update_of(c_idx)
+    got = swap(update_of(1 - c_idx))
     first = jnp.where(c_idx == 0, own, got)
     second = jnp.where(c_idx == 0, got, own)
     t_first = lax.dynamic_slice_in_dim(t_first, c_idx * half, half)

time: 167 us -> 170 us (1.018)
  waiting for transfers between devices: 44 us -> 39.2 us
  local copies, waits for them, and re-layouts: 23.7 us -> 26.8 us
  matrix products: 11.8 us -> 14.4 us
  other arithmetic: 22.7 us -> 24.8 us
    convert_element_type x0 -> x1, local copies, waits for them, and re-layouts: none -> 4.31 us  [local(): scaled = (x * factor[..., None]).astype(bf16)]
    all_to_all x1, waiting for transfers between devices: 17.6 us -> 14.5 us  [local(): rows = lax.all_to_all(message, 'z', 0, 0, tiled=True)]
    convert_element_type x0 -> x1, other arithmetic: none -> 2.83 us  [local(): scaled = (x * factor[..., None]).astype(bf16)]
    dot_general x1 -> x2, matrix products: 0.7 us -> 3.42 us  [update_of(): jnp.einsum('sgn,sghp->ghnp', lax.dynamic_slice_in_dim(b, core * groups, g...]
  transfers between devices with their start and end apart: 6 -> 6, of which waited for: 5 -> 4; matrix products, arithmetic and copies ran while one was open for 10% -> 13% of each run, Pallas kernels for 0% -> 0%
where the time goes in v13:
time: 170 us; the launch traced here: 169 us
  waiting for transfers between devices  39.2 us (23%)
  starting transfers between devices  36.2 us (21%)
  local copies, waits for them, and re-layouts  26.8 us (16%)
  blocking collectives  26.8 us (16%)
  other arithmetic  24.8 us (15%)
  matrix products  14.4 us (8%)
    all_to_all x1, blocking collectives, local(): back = lax.all_to_all(chip_in.astype(bf16), 'z', 0, 0, tiled=True)  26.8 us
    ppermute x3, starting transfers between devices, swap(): return lax.ppermute(value, 'core', [(0, 1), (1, 0)])  16.7 us
    all_to_all x1, waiting for transfers between devices, local(): rows = lax.all_to_all(message, 'z', 0, 0, tiled=True)  14.5 us
    all_to_all x1, waiting for transfers between devices, local(): gathered = lax.all_to_all(packed, 'seq', 0, 0, tiled=True)  13.8 us
    all_to_all x1, waiting for transfers between devices, local(): acc_s = lax.all_to_all(entering, 'seq', 0, 0, tiled=True)  10.4 us
    unnamed x22, local copies, waits for them, and re-layouts  10.1 us
    all_to_all x1, starting transfers between devices, local(): gathered = lax.all_to_all(packed, 'seq', 0, 0, tiled=True)  9.78 us
    all_to_all x1, starting transfers between devices, local(): acc_s = lax.all_to_all(entering, 'seq', 0, 0, tiled=True)  5.04 us
  transfers between devices with their start and end apart: 6, of which 4 were waited for; matrix products, arithmetic and copies ran while one was open for 13% of the time, Pallas kernels for 0%

profile of v13, /device:TPU:1, one launch (start us, length us, event | category | flops | bytes accessed | tf_op | source)
XLA Modules:
  0.0 168.7 jit_solution(985003941762374741)
XLA Ops:
  3.6 4.3 %copy.118 = f32[128,8192]{0,1:T(8,128)} copy(bf16[128,8192]{1,0:T(8,128)(2,1)} %param.6) | data formatting | bytes 6291456 | tf_op jit(solution)/shard_map/convert_element_type | solution.py:73
  7.9 2.8 %multiply_convert_fusion = bf16[128,8,16,64]{0,3,2,1:T(8,128)(2,1)S(1)} fusion(f32[128,8,16,64]{0,3,2,1:T(8,128)} %bitcast.125, f32[128,8,16]{0,2,1:T(8,128)S(1)} %bitcast.137), kind=kLoop, calls=%fused_computation.7 | loop fusion | flops 2097152 | bytes 6356992 | tf_op jit(solution)/shard_map/convert_element_type | solution.py:73
  12.1 1.8 %fusion.17 = f32[4,16,64,128]{3,2,1,0:T(8,128)} fusion(bf16[128,8,16,64]{0,3,2,1:T(8,128)(2,1)S(1)} %multiply_convert_fusion, s32[]{:T(128)S(6)} %select_n.108, bf16[128,8,128]{0,2,1:T(8,128)(2,1)S(1)} %bitcast.129), kind=kOutput, calls=%fused_computation.33 | convolution fusion | flops 134217728 | bytes 3277824 | tf_op jit(solution)/shard_map/sgn,sghp->ghnp/dot_general | solution.py:78
  13.8 8.8 %collective-permute-start.1 = (f32[64,128,64]{1,2,0:T(8,128)}, f32[64,128,64]{1,2,0:T(8,128)}, u32[]{:S(2)}, u32[]{:S(2)}) collective-permute-start(f32[64,128,64]{1,2,0:T(8,128)} %bitcast.16), channel_id=1, source_target_pairs={{0,1},{1,0},{2,3},{3,2},{4,5},{5,4},{6,7},{7,6},{8,9},{9,8},{10,11... | collective-permute-start | bytes 6291464 | tf_op jit(solution)/shard_map/ppermute | solution.py:12
  22.6 1.9 %collective-permute-start = (f32[136]{0:T(256)S(1)}, f32[136]{0:T(256)S(1)}, u32[]{:S(2)}, u32[]{:S(2)}) collective-permute-start(f32[136]{0:T(256)S(1)} %pad_maximum_fusion.2), channel_id=1, source_target_pairs={{0,1},{1,0},{2,3},{3,2},{4,5},{5,4},{6,7},{7,6},{8,9},{9,8},{10,11... | collective-permute-start | bytes 1640 | tf_op jit(solution)/shard_map/ppermute | solution.py:12
  27.1 2.0 %fusion.10 = bf16[64,128,64]{1,2,0:T(8,128)(2,1)S(1)} fusion(f32[64,128,64]{1,2,0:T(8,128)} %collective-permute-done.1, f32[4,16,64,128]{3,2,1,0:T(8,128)S(1)} %fusion.19, f32[64]{0:T(128)S(1)} %get-tuple-element.24, pred[]{:T(512)S(6)} %eq.2), kind=kLoop, calls=%fused_computation.22 | loop fusion | flops 2621440 | bytes 5243137 | tf_op jit(solution)/shard_map/convert_element_type | solution.py:93
  30.2 4.7 %all-to-all-start = ((bf16[8,9,128,64]{2,3,1,0:T(8,128)(2,1)}), bf16[8,9,128,64]{2,3,1,0:T(8,128)(2,1)S(1)}, u32[]{:S(2)}, u32[]{:S(2)}) async-start(bf16[8,9,128,64]{2,3,1,0:T(8,128)(2,1)} %pad_maximum_fusion), calls=%async_computation | async-start | bytes 2359296 | tf_op jit(solution)/shard_map/all_to_all | solution.py:109
  34.9 3.2 %copy.117 = bf16[128,8192]{0,1:T(8,128)(2,1)S(1)} copy(bf16[128,8192]{1,0:T(8,128)(2,1)} %param.6) | data formatting | bytes 4194304 | tf_op args[0]
  43.9 3.6 %fusion.1 = bf16[128,128,128]{2,1,0:T(8,128)(2,1)S(1)} fusion(f32[128,128]{1,0:T(8,128)} %copy.116, f32[128,128]{1,0:T(8,128)} %copy.114, f32[8,128,128]{2,1,0:T(8,128)S(1)} %fusion.22, pred[128,128]{1,0:T(8,128)(4,1)S(1)} %iota_compare_fusion.3), kind=kLoop, calls=%fused_computation.2 | loop fusion | flops 12582912 | bytes 4866048 | tf_op jit(solution)/shard_map/convert_element_type | solution.py:116
  47.5 5.0 %convolution_bitcast_fusion.1 = f32[128,128,64]{0,2,1:T(8,128)} fusion(bf16[128,128,128]{2,1,0:T(8,128)(2,1)S(1)} %fusion.1, bf16[128,128,64]{0,2,1:T(8,128)(2,1)S(1)} %bitcast.123), kind=kOutput, calls=%fused_computation.12 | convolution fusion | flops 268435456 | bytes 10485760 | tf_op jit(solution)/shard_map/hts,shp->thp/dot_general | solution.py:117
  52.5 14.5 %all-to-all-done = bf16[8,9,128,64]{2,3,1,0:T(8,128)(2,1)S(1)} async-done(((bf16[8,9,128,64]{2,3,1,0:T(8,128)(2,1)}), bf16[8,9,128,64]{2,3,1,0:T(8,128)(2,1)S(1)}, u32[]{:S(2)}, u32[]{:S(2)}) %all-to-all-start) | async-done | bytes 1179680 | tf_op jit(solution)/shard_map/all_to_all | solution.py:109
  67.9 2.1 %convolution_bitcast_fusion = f32[9,8,128,64]{2,0,3,1:T(8,128)S(1)} fusion(bf16[8,8,128,64]{2,3,1,0:T(8,128)(2,1)S(1)} %slice.87, f32[8,9,8,1]{1,0,2,3:T(8,128)S(1)} %fusion.15), kind=kOutput, calls=%fused_computation.11 | convolution fusion | flops 56623104 | bytes 3410176 | tf_op jit(solution)/shard_map/hab,bhnp->ahnp/dot_general | solution.py:126
  70.0 2.0 %copy-done.3 = f32[9,8,128,64]{2,0,3,1:T(8,128)} copy-done((f32[9,8,128,64]{2,0,3,1:T(8,128)}, f32[9,8,128,64]{2,0,3,1:T(8,128)S(1)}, u32[]{:S(2)}) %copy-start.3) | copy-done | bytes 2359320
  72.9 9.8 %all-to-all-start.1 = ((f32[32,24,128]{2,1,0:T(8,128)}), f32[32,24,128]{2,1,0:T(8,128)}, u32[]{:S(2)}, u32[]{:S(2)}) async-start(f32[32,24,128]{2,1,0:T(8,128)} %select_maximum_fusion), calls=%async_computation.1 | async-start | bytes 786432 | tf_op jit(solution)/shard_map/all_to_all | solution.py:145
  82.7 13.8 %all-to-all-done.1 = f32[32,24,128]{2,1,0:T(8,128)} async-done(((f32[32,24,128]{2,1,0:T(8,128)}), f32[32,24,128]{2,1,0:T(8,128)}, u32[]{:S(2)}, u32[]{:S(2)}) %all-to-all-start.1) | async-done | bytes 393248 | tf_op jit(solution)/shard_map/all_to_all | solution.py:145
  100.9 5.0 %all-to-all-start.2 = ((f32[32,16,128]{2,1,0:T(8,128)}), f32[32,16,128]{2,1,0:T(8,128)S(1)}, u32[]{:S(2)}, u32[]{:S(2)}) async-start(f32[32,16,128]{2,1,0:T(8,128)} %copy.138), calls=%async_computation.2 | async-start | bytes 524288 | tf_op jit(solution)/shard_map/all_to_all | solution.py:152
  106.0 10.4 %all-to-all-done.2 = f32[32,16,128]{2,1,0:T(8,128)S(1)} async-done(((f32[32,16,128]{2,1,0:T(8,128)}), f32[32,16,128]{2,1,0:T(8,128)S(1)}, u32[]{:S(2)}, u32[]{:S(2)}) %all-to-all-start.2) | async-done | bytes 262176 | tf_op jit(solution)/shard_map/all_to_all | solution.py:152
  116.4 1.9 %fusion.8 = bf16[8,8,128,64]{2,0,3,1:T(8,128)(2,1)S(1)} fusion(f32[9,8,128,64]{2,0,3,1:T(8,128)} %copy-done.3, f32[8,128,64]{1,2,0:T(8,128)S(1)} %bitcast.135, f32[8,8]{0,1:T(8,128)S(1)} %slice_exponential_fusion), kind=kLoop, calls=%fused_computation.17 | loop fusion | flops 1572864 | bytes 3408128 | tf_op jit(solution)/shard_map/convert_element_type | solution.py:156
  118.6 26.8 %all_to_all.20 = bf16[8,8,128,64]{2,3,1,0:T(8,128)(2,1)S(1)} all-to-all(bf16[8,8,128,64]{2,3,1,0:T(8,128)(2,1)S(1)} %copy.139), channel_id=1, replica_groups=mesh['seq'=32,'z'=8,'core'=2] {'z'}, dimensions={0} | all-to-all | bytes 2097152 | tf_op jit(solution)/shard_map/all_to_all | solution.py:156
  145.4 3.6 %fusion.6 = (bf16[64,128,64]{1,2,0:T(8,128)(2,1)}, bf16[64,128,64]{1,2,0:T(8,128)(2,1)}) fusion(bf16[8,8,128,64]{2,3,1,0:T(8,128)(2,1)S(1)} %all_to_all.20, f32[64]{0:T(128)S(1)} %get-tuple-element.22, pred[]{:T(512)S(6)} %eq.2, f32[64,128,64]{1,2,0:T(8,128)} %collective-permute-done.1, f32[4,16,64,128]{3,2,1,0:T(8,128)S(1)} %copy-done.1), kind=kLoop, calls=%fused_computation.14 | loop fusion | flops 4194304 | bytes 7340289 | tf_op jit(solution)/shard_map/convert_element_type | solution.py:160
  149.0 6.0 %collective-permute-start.2 = (bf16[64,128,64]{1,2,0:T(8,128)(2,1)}, bf16[64,128,64]{1,2,0:T(8,128)(2,1)}, u32[]{:S(2)}, u32[]{:S(2)}) collective-permute-start(bf16[64,128,64]{1,2,0:T(8,128)(2,1)} %get-tuple-element.12), channel_id=1, source_target_pairs={{0,1},{1,0},{2,3},{3,2},{4,5},{5,4},{6,7},{7,6},{8,9},{9,8},{10,11... | collective-permute-start | bytes 3145736 | tf_op jit(solution)/shard_map/ppermute | solution.py:12
  157.6 2.6 %maximum_select_fusion = bf16[128,128,64]{1,2,0:T(8,128)(2,1)S(1)} fusion(bf16[64,128,64]{1,2,0:T(8,128)(2,1)} %collective-permute-done.2, bf16[64,128,64]{1,2,0:T(8,128)(2,1)} %get-tuple-element.11, pred[]{:T(512)S(6)} %eq.2), kind=kLoop, calls=%fused_computation.18 | loop fusion | flops 3145728 | bytes 4194305 | tf_op jit(solution)/shard_map/jit(_where)/select_n | solution.py:163
  162.4 2.2 %fusion.4 = bf16[128,128,64]{0,2,1:T(8,128)(2,1)} fusion(f32[128,128,64]{0,2,1:T(8,128)S(1)} %copy-done.2, f32[8,16,64,128]{3,2,1,0:T(8,128)S(1)} %fusion.31, bf16[128,128,64]{0,2,1:T(8,128)(2,1)S(1)} %bitcast.124, f32[128]{0:T(128)S(1)} %add.77, f32[128,128]{0,1:T(8,128)S(1)} %copy-done.6), kind=kLoop, calls=%fused_computation.6 | loop fusion | flops 6291456 | bytes 12648960 | tf_op jit(solution)/shard_map/convert_element_type | solution.py:174
  164.6 4.1 %copy.143 = bf16[128,8192]{1,0:T(8,128)(2,1)} copy(bf16[128,8192]{0,1:T(8,128)(2,1)} %bitcast.126) | data formatting | bytes 4194304 | tf_op jit(solution)/shard_map/reshape | solution.py:174
  (84 shorter events, 25.5 us)
Async XLA Ops:
  0.9 25.8 %copy-start.5 = (f32[128,128]{1,0:T(8,128)}, f32[128,128]{1,0:T(8,128)S(1)}, u32[]{:S(2)}) copy-start(f32[128,128]{1,0:T(8,128)S(1)} %reduce_window_sum.11) | copy-start | bytes 196612
  10.7 1.3 copy-start.4
  10.8 11.9 %copy-start.8 = (f32[8]{0:T(128)S(1)}, f32[8]{0:T(128)}, u32[]{:S(2)}) copy-start(f32[8]{0:T(128)} %param.11) | copy-start | bytes 100
  13.8 13.2 %collective-permute-start.1 = (f32[64,128,64]{1,2,0:T(8,128)}, f32[64,128,64]{1,2,0:T(8,128)}, u32[]{:S(2)}, u32[]{:S(2)}) collective-permute-start(f32[64,128,64]{1,2,0:T(8,128)} %bitcast.16), channel_id=1, source_target_pairs={{0,1},{1,0},{2,3},{3,2},{4,5},{5,4},{6,7},{7,6},{8,9},{9,8},{10,11... | collective-permute-start | bytes 6291464 | tf_op jit(solution)/shard_map/ppermute | solution.py:12
  22.6 3.8 %collective-permute-start = (f32[136]{0:T(256)S(1)}, f32[136]{0:T(256)S(1)}, u32[]{:S(2)}, u32[]{:S(2)}) collective-permute-start(f32[136]{0:T(256)S(1)} %pad_maximum_fusion.2), channel_id=1, source_target_pairs={{0,1},{1,0},{2,3},{3,2},{4,5},{5,4},{6,7},{7,6},{8,9},{9,8},{10,11... | collective-permute-start | bytes 1640 | tf_op jit(solution)/shard_map/ppermute | solution.py:12
  26.2 2.9 %copy-start = (f32[4,16,64,128]{3,2,1,0:T(8,128)}, f32[4,16,64,128]{3,2,1,0:T(8,128)S(1)}, u32[]{:S(2)}) copy-start(f32[4,16,64,128]{3,2,1,0:T(8,128)S(1)} %fusion.19) | copy-start | bytes 6291460
  30.2 36.7 %all-to-all-start = ((bf16[8,9,128,64]{2,3,1,0:T(8,128)(2,1)}), bf16[8,9,128,64]{2,3,1,0:T(8,128)(2,1)S(1)}, u32[]{:S(2)}, u32[]{:S(2)}) async-start(bf16[8,9,128,64]{2,3,1,0:T(8,128)(2,1)} %pad_maximum_fusion), calls=%async_computation | async-start | bytes 2359296 | tf_op jit(solution)/shard_map/all_to_all | solution.py:109
  70.0 2.0 %copy-start.3 = (f32[9,8,128,64]{2,0,3,1:T(8,128)}, f32[9,8,128,64]{2,0,3,1:T(8,128)S(1)}, u32[]{:S(2)}) copy-start(f32[9,8,128,64]{2,0,3,1:T(8,128)S(1)} %convolution_bitcast_fusion) | copy-start | bytes 7077892
  72.9 23.6 %all-to-all-start.1 = ((f32[32,24,128]{2,1,0:T(8,128)}), f32[32,24,128]{2,1,0:T(8,128)}, u32[]{:S(2)}, u32[]{:S(2)}) async-start(f32[32,24,128]{2,1,0:T(8,128)} %select_maximum_fusion), calls=%async_computation.1 | async-start | bytes 786432 | tf_op jit(solution)/shard_map/all_to_all | solution.py:145
  100.9 15.5 %all-to-all-start.2 = ((f32[32,16,128]{2,1,0:T(8,128)}), f32[32,16,128]{2,1,0:T(8,128)S(1)}, u32[]{:S(2)}, u32[]{:S(2)}) async-start(f32[32,16,128]{2,1,0:T(8,128)} %copy.138), calls=%async_computation.2 | async-start | bytes 524288 | tf_op jit(solution)/shard_map/all_to_all | solution.py:152
  118.3 27.1 %copy-start.1 = (f32[4,16,64,128]{3,2,1,0:T(8,128)S(1)}, f32[4,16,64,128]{3,2,1,0:T(8,128)}, u32[]{:S(2)}) copy-start(f32[4,16,64,128]{3,2,1,0:T(8,128)} %copy-done) | copy-start | bytes 6291460
  145.4 9.6 %copy-start.7 = (f32[128,128]{1,0:T(8,128)S(1)}, f32[128,128]{1,0:T(8,128)}, u32[]{:S(2)}) copy-start(f32[128,128]{1,0:T(8,128)} %get-tuple-element.15) | copy-start | bytes 196612
  149.0 8.6 %collective-permute-start.2 = (bf16[64,128,64]{1,2,0:T(8,128)(2,1)}, bf16[64,128,64]{1,2,0:T(8,128)(2,1)}, u32[]{:S(2)}, u32[]{:S(2)}) collective-permute-start(bf16[64,128,64]{1,2,0:T(8,128)(2,1)} %get-tuple-element.12), channel_id=1, source_target_pairs={{0,1},{1,0},{2,3},{3,2},{4,5},{5,4},{6,7},{7,6},{8,9},{9,8},{10,11... | collective-permute-start | bytes 3145736 | tf_op jit(solution)/shard_map/ppermute | solution.py:12
  160.2 2.2 %copy-start.2 = (f32[128,128,64]{0,2,1:T(8,128)S(1)}, f32[128,128,64]{0,2,1:T(8,128)}, u32[]{:S(2)}) copy-start(f32[128,128,64]{0,2,1:T(8,128)} %convolution_bitcast_fusion.1) | copy-start | bytes 12582916
  160.2 2.2 %copy-start.6 = (f32[128,128]{0,1:T(8,128)S(1)}, f32[128,128]{0,1:T(8,128)}, u32[]{:S(2)}) copy-start(f32[128,128]{0,1:T(8,128)} %copy.131) | copy-start | bytes 196612

commit v14 on v12

--- a/solution.py
+++ b/solution.py
@@ -143,7 +143,7 @@
         gathered[:, :per],
         precision=lax.Precision.HIGHEST,
     )
-    acc_s = lax.all_to_all(entering, "seq", 0, 0, tiled=True)
+    acc_s = lax.all_to_all(entering.astype(bf16), "seq", 0, 0, tiled=True).astype(f32)
     acc_s = acc_s.reshape(quarter, width, state).transpose(0, 2, 1)
 
     chip_in = starts + jnp.exp(lead)[:, :, None, None] * acc_s[None]

time: 167 us -> 166 us (level)
  no operation moved by 1% of the time
where the time goes in v14:
time: 166 us; the launch traced here: 164 us
  waiting for transfers between devices  42.9 us (26%)
  starting transfers between devices  35 us (21%)
  blocking collectives  27.8 us (17%)
  local copies, waits for them, and re-layouts  23.6 us (14%)
  other arithmetic  22.8 us (14%)
  matrix products  11.8 us (7%)
    all_to_all x1, blocking collectives, local(): back = lax.all_to_all(chip_in.astype(bf16), 'z', 0, 0, tiled=True)  27.8 us
    all_to_all x1, waiting for transfers between devices, local(): rows = lax.all_to_all(message, 'z', 0, 0, tiled=True)  17.6 us
    ppermute x3, starting transfers between devices, swap(): return lax.ppermute(value, 'core', [(0, 1), (1, 0)])  15.6 us
    all_to_all x1, waiting for transfers between devices, local(): gathered = lax.all_to_all(packed, 'seq', 0, 0, tiled=True)  13.8 us
    all_to_all x1, starting transfers between devices, local(): gathered = lax.all_to_all(packed, 'seq', 0, 0, tiled=True)  9.78 us
    unnamed x22, local copies, waits for them, and re-layouts  9.65 us
    all_to_all x1, waiting for transfers between devices, local(): lax.all_to_all(entering.astype(bf16), 'seq', 0, 0, tiled=True).astype(f32)  9.34 us
    all_to_all x1, starting transfers between devices, local(): lax.all_to_all(entering.astype(bf16), 'seq', 0, 0, tiled=True).astype(f32)  5.04 us
  transfers between devices with their start and end apart: 6, of which 5 were waited for; matrix products, arithmetic and copies ran while one was open for 10% of the time, Pallas kernels for 0%

profile of v14, /device:TPU:1, one launch (start us, length us, event | category | flops | bytes accessed | tf_op | source)
XLA Modules:
  0.0 164.3 jit_solution(12450859027241759157)
XLA Ops:
  3.5 3.2 %copy.112 = bf16[128,8192]{0,1:T(8,128)(2,1)S(1)} copy(bf16[128,8192]{1,0:T(8,128)(2,1)} %param.6) | data formatting | bytes 4194304 | tf_op args[0]
  7.4 1.6 constant_dynamic-slice_fusion
  10.0 8.8 %collective-permute-start.1 = (f32[64,128,64]{1,2,0:T(8,128)}, f32[64,128,64]{1,2,0:T(8,128)}, u32[]{:S(2)}, u32[]{:S(2)}) collective-permute-start(f32[64,128,64]{1,2,0:T(8,128)} %constant_dynamic-slice_fusion), channel_id=1, source_target_pairs={{0,1},{1,0},{2,3},{3,2},{4,5},{5,4},{6,7},{7,6},{8,9},{9,8},{10,11... | collective-permute-start | bytes 6291464 | tf_op jit(solution)/shard_map/ppermute | solution.py:12
  18.8 1.9 %collective-permute-start = (f32[136]{0:T(256)S(1)}, f32[136]{0:T(256)S(1)}, u32[]{:S(2)}, u32[]{:S(2)}) collective-permute-start(f32[136]{0:T(256)S(1)} %pad_maximum_fusion.2), channel_id=1, source_target_pairs={{0,1},{1,0},{2,3},{3,2},{4,5},{5,4},{6,7},{7,6},{8,9},{9,8},{10,11... | collective-permute-start | bytes 1640 | tf_op jit(solution)/shard_map/ppermute | solution.py:12
  21.0 1.6 collective-permute-done
  23.2 2.6 %add_convert_fusion = bf16[64,128,64]{1,2,0:T(8,128)(2,1)S(1)} fusion(f32[64,128,64]{1,2,0:T(8,128)} %collective-permute-done.1, f32[128,128,64]{1,2,0:T(8,128)} %bitcast.113, s32[]{:T(128)S(6)} %select_n.101, f32[64]{0:T(128)S(1)} %get-tuple-element.24, pred[]{:T(512)S(6)} %eq.2), kind=kLoop, calls=%fused_computation.21 | loop fusion | flops 2621440 | bytes 5243141 | tf_op jit(solution)/shard_map/convert_element_type | solution.py:87
  27.0 4.7 %all-to-all-start = ((bf16[8,9,128,64]{2,3,1,0:T(8,128)(2,1)}), bf16[8,9,128,64]{2,3,1,0:T(8,128)(2,1)S(1)}, u32[]{:S(2)}, u32[]{:S(2)}) async-start(bf16[8,9,128,64]{2,3,1,0:T(8,128)(2,1)} %pad_maximum_fusion), calls=%async_computation | async-start | bytes 2359296 | tf_op jit(solution)/shard_map/all_to_all | solution.py:103
  34.6 1.6 copy.111
  37.5 3.6 %fusion.1 = bf16[128,128,128]{2,1,0:T(8,128)(2,1)S(1)} fusion(f32[128,128]{1,0:T(8,128)} %copy.111, f32[128,128]{1,0:T(8,128)} %copy.109, f32[8,128,128]{2,1,0:T(8,128)S(1)} %fusion.21, pred[128,128]{1,0:T(8,128)(4,1)S(1)} %iota_compare_fusion.3), kind=kLoop, calls=%fused_computation.2 | loop fusion | flops 12582912 | bytes 4866048 | tf_op jit(solution)/shard_map/convert_element_type | solution.py:110
  41.1 5.0 %convolution_bitcast_fusion.1 = f32[128,128,64]{0,2,1:T(8,128)} fusion(bf16[128,128,128]{2,1,0:T(8,128)(2,1)S(1)} %fusion.1, bf16[128,128,64]{0,2,1:T(8,128)(2,1)S(1)} %bitcast.110), kind=kOutput, calls=%fused_computation.13 | convolution fusion | flops 268435456 | bytes 10485760 | tf_op jit(solution)/shard_map/hts,shp->thp/dot_general | solution.py:111
  46.1 17.6 %all-to-all-done = bf16[8,9,128,64]{2,3,1,0:T(8,128)(2,1)S(1)} async-done(((bf16[8,9,128,64]{2,3,1,0:T(8,128)(2,1)}), bf16[8,9,128,64]{2,3,1,0:T(8,128)(2,1)S(1)}, u32[]{:S(2)}, u32[]{:S(2)}) %all-to-all-start) | async-done | bytes 1179680 | tf_op jit(solution)/shard_map/all_to_all | solution.py:103
  64.8 2.1 %convolution_bitcast_fusion = f32[9,8,128,64]{2,0,3,1:T(8,128)S(1)} fusion(bf16[8,8,128,64]{2,3,1,0:T(8,128)(2,1)S(1)} %slice.87, f32[8,9,8,1]{1,0,2,3:T(8,128)S(1)} %fusion.18), kind=kOutput, calls=%fused_computation.12 | convolution fusion | flops 56623104 | bytes 3410176 | tf_op jit(solution)/shard_map/hab,bhnp->ahnp/dot_general | solution.py:120
  66.8 2.0 %copy-done.3 = f32[9,8,128,64]{2,0,3,1:T(8,128)} copy-done((f32[9,8,128,64]{2,0,3,1:T(8,128)}, f32[9,8,128,64]{2,0,3,1:T(8,128)S(1)}, u32[]{:S(2)}) %copy-start.3) | copy-done | bytes 2359320
  69.7 9.8 %all-to-all-start.1 = ((f32[32,24,128]{2,1,0:T(8,128)}), f32[32,24,128]{2,1,0:T(8,128)}, u32[]{:S(2)}, u32[]{:S(2)}) async-start(f32[32,24,128]{2,1,0:T(8,128)} %select_maximum_fusion), calls=%async_computation.1 | async-start | bytes 786432 | tf_op jit(solution)/shard_map/all_to_all | solution.py:139
  79.5 13.8 %all-to-all-done.1 = f32[32,24,128]{2,1,0:T(8,128)} async-done(((f32[32,24,128]{2,1,0:T(8,128)}), f32[32,24,128]{2,1,0:T(8,128)}, u32[]{:S(2)}, u32[]{:S(2)}) %all-to-all-start.1) | async-done | bytes 393248 | tf_op jit(solution)/shard_map/all_to_all | solution.py:139
  97.6 5.0 %all-to-all-start.2 = ((bf16[32,16,128]{2,1,0:T(8,128)(2,1)}), bf16[32,16,128]{2,1,0:T(8,128)(2,1)S(1)}, u32[]{:S(2)}, u32[]{:S(2)}) async-start(bf16[32,16,128]{2,1,0:T(8,128)(2,1)} %copy.132), calls=%async_computation.2 | async-start | bytes 262144 | tf_op jit(solution)/shard_map/all_to_all | solution.py:146
  102.6 9.3 %all-to-all-done.2 = bf16[32,16,128]{2,1,0:T(8,128)(2,1)S(1)} async-done(((bf16[32,16,128]{2,1,0:T(8,128)(2,1)}), bf16[32,16,128]{2,1,0:T(8,128)(2,1)S(1)}, u32[]{:S(2)}, u32[]{:S(2)}) %all-to-all-start.2) | async-done | bytes 131104 | tf_op jit(solution)/shard_map/all_to_all | solution.py:146
  112.0 2.0 %fusion.11 = bf16[8,8,128,64]{2,0,3,1:T(8,128)(2,1)S(1)} fusion(f32[9,8,128,64]{2,0,3,1:T(8,128)} %copy-done.3, f32[8,128,64]{1,2,0:T(8,128)S(1)} %convert_bitcast_fusion, f32[8,8]{0,1:T(8,128)S(1)} %slice_exponential_fusion), kind=kLoop, calls=%fused_computation.19 | loop fusion | flops 1572864 | bytes 3408128 | tf_op jit(solution)/shard_map/convert_element_type | solution.py:150
  114.2 27.8 %all_to_all.20 = bf16[8,8,128,64]{2,3,1,0:T(8,128)(2,1)S(1)} all-to-all(bf16[8,8,128,64]{2,3,1,0:T(8,128)(2,1)S(1)} %copy.133), channel_id=1, replica_groups=mesh['seq'=32,'z'=8,'core'=2] {'z'}, dimensions={0} | all-to-all | bytes 2097152 | tf_op jit(solution)/shard_map/all_to_all | solution.py:150
  142.1 3.6 %fusion.7 = (bf16[64,128,64]{1,2,0:T(8,128)(2,1)}, bf16[64,128,64]{1,2,0:T(8,128)(2,1)}) fusion(bf16[8,8,128,64]{2,3,1,0:T(8,128)(2,1)S(1)} %all_to_all.20, f32[64]{0:T(128)S(1)} %get-tuple-element.22, pred[]{:T(512)S(6)} %eq.2, f32[64,128,64]{1,2,0:T(8,128)} %collective-permute-done.1, f32[128,128,64]{1,2,0:T(8,128)S(1)} %bitcast.114, s32[]{:T(128)S(6)} %select_n.101), kind=kLoop, calls=%fused_computation.15 | loop fusion | flops 4194304 | bytes 7340293 | tf_op jit(solution)/shard_map/convert_element_type | solution.py:154
  145.6 4.9 %collective-permute-start.2 = (bf16[64,128,64]{1,2,0:T(8,128)(2,1)}, bf16[64,128,64]{1,2,0:T(8,128)(2,1)}, u32[]{:S(2)}, u32[]{:S(2)}) collective-permute-start(bf16[64,128,64]{1,2,0:T(8,128)(2,1)} %get-tuple-element.12), channel_id=1, source_target_pairs={{0,1},{1,0},{2,3},{3,2},{4,5},{5,4},{6,7},{7,6},{8,9},{9,8},{10,11... | collective-permute-start | bytes 3145736 | tf_op jit(solution)/shard_map/ppermute | solution.py:12
  153.1 2.8 %maximum_select_fusion = bf16[128,128,64]{1,2,0:T(8,128)(2,1)S(1)} fusion(bf16[64,128,64]{1,2,0:T(8,128)(2,1)} %collective-permute-done.2, bf16[64,128,64]{1,2,0:T(8,128)(2,1)} %get-tuple-element.11, pred[]{:T(512)S(6)} %eq.2), kind=kLoop, calls=%fused_computation.20 | loop fusion | flops 3145728 | bytes 4194305 | tf_op jit(solution)/shard_map/jit(_where)/select_n | solution.py:157
  158.1 2.2 %fusion.4 = bf16[128,128,64]{0,2,1:T(8,128)(2,1)} fusion(f32[128,128,64]{0,2,1:T(8,128)S(1)} %copy-done.2, f32[8,16,64,128]{3,2,1,0:T(8,128)S(1)} %fusion.32, bf16[128,128,64]{0,2,1:T(8,128)(2,1)S(1)} %bitcast.111, f32[128]{0:T(128)S(1)} %add.72, f32[128,128]{0,1:T(8,128)S(1)} %copy-done.6), kind=kLoop, calls=%fused_computation.6 | loop fusion | flops 6291456 | bytes 12648960 | tf_op jit(solution)/shard_map/convert_element_type | solution.py:168
  160.3 4.1 %copy.137 = bf16[128,8192]{1,0:T(8,128)(2,1)} copy(bf16[128,8192]{0,1:T(8,128)(2,1)} %bitcast.115) | data formatting | bytes 4194304 | tf_op jit(solution)/shard_map/reshape | solution.py:168
  (83 shorter events, 22.4 us)
Async XLA Ops:
  0.9 22.0 %copy-start.5 = (f32[128,128]{1,0:T(8,128)}, f32[128,128]{1,0:T(8,128)S(1)}, u32[]{:S(2)}) copy-start(f32[128,128]{1,0:T(8,128)S(1)} %reduce_window_sum.11) | copy-start | bytes 196612
  7.4 2.6 %copy-start = (f32[8,16,64,128]{3,2,1,0:T(8,128)}, f32[8,16,64,128]{3,2,1,0:T(8,128)S(1)}, u32[]{:S(2)}) copy-start(f32[8,16,64,128]{3,2,1,0:T(8,128)S(1)} %fusion.9) | copy-start | bytes 12582916
  7.4 11.4 %copy-start.8 = (f32[8]{0:T(128)S(1)}, f32[8]{0:T(128)}, u32[]{:S(2)}) copy-start(f32[8]{0:T(128)} %param.11) | copy-start | bytes 100
  10.0 13.2 %collective-permute-start.1 = (f32[64,128,64]{1,2,0:T(8,128)}, f32[64,128,64]{1,2,0:T(8,128)}, u32[]{:S(2)}, u32[]{:S(2)}) collective-permute-start(f32[64,128,64]{1,2,0:T(8,128)} %constant_dynamic-slice_fusion), channel_id=1, source_target_pairs={{0,1},{1,0},{2,3},{3,2},{4,5},{5,4},{6,7},{7,6},{8,9},{9,8},{10,11... | collective-permute-start | bytes 6291464 | tf_op jit(solution)/shard_map/ppermute | solution.py:12
  18.8 3.7 %collective-permute-start = (f32[136]{0:T(256)S(1)}, f32[136]{0:T(256)S(1)}, u32[]{:S(2)}, u32[]{:S(2)}) collective-permute-start(f32[136]{0:T(256)S(1)} %pad_maximum_fusion.2), channel_id=1, source_target_pairs={{0,1},{1,0},{2,3},{3,2},{4,5},{5,4},{6,7},{7,6},{8,9},{9,8},{10,11... | collective-permute-start | bytes 1640 | tf_op jit(solution)/shard_map/ppermute | solution.py:12
  25.9 10.3 %copy-start.4 = (bf16[128,1024]{1,0:T(8,128)(2,1)S(1)}, bf16[128,1024]{1,0:T(8,128)(2,1)}, u32[]{:S(2)}) copy-start(bf16[128,1024]{1,0:T(8,128)(2,1)} %param.9) | copy-start | bytes 786436
  27.0 36.8 %all-to-all-start = ((bf16[8,9,128,64]{2,3,1,0:T(8,128)(2,1)}), bf16[8,9,128,64]{2,3,1,0:T(8,128)(2,1)S(1)}, u32[]{:S(2)}, u32[]{:S(2)}) async-start(bf16[8,9,128,64]{2,3,1,0:T(8,128)(2,1)} %pad_maximum_fusion), calls=%async_computation | async-start | bytes 2359296 | tf_op jit(solution)/shard_map/all_to_all | solution.py:103
  66.8 2.0 %copy-start.3 = (f32[9,8,128,64]{2,0,3,1:T(8,128)}, f32[9,8,128,64]{2,0,3,1:T(8,128)S(1)}, u32[]{:S(2)}) copy-start(f32[9,8,128,64]{2,0,3,1:T(8,128)S(1)} %convolution_bitcast_fusion) | copy-start | bytes 7077892
  69.7 23.6 %all-to-all-start.1 = ((f32[32,24,128]{2,1,0:T(8,128)}), f32[32,24,128]{2,1,0:T(8,128)}, u32[]{:S(2)}, u32[]{:S(2)}) async-start(f32[32,24,128]{2,1,0:T(8,128)} %select_maximum_fusion), calls=%async_computation.1 | async-start | bytes 786432 | tf_op jit(solution)/shard_map/all_to_all | solution.py:139
  97.6 14.4 %all-to-all-start.2 = ((bf16[32,16,128]{2,1,0:T(8,128)(2,1)}), bf16[32,16,128]{2,1,0:T(8,128)(2,1)S(1)}, u32[]{:S(2)}, u32[]{:S(2)}) async-start(bf16[32,16,128]{2,1,0:T(8,128)(2,1)} %copy.132), calls=%async_computation.2 | async-start | bytes 262144 | tf_op jit(solution)/shard_map/all_to_all | solution.py:146
  114.0 28.1 %copy-start.1 = (f32[8,16,64,128]{3,2,1,0:T(8,128)S(1)}, f32[8,16,64,128]{3,2,1,0:T(8,128)}, u32[]{:S(2)}) copy-start(f32[8,16,64,128]{3,2,1,0:T(8,128)} %copy-done) | copy-start | bytes 12582916
  142.1 8.5 %copy-start.7 = (f32[128,128]{1,0:T(8,128)S(1)}, f32[128,128]{1,0:T(8,128)}, u32[]{:S(2)}) copy-start(f32[128,128]{1,0:T(8,128)} %get-tuple-element.15) | copy-start | bytes 196612
  145.6 7.5 %collective-permute-start.2 = (bf16[64,128,64]{1,2,0:T(8,128)(2,1)}, bf16[64,128,64]{1,2,0:T(8,128)(2,1)}, u32[]{:S(2)}, u32[]{:S(2)}) collective-permute-start(bf16[64,128,64]{1,2,0:T(8,128)(2,1)} %get-tuple-element.12), channel_id=1, source_target_pairs={{0,1},{1,0},{2,3},{3,2},{4,5},{5,4},{6,7},{7,6},{8,9},{9,8},{10,11... | collective-permute-start | bytes 3145736 | tf_op jit(solution)/shard_map/ppermute | solution.py:12
  155.9 2.2 %copy-start.2 = (f32[128,128,64]{0,2,1:T(8,128)S(1)}, f32[128,128,64]{0,2,1:T(8,128)}, u32[]{:S(2)}) copy-start(f32[128,128,64]{0,2,1:T(8,128)} %convolution_bitcast_fusion.1) | copy-start | bytes 12582916
  155.9 2.2 %copy-start.6 = (f32[128,128]{0,1:T(8,128)S(1)}, f32[128,128]{0,1:T(8,128)}, u32[]{:S(2)}) copy-start(f32[128,128]{0,1:T(8,128)} %copy.125) | copy-start | bytes 196612

commit v15 on v14

--- a/solution.py
+++ b/solution.py
@@ -33,8 +33,9 @@
     a = jnp.arange(outs)[:, None, None]
     b = jnp.arange(count)[None, :, None]
     m = jnp.arange(count)[None, None, :]
-    between = ((b < m) & (m < a)).astype(jnp.float32)
-    exponent = jnp.einsum("abm,mh->hab", between, totals, precision=lax.Precision.HIGHEST)
+    between = (b < m) & (m < a)
+    exponent = jnp.sum(jnp.where(between[..., None], totals[None, None], 0.0), axis=2)
+    exponent = exponent.transpose(2, 0, 1)
     earlier = (b < a)[None, :, :, 0]
     return jnp.where(earlier, jnp.exp(jnp.where(earlier, exponent, 0.0)), 0.0)
 

time: 166 us -> 169 us (1.018)
  other arithmetic: 22.8 us -> 26.3 us
    reduce_sum x0 -> x2, other arithmetic: none -> 2.36 us  [decay_matrix(): jnp.sum(jnp.where(between[..., None], totals[None, None], 0.0), axis=2)]
where the time goes in v15:
time: 169 us; the launch traced here: 168 us
  waiting for transfers between devices  42.6 us (25%)
  starting transfers between devices  35.2 us (21%)
  blocking collectives  27.8 us (16%)
  other arithmetic  26.3 us (16%)
  local copies, waits for them, and re-layouts  24.9 us (15%)
  matrix products  10.3 us (6%)
    all_to_all x1, blocking collectives, local(): back = lax.all_to_all(chip_in.astype(bf16), 'z', 0, 0, tiled=True)  27.8 us
    all_to_all x1, waiting for transfers between devices, local(): rows = lax.all_to_all(message, 'z', 0, 0, tiled=True)  17.6 us
    ppermute x3, starting transfers between devices, swap(): return lax.ppermute(value, 'core', [(0, 1), (1, 0)])  15.6 us
    all_to_all x1, waiting for transfers between devices, local(): gathered = lax.all_to_all(packed, 'seq', 0, 0, tiled=True)  13.7 us
    all_to_all x1, starting transfers between devices, local(): gathered = lax.all_to_all(packed, 'seq', 0, 0, tiled=True)  9.78 us
    unnamed x22, local copies, waits for them, and re-layouts  9.68 us
    all_to_all x1, waiting for transfers between devices, local(): lax.all_to_all(entering.astype(bf16), 'seq', 0, 0, tiled=True).astype(f32)  9.16 us
    all_to_all x1, starting transfers between devices, local(): lax.all_to_all(entering.astype(bf16), 'seq', 0, 0, tiled=True).astype(f32)  5.22 us
  transfers between devices with their start and end apart: 6, of which 5 were waited for; matrix products, arithmetic and copies ran while one was open for 10% of the time, Pallas kernels for 0%

profile of v15, /device:TPU:1, one launch (start us, length us, event | category | flops | bytes accessed | tf_op | source)
XLA Modules:
  0.0 167.6 jit_solution(14790344558802550604)
XLA Ops:
  3.5 3.2 %copy.135 = bf16[128,8192]{0,1:T(8,128)(2,1)S(1)} copy(bf16[128,8192]{1,0:T(8,128)(2,1)} %param.6) | data formatting | bytes 4194304 | tf_op args[0]
  7.4 1.6 constant_dynamic-slice_fusion
  10.0 8.8 %collective-permute-start.1 = (f32[64,128,64]{1,2,0:T(8,128)}, f32[64,128,64]{1,2,0:T(8,128)}, u32[]{:S(2)}, u32[]{:S(2)}) collective-permute-start(f32[64,128,64]{1,2,0:T(8,128)} %constant_dynamic-slice_fusion), channel_id=1, source_target_pairs={{0,1},{1,0},{2,3},{3,2},{4,5},{5,4},{6,7},{7,6},{8,9},{9,8},{10,11... | collective-permute-start | bytes 6291464 | tf_op jit(solution)/shard_map/ppermute | solution.py:12
  18.8 1.9 %collective-permute-start = (f32[136]{0:T(256)S(1)}, f32[136]{0:T(256)S(1)}, u32[]{:S(2)}, u32[]{:S(2)}) collective-permute-start(f32[136]{0:T(256)S(1)} %pad_maximum_fusion.2), channel_id=1, source_target_pairs={{0,1},{1,0},{2,3},{3,2},{4,5},{5,4},{6,7},{7,6},{8,9},{9,8},{10,11... | collective-permute-start | bytes 1640 | tf_op jit(solution)/shard_map/ppermute | solution.py:12
  21.0 1.6 collective-permute-done
  23.2 2.6 %add_convert_fusion = bf16[64,128,64]{1,2,0:T(8,128)(2,1)S(1)} fusion(f32[64,128,64]{1,2,0:T(8,128)} %collective-permute-done.1, f32[128,128,64]{1,2,0:T(8,128)} %bitcast.112, s32[]{:T(128)S(6)} %select_n.117, f32[64]{0:T(128)S(1)} %get-tuple-element.24, pred[]{:T(512)S(6)} %eq.2), kind=kLoop, calls=%fused_computation.22 | loop fusion | flops 2621440 | bytes 5243141 | tf_op jit(solution)/shard_map/convert_element_type | solution.py:88
  27.0 4.7 %all-to-all-start = ((bf16[8,9,128,64]{2,3,1,0:T(8,128)(2,1)}), bf16[8,9,128,64]{2,3,1,0:T(8,128)(2,1)S(1)}, u32[]{:S(2)}, u32[]{:S(2)}) async-start(bf16[8,9,128,64]{2,3,1,0:T(8,128)(2,1)} %pad_maximum_fusion), calls=%async_computation | async-start | bytes 2359296 | tf_op jit(solution)/shard_map/all_to_all | solution.py:104
  37.5 3.6 %fusion.1 = bf16[128,128,128]{2,1,0:T(8,128)(2,1)S(1)} fusion(f32[128,128]{1,0:T(8,128)} %copy.134, f32[128,128]{1,0:T(8,128)} %copy.132, f32[8,128,128]{2,1,0:T(8,128)S(1)} %fusion.15, pred[128,128]{1,0:T(8,128)(4,1)S(1)} %iota_compare_fusion.3), kind=kLoop, calls=%fused_computation.2 | loop fusion | flops 12582912 | bytes 4866048 | tf_op jit(solution)/shard_map/convert_element_type | solution.py:111
  41.2 5.0 %convolution_bitcast_fusion.1 = f32[128,128,64]{0,2,1:T(8,128)} fusion(bf16[128,128,128]{2,1,0:T(8,128)(2,1)S(1)} %fusion.1, bf16[128,128,64]{0,2,1:T(8,128)(2,1)S(1)} %bitcast.109), kind=kOutput, calls=%fused_computation.14 | convolution fusion | flops 268435456 | bytes 10485760 | tf_op jit(solution)/shard_map/hts,shp->thp/dot_general | solution.py:112
  46.2 17.6 %all-to-all-done = bf16[8,9,128,64]{2,3,1,0:T(8,128)(2,1)S(1)} async-done(((bf16[8,9,128,64]{2,3,1,0:T(8,128)(2,1)}), bf16[8,9,128,64]{2,3,1,0:T(8,128)(2,1)S(1)}, u32[]{:S(2)}, u32[]{:S(2)}) %all-to-all-start) | async-done | bytes 1179680 | tf_op jit(solution)/shard_map/all_to_all | solution.py:104
  64.7 2.1 %convolution_bitcast_fusion = f32[9,8,128,64]{2,0,3,1:T(8,128)S(1)} fusion(bf16[8,8,128,64]{2,3,1,0:T(8,128)(2,1)S(1)} %slice.87, f32[8,9,8,1]{1,0,2,3:T(8,128)S(1)} %select_bitcast_fusion.1), kind=kOutput, calls=%fused_computation.13 | convolution fusion | flops 56623104 | bytes 3410176 | tf_op jit(solution)/shard_map/hab,bhnp->ahnp/dot_general | solution.py:121
  66.7 2.0 %copy-done.3 = f32[9,8,128,64]{2,0,3,1:T(8,128)} copy-done((f32[9,8,128,64]{2,0,3,1:T(8,128)}, f32[9,8,128,64]{2,0,3,1:T(8,128)S(1)}, u32[]{:S(2)}) %copy-start.3) | copy-done | bytes 2359320
  69.6 9.8 %all-to-all-start.1 = ((f32[32,24,128]{2,1,0:T(8,128)}), f32[32,24,128]{2,1,0:T(8,128)}, u32[]{:S(2)}, u32[]{:S(2)}) async-start(f32[32,24,128]{2,1,0:T(8,128)} %select_maximum_fusion), calls=%async_computation.1 | async-start | bytes 786432 | tf_op jit(solution)/shard_map/all_to_all | solution.py:140
  79.5 13.7 %all-to-all-done.1 = f32[32,24,128]{2,1,0:T(8,128)} async-done(((f32[32,24,128]{2,1,0:T(8,128)}), f32[32,24,128]{2,1,0:T(8,128)}, u32[]{:S(2)}, u32[]{:S(2)}) %all-to-all-start.1) | async-done | bytes 393248 | tf_op jit(solution)/shard_map/all_to_all | solution.py:140
  94.2 2.2 %select_reduce_fusion = f32[32,32,16]{2,1,0:T(8,128)S(1)} fusion(f32[32,16]{0,1:T(8,128)S(1)} %copy.152, pred[32,32,32]{2,1,0:T(8,128)(4,1)S(1)} %broadcast_and_fusion), kind=kLoop, calls=%fused_computation.3 | loop fusion | flops 1032192 | bytes 100352 | tf_op jit(solution)/shard_map/reduce_sum | solution.py:37
  100.9 5.2 %all-to-all-start.2 = ((bf16[32,16,128]{2,1,0:T(8,128)(2,1)}), bf16[32,16,128]{2,1,0:T(8,128)(2,1)S(1)}, u32[]{:S(2)}, u32[]{:S(2)}) async-start(bf16[32,16,128]{2,1,0:T(8,128)(2,1)} %copy.154), calls=%async_computation.2 | async-start | bytes 262144 | tf_op jit(solution)/shard_map/all_to_all | solution.py:147
  106.1 9.2 %all-to-all-done.2 = bf16[32,16,128]{2,1,0:T(8,128)(2,1)S(1)} async-done(((bf16[32,16,128]{2,1,0:T(8,128)(2,1)}), bf16[32,16,128]{2,1,0:T(8,128)(2,1)S(1)}, u32[]{:S(2)}, u32[]{:S(2)}) %all-to-all-start.2) | async-done | bytes 131104 | tf_op jit(solution)/shard_map/all_to_all | solution.py:147
  115.3 2.0 %fusion.11 = bf16[8,8,128,64]{2,0,3,1:T(8,128)(2,1)S(1)} fusion(f32[9,8,128,64]{2,0,3,1:T(8,128)} %copy-done.3, f32[8,128,64]{1,2,0:T(8,128)S(1)} %convert_bitcast_fusion, f32[8,8]{0,1:T(8,128)S(1)} %slice_exponential_fusion), kind=kLoop, calls=%fused_computation.20 | loop fusion | flops 1572864 | bytes 3408128 | tf_op jit(solution)/shard_map/convert_element_type | solution.py:151
  117.5 27.8 %all_to_all.20 = bf16[8,8,128,64]{2,3,1,0:T(8,128)(2,1)S(1)} all-to-all(bf16[8,8,128,64]{2,3,1,0:T(8,128)(2,1)S(1)} %copy.155), channel_id=1, replica_groups=mesh['seq'=32,'z'=8,'core'=2] {'z'}, dimensions={0} | all-to-all | bytes 2097152 | tf_op jit(solution)/shard_map/all_to_all | solution.py:151
  145.3 3.6 %fusion.7 = (bf16[64,128,64]{1,2,0:T(8,128)(2,1)}, bf16[64,128,64]{1,2,0:T(8,128)(2,1)}) fusion(bf16[8,8,128,64]{2,3,1,0:T(8,128)(2,1)S(1)} %all_to_all.20, f32[64]{0:T(128)S(1)} %get-tuple-element.22, pred[]{:T(512)S(6)} %eq.2, f32[64,128,64]{1,2,0:T(8,128)} %collective-permute-done.1, f32[128,128,64]{1,2,0:T(8,128)S(1)} %bitcast.113, s32[]{:T(128)S(6)} %select_n.117), kind=kLoop, calls=%fused_computation.16 | loop fusion | flops 4194304 | bytes 7340293 | tf_op jit(solution)/shard_map/convert_element_type | solution.py:155
  148.9 4.9 %collective-permute-start.2 = (bf16[64,128,64]{1,2,0:T(8,128)(2,1)}, bf16[64,128,64]{1,2,0:T(8,128)(2,1)}, u32[]{:S(2)}, u32[]{:S(2)}) collective-permute-start(bf16[64,128,64]{1,2,0:T(8,128)(2,1)} %get-tuple-element.12), channel_id=1, source_target_pairs={{0,1},{1,0},{2,3},{3,2},{4,5},{5,4},{6,7},{7,6},{8,9},{9,8},{10,11... | collective-permute-start | bytes 3145736 | tf_op jit(solution)/shard_map/ppermute | solution.py:12
  156.4 2.8 %maximum_select_fusion = bf16[128,128,64]{1,2,0:T(8,128)(2,1)S(1)} fusion(bf16[64,128,64]{1,2,0:T(8,128)(2,1)} %collective-permute-done.2, bf16[64,128,64]{1,2,0:T(8,128)(2,1)} %get-tuple-element.11, pred[]{:T(512)S(6)} %eq.2), kind=kLoop, calls=%fused_computation.21 | loop fusion | flops 3145728 | bytes 4194305 | tf_op jit(solution)/shard_map/jit(_where)/select_n | solution.py:158
  161.4 2.2 %fusion.4 = bf16[128,128,64]{0,2,1:T(8,128)(2,1)} fusion(f32[128,128,64]{0,2,1:T(8,128)S(1)} %copy-done.2, f32[8,16,64,128]{3,2,1,0:T(8,128)S(1)} %fusion.26, bf16[128,128,64]{0,2,1:T(8,128)(2,1)S(1)} %bitcast.110, f32[128]{0:T(128)S(1)} %add.72, f32[128,128]{0,1:T(8,128)S(1)} %copy-done.6), kind=kLoop, calls=%fused_computation.7 | loop fusion | flops 6291456 | bytes 12648960 | tf_op jit(solution)/shard_map/convert_element_type | solution.py:169
  163.6 4.1 %copy.159 = bf16[128,8192]{1,0:T(8,128)(2,1)} copy(bf16[128,8192]{0,1:T(8,128)(2,1)} %bitcast.114) | data formatting | bytes 4194304 | tf_op jit(solution)/shard_map/reshape | solution.py:169
  (90 shorter events, 25.2 us)
Async XLA Ops:
  0.9 22.0 %copy-start.5 = (f32[128,128]{1,0:T(8,128)}, f32[128,128]{1,0:T(8,128)S(1)}, u32[]{:S(2)}) copy-start(f32[128,128]{1,0:T(8,128)S(1)} %reduce_window_sum.11) | copy-start | bytes 196612
  7.4 2.6 %copy-start = (f32[8,16,64,128]{3,2,1,0:T(8,128)}, f32[8,16,64,128]{3,2,1,0:T(8,128)S(1)}, u32[]{:S(2)}) copy-start(f32[8,16,64,128]{3,2,1,0:T(8,128)S(1)} %fusion.9) | copy-start | bytes 12582916
  7.4 11.4 %copy-start.8 = (f32[8]{0:T(128)S(1)}, f32[8]{0:T(128)}, u32[]{:S(2)}) copy-start(f32[8]{0:T(128)} %param.11) | copy-start | bytes 100
  10.0 13.2 %collective-permute-start.1 = (f32[64,128,64]{1,2,0:T(8,128)}, f32[64,128,64]{1,2,0:T(8,128)}, u32[]{:S(2)}, u32[]{:S(2)}) collective-permute-start(f32[64,128,64]{1,2,0:T(8,128)} %constant_dynamic-slice_fusion), channel_id=1, source_target_pairs={{0,1},{1,0},{2,3},{3,2},{4,5},{5,4},{6,7},{7,6},{8,9},{9,8},{10,11... | collective-permute-start | bytes 6291464 | tf_op jit(solution)/shard_map/ppermute | solution.py:12
  18.8 3.7 %collective-permute-start = (f32[136]{0:T(256)S(1)}, f32[136]{0:T(256)S(1)}, u32[]{:S(2)}, u32[]{:S(2)}) collective-permute-start(f32[136]{0:T(256)S(1)} %pad_maximum_fusion.2), channel_id=1, source_target_pairs={{0,1},{1,0},{2,3},{3,2},{4,5},{5,4},{6,7},{7,6},{8,9},{9,8},{10,11... | collective-permute-start | bytes 1640 | tf_op jit(solution)/shard_map/ppermute | solution.py:12
  25.9 10.3 %copy-start.4 = (bf16[128,1024]{1,0:T(8,128)(2,1)S(1)}, bf16[128,1024]{1,0:T(8,128)(2,1)}, u32[]{:S(2)}) copy-start(bf16[128,1024]{1,0:T(8,128)(2,1)} %param.9) | copy-start | bytes 786436
  27.0 36.8 %all-to-all-start = ((bf16[8,9,128,64]{2,3,1,0:T(8,128)(2,1)}), bf16[8,9,128,64]{2,3,1,0:T(8,128)(2,1)S(1)}, u32[]{:S(2)}, u32[]{:S(2)}) async-start(bf16[8,9,128,64]{2,3,1,0:T(8,128)(2,1)} %pad_maximum_fusion), calls=%async_computation | async-start | bytes 2359296 | tf_op jit(solution)/shard_map/all_to_all | solution.py:104
  66.7 2.0 %copy-start.3 = (f32[9,8,128,64]{2,0,3,1:T(8,128)}, f32[9,8,128,64]{2,0,3,1:T(8,128)S(1)}, u32[]{:S(2)}) copy-start(f32[9,8,128,64]{2,0,3,1:T(8,128)S(1)} %convolution_bitcast_fusion) | copy-start | bytes 7077892
  69.6 23.6 %all-to-all-start.1 = ((f32[32,24,128]{2,1,0:T(8,128)}), f32[32,24,128]{2,1,0:T(8,128)}, u32[]{:S(2)}, u32[]{:S(2)}) async-start(f32[32,24,128]{2,1,0:T(8,128)} %select_maximum_fusion), calls=%async_computation.1 | async-start | bytes 786432 | tf_op jit(solution)/shard_map/all_to_all | solution.py:140
  100.9 14.4 %all-to-all-start.2 = ((bf16[32,16,128]{2,1,0:T(8,128)(2,1)}), bf16[32,16,128]{2,1,0:T(8,128)(2,1)S(1)}, u32[]{:S(2)}, u32[]{:S(2)}) async-start(bf16[32,16,128]{2,1,0:T(8,128)(2,1)} %copy.154), calls=%async_computation.2 | async-start | bytes 262144 | tf_op jit(solution)/shard_map/all_to_all | solution.py:147
  117.2 28.1 %copy-start.1 = (f32[8,16,64,128]{3,2,1,0:T(8,128)S(1)}, f32[8,16,64,128]{3,2,1,0:T(8,128)}, u32[]{:S(2)}) copy-start(f32[8,16,64,128]{3,2,1,0:T(8,128)} %copy-done) | copy-start | bytes 12582916
  145.3 8.4 %copy-start.7 = (f32[128,128]{1,0:T(8,128)S(1)}, f32[128,128]{1,0:T(8,128)}, u32[]{:S(2)}) copy-start(f32[128,128]{1,0:T(8,128)} %get-tuple-element.15) | copy-start | bytes 196612
  148.9 7.5 %collective-permute-start.2 = (bf16[64,128,64]{1,2,0:T(8,128)(2,1)}, bf16[64,128,64]{1,2,0:T(8,128)(2,1)}, u32[]{:S(2)}, u32[]{:S(2)}) collective-permute-start(bf16[64,128,64]{1,2,0:T(8,128)(2,1)} %get-tuple-element.12), channel_id=1, source_target_pairs={{0,1},{1,0},{2,3},{3,2},{4,5},{5,4},{6,7},{7,6},{8,9},{9,8},{10,11... | collective-permute-start | bytes 3145736 | tf_op jit(solution)/shard_map/ppermute | solution.py:12
  159.2 2.2 %copy-start.2 = (f32[128,128,64]{0,2,1:T(8,128)S(1)}, f32[128,128,64]{0,2,1:T(8,128)}, u32[]{:S(2)}) copy-start(f32[128,128,64]{0,2,1:T(8,128)} %convolution_bitcast_fusion.1) | copy-start | bytes 12582916
  159.2 2.2 %copy-start.6 = (f32[128,128]{0,1:T(8,128)S(1)}, f32[128,128]{0,1:T(8,128)}, u32[]{:S(2)}) copy-start(f32[128,128]{0,1:T(8,128)} %copy.148) | copy-start | bytes 196612

commit v16 on v14

--- a/solution.py
+++ b/solution.py
@@ -132,15 +132,16 @@
     per = quarter * width // n_seq
     chunks = run.transpose(0, 2, 1).reshape(n_seq, per, state)
     row_totals = jnp.repeat(before, width).reshape(n_seq, per)
+    totals3 = split3(row_totals).transpose(0, 2, 1)
     packed = jnp.concatenate(
-        [chunks, jnp.pad(row_totals, ((0, 0), (0, state - per)))[:, None, :]], axis=1
+        [chunks.astype(bf16), jnp.pad(totals3, ((0, 0), (0, 0), (0, state - per)))], axis=1
     )
-    packed = jnp.pad(packed, ((0, 0), (0, -(per + 1) % 8), (0, 0)))
+    packed = jnp.pad(packed, ((0, 0), (0, -(per + 3) % 16), (0, 0)))
     gathered = lax.all_to_all(packed, "seq", 0, 0, tiled=True)
     entering = jnp.einsum(
         "rab,brn->arn",
-        decay_matrix(gathered[:, per, :per], n_seq),
-        gathered[:, :per],
+        decay_matrix(join3(gathered[:, per : per + 3, :per].transpose(0, 2, 1)), n_seq),
+        gathered[:, :per].astype(f32),
         precision=lax.Precision.HIGHEST,
     )
     acc_s = lax.all_to_all(entering.astype(bf16), "seq", 0, 0, tiled=True).astype(f32)

time: 166 us -> 161 us (0.970)
  waiting for transfers between devices: 42.9 us -> 40.6 us
    all_to_all x1, waiting for transfers between devices: 13.8 us -> 11.5 us  [local(): gathered = lax.all_to_all(packed, 'seq', 0, 0, tiled=True)]
    slice x2 -> x1, local copies, waits for them, and re-layouts: 1.89 us -> 0.01 us  [local(): gathered[:, :per].astype(f32)]
    unnamed x22 -> x23, local copies, waits for them, and re-layouts: 9.65 us -> 9.66 us
  transfers between devices with their start and end apart: 6 -> 6, of which waited for: 5 -> 5; matrix products, arithmetic and copies ran while one was open for 10% -> 11% of each run, Pallas kernels for 0% -> 0%
where the time goes in v16:
time: 161 us; the launch traced here: 160 us
  waiting for transfers between devices  40.6 us (25%)
  starting transfers between devices  34.1 us (21%)
  blocking collectives  28.1 us (17%)
  local copies, waits for them, and re-layouts  22.4 us (14%)
  other arithmetic  22.1 us (14%)
  matrix products  11.6 us (7%)
    all_to_all x1, blocking collectives, local(): back = lax.all_to_all(chip_in.astype(bf16), 'z', 0, 0, tiled=True)  28.1 us
    all_to_all x1, waiting for transfers between devices, local(): rows = lax.all_to_all(message, 'z', 0, 0, tiled=True)  17.7 us
    ppermute x3, starting transfers between devices, swap(): return lax.ppermute(value, 'core', [(0, 1), (1, 0)])  15.2 us
    all_to_all x1, waiting for transfers between devices, local(): gathered = lax.all_to_all(packed, 'seq', 0, 0, tiled=True)  11.5 us
    all_to_all x1, starting transfers between devices, local(): gathered = lax.all_to_all(packed, 'seq', 0, 0, tiled=True)  9.67 us
    unnamed x23, local copies, waits for them, and re-layouts  9.66 us
    all_to_all x1, waiting for transfers between devices, local(): lax.all_to_all(entering.astype(bf16), 'seq', 0, 0, tiled=True).astype(f32)  9.34 us
    dot_general x1, matrix products, local(): inside = jnp.einsum('hts,shp->thp', weight, x, preferred_element_type=f32)  5.01 us
  transfers between devices with their start and end apart: 6, of which 5 were waited for; matrix products, arithmetic and copies ran while one was open for 11% of the time, Pallas kernels for 0%

profile of v16, /device:TPU:1, one launch (start us, length us, event | category | flops | bytes accessed | tf_op | source)
XLA Modules:
  0.0 159.5 jit_solution(9564379432836556298)
XLA Ops:
  3.5 3.2 %copy.166 = bf16[128,8192]{0,1:T(8,128)(2,1)S(1)} copy(bf16[128,8192]{1,0:T(8,128)(2,1)} %param.6) | data formatting | bytes 4194304 | tf_op args[0]
  7.4 1.6 %constant_dynamic-slice_fusion = f32[64,128,64]{1,2,0:T(8,128)} fusion(f32[128,128,64]{1,2,0:T(8,128)S(1)} %bitcast.114, s32[]{:T(128)S(6)} %select_n.103), kind=kLoop, calls=%fused_computation.115 | loop fusion | bytes 4194308 | tf_op jit(solution)/shard_map/dynamic_slice | solution.py:80
  10.0 8.8 %collective-permute-start.1 = (f32[64,128,64]{1,2,0:T(8,128)}, f32[64,128,64]{1,2,0:T(8,128)}, u32[]{:S(2)}, u32[]{:S(2)}) collective-permute-start(f32[64,128,64]{1,2,0:T(8,128)} %constant_dynamic-slice_fusion), channel_id=1, source_target_pairs={{0,1},{1,0},{2,3},{3,2},{4,5},{5,4},{6,7},{7,6},{8,9},{9,8},{10,11... | collective-permute-start | bytes 6291464 | tf_op jit(solution)/shard_map/ppermute | solution.py:12
  18.8 1.9 %collective-permute-start = (f32[136]{0:T(256)S(1)}, f32[136]{0:T(256)S(1)}, u32[]{:S(2)}, u32[]{:S(2)}) collective-permute-start(f32[136]{0:T(256)S(1)} %pad_maximum_fusion.3), channel_id=1, source_target_pairs={{0,1},{1,0},{2,3},{3,2},{4,5},{5,4},{6,7},{7,6},{8,9},{9,8},{10,11... | collective-permute-start | bytes 1640 | tf_op jit(solution)/shard_map/ppermute | solution.py:12
  20.9 1.6 %collective-permute-done = f32[136]{0:T(256)S(1)} collective-permute-done((f32[136]{0:T(256)S(1)}, f32[136]{0:T(256)S(1)}, u32[]{:S(2)}, u32[]{:S(2)}) %collective-permute-start) | collective-permute-done | bytes 576 | tf_op jit(solution)/shard_map/ppermute | solution.py:12
  23.2 2.6 %add_convert_fusion = bf16[64,128,64]{1,2,0:T(8,128)(2,1)S(1)} fusion(f32[64,128,64]{1,2,0:T(8,128)} %collective-permute-done.1, f32[128,128,64]{1,2,0:T(8,128)} %bitcast.115, s32[]{:T(128)S(6)} %select_n.101, f32[64]{0:T(128)S(1)} %get-tuple-element.24, pred[]{:T(512)S(6)} %eq.2), kind=kLoop, calls=%fused_computation.21 | loop fusion | flops 2621440 | bytes 5243141 | tf_op jit(solution)/shard_map/convert_element_type | solution.py:87
  27.0 4.7 %all-to-all-start = ((bf16[8,9,128,64]{2,3,1,0:T(8,128)(2,1)}), bf16[8,9,128,64]{2,3,1,0:T(8,128)(2,1)S(1)}, u32[]{:S(2)}, u32[]{:S(2)}) async-start(bf16[8,9,128,64]{2,3,1,0:T(8,128)(2,1)} %pad_maximum_fusion), calls=%async_computation | async-start | bytes 2359296 | tf_op jit(solution)/shard_map/all_to_all | solution.py:103
  31.7 1.6 copy.163
  37.4 3.6 %fusion.1 = bf16[128,128,128]{2,1,0:T(8,128)(2,1)S(1)} fusion(f32[128,128]{1,0:T(8,128)} %copy.165, f32[128,128]{1,0:T(8,128)} %copy.163, f32[8,128,128]{2,1,0:T(8,128)S(1)} %fusion.22, pred[128,128]{1,0:T(8,128)(4,1)S(1)} %iota_compare_fusion.3), kind=kLoop, calls=%fused_computation.2 | loop fusion | flops 12582912 | bytes 4866048 | tf_op jit(solution)/shard_map/convert_element_type | solution.py:110
  41.1 5.0 %convolution_bitcast_fusion.1 = f32[128,128,64]{0,2,1:T(8,128)} fusion(bf16[128,128,128]{2,1,0:T(8,128)(2,1)S(1)} %fusion.1, bf16[128,128,64]{0,2,1:T(8,128)(2,1)S(1)} %bitcast.112), kind=kOutput, calls=%fused_computation.13 | convolution fusion | flops 268435456 | bytes 10485760 | tf_op jit(solution)/shard_map/hts,shp->thp/dot_general | solution.py:111
  46.1 17.7 %all-to-all-done = bf16[8,9,128,64]{2,3,1,0:T(8,128)(2,1)S(1)} async-done(((bf16[8,9,128,64]{2,3,1,0:T(8,128)(2,1)}), bf16[8,9,128,64]{2,3,1,0:T(8,128)(2,1)S(1)}, u32[]{:S(2)}, u32[]{:S(2)}) %all-to-all-start) | async-done | bytes 1179680 | tf_op jit(solution)/shard_map/all_to_all | solution.py:103
  64.8 2.1 %convolution_bitcast_fusion = f32[9,8,128,64]{2,0,3,1:T(8,128)S(1)} fusion(bf16[8,8,128,64]{2,3,1,0:T(8,128)(2,1)S(1)} %slice.100, f32[8,9,8,1]{1,0,2,3:T(8,128)S(1)} %fusion.18), kind=kOutput, calls=%fused_computation.12 | convolution fusion | flops 56623104 | bytes 3410176 | tf_op jit(solution)/shard_map/hab,bhnp->ahnp/dot_general | solution.py:120
  66.9 2.0 %copy-done.3 = f32[9,8,128,64]{2,0,3,1:T(8,128)} copy-done((f32[9,8,128,64]{2,0,3,1:T(8,128)}, f32[9,8,128,64]{2,0,3,1:T(8,128)S(1)}, u32[]{:S(2)}) %copy-start.3) | copy-done | bytes 2359320
  69.8 9.7 %all-to-all-start.1 = ((bf16[32,32,128]{2,1,0:T(8,128)(2,1)}), bf16[32,32,128]{2,1,0:T(8,128)(2,1)S(1)}, u32[]{:S(2)}, u32[]{:S(2)}) async-start(bf16[32,32,128]{2,1,0:T(8,128)(2,1)} %pad.14), calls=%async_computation.1 | async-start | bytes 524288 | tf_op jit(solution)/shard_map/all_to_all | solution.py:140
  79.5 11.5 %all-to-all-done.1 = bf16[32,32,128]{2,1,0:T(8,128)(2,1)S(1)} async-done(((bf16[32,32,128]{2,1,0:T(8,128)(2,1)}), bf16[32,32,128]{2,1,0:T(8,128)(2,1)S(1)}, u32[]{:S(2)}, u32[]{:S(2)}) %all-to-all-start.1) | async-done | bytes 262176 | tf_op jit(solution)/shard_map/all_to_all | solution.py:140
  93.2 4.6 %all-to-all-start.2 = ((bf16[32,16,128]{2,1,0:T(8,128)(2,1)}), bf16[32,16,128]{2,1,0:T(8,128)(2,1)S(1)}, u32[]{:S(2)}, u32[]{:S(2)}) async-start(bf16[32,16,128]{2,1,0:T(8,128)(2,1)} %copy.187), calls=%async_computation.2 | async-start | bytes 262144 | tf_op jit(solution)/shard_map/all_to_all | solution.py:147
  97.8 9.3 %all-to-all-done.2 = bf16[32,16,128]{2,1,0:T(8,128)(2,1)S(1)} async-done(((bf16[32,16,128]{2,1,0:T(8,128)(2,1)}), bf16[32,16,128]{2,1,0:T(8,128)(2,1)S(1)}, u32[]{:S(2)}, u32[]{:S(2)}) %all-to-all-start.2) | async-done | bytes 131104 | tf_op jit(solution)/shard_map/all_to_all | solution.py:147
  107.2 2.0 %fusion.11 = bf16[8,8,128,64]{2,0,3,1:T(8,128)(2,1)S(1)} fusion(f32[9,8,128,64]{2,0,3,1:T(8,128)} %copy-done.3, f32[8,128,64]{1,2,0:T(8,128)S(1)} %convert_bitcast_fusion, f32[8,8]{0,1:T(8,128)S(1)} %slice_exponential_fusion), kind=kLoop, calls=%fused_computation.19 | loop fusion | flops 1572864 | bytes 3408128 | tf_op jit(solution)/shard_map/convert_element_type | solution.py:151
  109.4 28.1 %all_to_all.20 = bf16[8,8,128,64]{2,3,1,0:T(8,128)(2,1)S(1)} all-to-all(bf16[8,8,128,64]{2,3,1,0:T(8,128)(2,1)S(1)} %copy.188), channel_id=1, replica_groups=mesh['seq'=32,'z'=8,'core'=2] {'z'}, dimensions={0} | all-to-all | bytes 2097152 | tf_op jit(solution)/shard_map/all_to_all | solution.py:151
  137.6 3.6 %fusion.7 = (bf16[64,128,64]{1,2,0:T(8,128)(2,1)}, bf16[64,128,64]{1,2,0:T(8,128)(2,1)}) fusion(bf16[8,8,128,64]{2,3,1,0:T(8,128)(2,1)S(1)} %all_to_all.20, f32[64]{0:T(128)S(1)} %get-tuple-element.22, pred[]{:T(512)S(6)} %eq.2, f32[64,128,64]{1,2,0:T(8,128)} %collective-permute-done.1, f32[128,128,64]{1,2,0:T(8,128)S(1)} %bitcast.116, s32[]{:T(128)S(6)} %select_n.101), kind=kLoop, calls=%fused_computation.15 | loop fusion | flops 4194304 | bytes 7340293 | tf_op jit(solution)/shard_map/convert_element_type | solution.py:155
  141.2 4.5 %collective-permute-start.2 = (bf16[64,128,64]{1,2,0:T(8,128)(2,1)}, bf16[64,128,64]{1,2,0:T(8,128)(2,1)}, u32[]{:S(2)}, u32[]{:S(2)}) collective-permute-start(bf16[64,128,64]{1,2,0:T(8,128)(2,1)} %get-tuple-element.12), channel_id=1, source_target_pairs={{0,1},{1,0},{2,3},{3,2},{4,5},{5,4},{6,7},{7,6},{8,9},{9,8},{10,11... | collective-permute-start | bytes 3145736 | tf_op jit(solution)/shard_map/ppermute | solution.py:12
  148.3 2.8 %maximum_select_fusion = bf16[128,128,64]{1,2,0:T(8,128)(2,1)S(1)} fusion(bf16[64,128,64]{1,2,0:T(8,128)(2,1)} %collective-permute-done.2, bf16[64,128,64]{1,2,0:T(8,128)(2,1)} %get-tuple-element.11, pred[]{:T(512)S(6)} %eq.2), kind=kLoop, calls=%fused_computation.20 | loop fusion | flops 3145728 | bytes 4194305 | tf_op jit(solution)/shard_map/jit(_where)/select_n | solution.py:158
  153.3 2.2 %fusion.4 = bf16[128,128,64]{0,2,1:T(8,128)(2,1)} fusion(f32[128,128,64]{0,2,1:T(8,128)S(1)} %copy-done.2, f32[8,16,64,128]{3,2,1,0:T(8,128)S(1)} %fusion.32, bf16[128,128,64]{0,2,1:T(8,128)(2,1)S(1)} %bitcast.113, f32[128]{0:T(128)S(1)} %add.85, f32[128,128]{0,1:T(8,128)S(1)} %copy-done.6), kind=kLoop, calls=%fused_computation.6 | loop fusion | flops 6291456 | bytes 12648960 | tf_op jit(solution)/shard_map/convert_element_type | solution.py:169
  155.5 4.1 %copy.192 = bf16[128,8192]{1,0:T(8,128)(2,1)} copy(bf16[128,8192]{0,1:T(8,128)(2,1)} %bitcast.117) | data formatting | bytes 4194304 | tf_op jit(solution)/shard_map/reshape | solution.py:169
  (90 shorter events, 20.4 us)
Async XLA Ops:
  0.9 22.0 %copy-start.5 = (f32[128,128]{1,0:T(8,128)}, f32[128,128]{1,0:T(8,128)S(1)}, u32[]{:S(2)}) copy-start(f32[128,128]{1,0:T(8,128)S(1)} %reduce_window_sum.11) | copy-start | bytes 196612
  7.4 2.6 %copy-start = (f32[8,16,64,128]{3,2,1,0:T(8,128)}, f32[8,16,64,128]{3,2,1,0:T(8,128)S(1)}, u32[]{:S(2)}) copy-start(f32[8,16,64,128]{3,2,1,0:T(8,128)S(1)} %fusion.9) | copy-start | bytes 12582916
  7.4 11.4 %copy-start.8 = (f32[8]{0:T(128)S(1)}, f32[8]{0:T(128)}, u32[]{:S(2)}) copy-start(f32[8]{0:T(128)} %param.11) | copy-start | bytes 100
  10.0 13.2 %collective-permute-start.1 = (f32[64,128,64]{1,2,0:T(8,128)}, f32[64,128,64]{1,2,0:T(8,128)}, u32[]{:S(2)}, u32[]{:S(2)}) collective-permute-start(f32[64,128,64]{1,2,0:T(8,128)} %constant_dynamic-slice_fusion), channel_id=1, source_target_pairs={{0,1},{1,0},{2,3},{3,2},{4,5},{5,4},{6,7},{7,6},{8,9},{9,8},{10,11... | collective-permute-start | bytes 6291464 | tf_op jit(solution)/shard_map/ppermute | solution.py:12
  18.8 3.7 %collective-permute-start = (f32[136]{0:T(256)S(1)}, f32[136]{0:T(256)S(1)}, u32[]{:S(2)}, u32[]{:S(2)}) collective-permute-start(f32[136]{0:T(256)S(1)} %pad_maximum_fusion.3), channel_id=1, source_target_pairs={{0,1},{1,0},{2,3},{3,2},{4,5},{5,4},{6,7},{7,6},{8,9},{9,8},{10,11... | collective-permute-start | bytes 1640 | tf_op jit(solution)/shard_map/ppermute | solution.py:12
  25.9 10.3 %copy-start.4 = (bf16[128,1024]{1,0:T(8,128)(2,1)S(1)}, bf16[128,1024]{1,0:T(8,128)(2,1)}, u32[]{:S(2)}) copy-start(bf16[128,1024]{1,0:T(8,128)(2,1)} %param.9) | copy-start | bytes 786436
  27.0 36.8 %all-to-all-start = ((bf16[8,9,128,64]{2,3,1,0:T(8,128)(2,1)}), bf16[8,9,128,64]{2,3,1,0:T(8,128)(2,1)S(1)}, u32[]{:S(2)}, u32[]{:S(2)}) async-start(bf16[8,9,128,64]{2,3,1,0:T(8,128)(2,1)} %pad_maximum_fusion), calls=%async_computation | async-start | bytes 2359296 | tf_op jit(solution)/shard_map/all_to_all | solution.py:103
  66.9 2.0 %copy-start.3 = (f32[9,8,128,64]{2,0,3,1:T(8,128)}, f32[9,8,128,64]{2,0,3,1:T(8,128)S(1)}, u32[]{:S(2)}) copy-start(f32[9,8,128,64]{2,0,3,1:T(8,128)S(1)} %convolution_bitcast_fusion) | copy-start | bytes 7077892
  69.8 21.1 %all-to-all-start.1 = ((bf16[32,32,128]{2,1,0:T(8,128)(2,1)}), bf16[32,32,128]{2,1,0:T(8,128)(2,1)S(1)}, u32[]{:S(2)}, u32[]{:S(2)}) async-start(bf16[32,32,128]{2,1,0:T(8,128)(2,1)} %pad.14), calls=%async_computation.1 | async-start | bytes 524288 | tf_op jit(solution)/shard_map/all_to_all | solution.py:140
  93.2 13.9 %all-to-all-start.2 = ((bf16[32,16,128]{2,1,0:T(8,128)(2,1)}), bf16[32,16,128]{2,1,0:T(8,128)(2,1)S(1)}, u32[]{:S(2)}, u32[]{:S(2)}) async-start(bf16[32,16,128]{2,1,0:T(8,128)(2,1)} %copy.187), calls=%async_computation.2 | async-start | bytes 262144 | tf_op jit(solution)/shard_map/all_to_all | solution.py:147
  109.2 28.4 %copy-start.1 = (f32[8,16,64,128]{3,2,1,0:T(8,128)S(1)}, f32[8,16,64,128]{3,2,1,0:T(8,128)}, u32[]{:S(2)}) copy-start(f32[8,16,64,128]{3,2,1,0:T(8,128)} %copy-done) | copy-start | bytes 12582916
  137.6 8.1 %copy-start.7 = (f32[128,128]{1,0:T(8,128)S(1)}, f32[128,128]{1,0:T(8,128)}, u32[]{:S(2)}) copy-start(f32[128,128]{1,0:T(8,128)} %get-tuple-element.15) | copy-start | bytes 196612
  141.2 7.1 %collective-permute-start.2 = (bf16[64,128,64]{1,2,0:T(8,128)(2,1)}, bf16[64,128,64]{1,2,0:T(8,128)(2,1)}, u32[]{:S(2)}, u32[]{:S(2)}) collective-permute-start(bf16[64,128,64]{1,2,0:T(8,128)(2,1)} %get-tuple-element.12), channel_id=1, source_target_pairs={{0,1},{1,0},{2,3},{3,2},{4,5},{5,4},{6,7},{7,6},{8,9},{9,8},{10,11... | collective-permute-start | bytes 3145736 | tf_op jit(solution)/shard_map/ppermute | solution.py:12
  151.1 2.2 %copy-start.2 = (f32[128,128,64]{0,2,1:T(8,128)S(1)}, f32[128,128,64]{0,2,1:T(8,128)}, u32[]{:S(2)}) copy-start(f32[128,128,64]{0,2,1:T(8,128)} %convolution_bitcast_fusion.1) | copy-start | bytes 12582916
  151.1 2.2 %copy-start.6 = (f32[128,128]{0,1:T(8,128)S(1)}, f32[128,128]{0,1:T(8,128)}, u32[]{:S(2)}) copy-start(f32[128,128]{0,1:T(8,128)} %copy.179) | copy-start | bytes 196612
